TPU v7x, 512 devices: a whole 4x4x16 slice. The times are simulated.
512 devices in a mesh: seq: 32 (over z, core), head: 16 (over y, x).
Axes of the slice: x: 4, y: 4, z: 16, core: 2. Of those that a mesh axis runs over, the one named last changes fastest.
Arguments:
- head_inputs: float32 [16384, 8192], P('seq', 'head'), may hold values from -0.625 to 0.625
- input_proj: float32 [16384, 128], P('seq'), may hold values from -1.75 to 1.75
- output_mapping: float32 [16384, 128], P('seq'), may hold values from -1.75 to 1.75
- decay_codes: int32 [128, 16384], P('head', 'seq'), may hold values from 0 to 15
- boundary: int32 [16384], P('seq'), may hold values 0 or 1
- head_decay_speeds: float32 [128], P('head'), may hold values from 0 to 1, as said below
- out_grad: float32 [16384, 8192], P('seq', 'head'), may hold values from -0.0625 to 0.0625
Outputs:
- grad_inputs: float32 [16384, 8192], P('seq', 'head')
- grad_in_proj: float32 [16384, 128], P(('seq', 'head'))
- grad_out_proj: float32 [16384, 128], P(('seq', 'head'))
Inputs may be any that keep to these rules, and one draw needn't show every extreme that they name: `head_decay_speeds`: each head's decay rate is positive.
All inputs are finite; a program needn't handle non-finite values. No bound on the sum of `boundary` on one device may be relied on, other than what follows from the above.
Results may differ from a plain program's by a relative error of at most 0.0001.
Values sent between devices are 32-bit elements; how exact they have to be, the bound alone decides.
No kernel may reach another device: no remote copies, remote signals or barrier semaphores. Data moves between devices by JAX's collectives and lax.ppermute only.
A program may use at most 64 MiB of HBM per device.

v0:
```python
import jax
import jax.numpy as jnp
from jax import lax
from jax.sharding import PartitionSpec as P

sudden_falloff = 0.35
highest = lax.Precision.HIGHEST


def prefix(value, axis, join, neutral, backward):
    count, mine = (lax.axis_size(axis), lax.axis_index(axis))
    pieces = jax.tree.map(lambda part: lax.all_gather(part, axis), value)
    if backward:
        pieces = jax.tree.map(lambda part: part[::-1], pieces)
        mine = count - 1 - mine
    running = jax.tree.map(
        lambda part, zero: jnp.full_like(part, 0) + jnp.asarray(zero, part.dtype), value, neutral
    )

    def step(position, running):
        longer = join(running, jax.tree.map(lambda part: part[position], pieces))
        return jax.tree.map(lambda new, old: jnp.where(position < mine, new, old), longer, running)

    return lax.fori_loop(0, count - 1, step, running)


def step_table(decay_codes):
    levels = jnp.arange(16, dtype=jnp.int32)
    values = 0.5 * 4.0 ** (levels.astype(jnp.float32) / 15.0)
    matching_label = decay_codes[None, :, :] == levels[:, None, None]
    return jnp.sum(jnp.where(matching_label, values[:, None, None], 0.0), axis=0)


def spread_heads(per_head, head_width):
    head_count, tok_count = per_head.shape
    wide = jnp.broadcast_to(per_head.T[:, :, None], (tok_count, head_count, head_width))
    return wide.reshape(tok_count, head_count * head_width)


def chain_step(earlier, later):
    return (earlier[0] + later[0], jnp.exp(later[0])[:, None, None] * earlier[1] + later[1])


def per_device(
    head_inputs, input_proj, output_mapping, decay_codes, boundary, head_decay_speeds, out_grad
):
    tok_count = head_inputs.shape[0]
    head_count = decay_codes.shape[0]
    head_width = head_inputs.shape[1] // head_count
    state_width = input_proj.shape[1]
    increment_length = step_table(decay_codes)
    logarithm_decay = (
        -head_decay_speeds[:, None] * increment_length
        - sudden_falloff * boundary.astype(jnp.float32)[None, :]
    )
    cumul = jnp.cumsum(logarithm_decay, axis=1)
    group_total = cumul[:, -1]
    to_end = spread_heads(jnp.exp(group_total[:, None] - cumul), head_width)
    from_start = spread_heads(jnp.exp(cumul), head_width)
    scaled_in = head_inputs * spread_heads(increment_length, head_width)
    scores = jnp.einsum("tn,sn->ts", output_mapping, input_proj, precision=highest)
    positions = jnp.arange(tok_count, dtype=jnp.int32)
    lower_mask = positions[:, None] >= positions[None, :]

    def one_head(loop_carry, head_index):
        grad_scores, grad_scaled = loop_carry
        cum_row = lax.dynamic_index_in_dim(cumul, head_index, 0, keepdims=False)
        col_start = head_index * head_width
        own_in = lax.dynamic_slice_in_dim(scaled_in, col_start, head_width, 1)
        own_grad = lax.dynamic_slice_in_dim(out_grad, col_start, head_width, 1)
        decay_gap = jnp.where(lower_mask, cum_row[:, None] - cum_row[None, :], 0.0)
        decay_mat = jnp.where(lower_mask, jnp.exp(decay_gap), 0.0)
        mixing = scores * decay_mat
        back_flow = jnp.einsum("ts,tp->sp", mixing, own_grad, precision=highest)
        pair_weights = jnp.einsum("tp,sp->ts", own_grad, own_in, precision=highest)
        grad_scaled = lax.dynamic_update_slice_in_dim(grad_scaled, back_flow, col_start, 1)
        return ((grad_scores + pair_weights * decay_mat, grad_scaled), None)

    start_carry = (
        jnp.zeros((tok_count, tok_count), jnp.float32),
        jnp.zeros(head_inputs.shape, jnp.float32),
    )
    (grad_scores, grad_scaled), unused = lax.scan(
        one_head, start_carry, jnp.arange(head_count, dtype=jnp.int32)
    )
    block_b = jnp.einsum("ts,tn->sn", grad_scores, output_mapping, precision=highest)
    block_c = jnp.dot(grad_scores, input_proj, precision=highest)
    weighted_in = scaled_in * to_end
    weighted_grad = out_grad * from_start
    ends = jnp.einsum("tk,tn->kn", weighted_in, input_proj, precision=highest)
    starts = jnp.einsum("tk,tn->kn", weighted_grad, output_mapping, precision=highest)
    identity = (
        jnp.zeros((head_count,), jnp.float32),
        jnp.zeros((head_count, head_width, state_width), jnp.float32),
    )
    unused_in, state_in = prefix(
        (group_total, ends.reshape(head_count, head_width, state_width)),
        "seq",
        chain_step,
        identity,
        False,
    )
    unused_back, state_grad = prefix(
        (group_total, starts.reshape(head_count, head_width, state_width)),
        "seq",
        chain_step,
        identity,
        True,
    )
    flat_in = state_in.reshape(head_count * head_width, state_width)
    flat_grad = state_grad.reshape(head_count * head_width, state_width)
    carry_c = jnp.dot(weighted_grad, flat_in, precision=highest)
    carry_b = jnp.dot(weighted_in, flat_grad, precision=highest)
    carry_x = to_end * jnp.einsum("tn,kn->tk", input_proj, flat_grad, precision=highest)
    grad_inputs = (grad_scaled + carry_x) * spread_heads(increment_length, head_width)
    grad_in_proj, grad_out_proj = (
        lax.psum_scatter(block_b + carry_b, "head", scatter_dimension=0, tiled=True),
        lax.psum_scatter(block_c + carry_c, "head", scatter_dimension=0, tiled=True),
    )
    return (grad_inputs, grad_in_proj, grad_out_proj)


def solution(mesh):
    return jax.shard_map(
        per_device,
        mesh=mesh,
        in_specs=(
            P("seq", "head"),
            P("seq", None),
            P("seq", None),
            P("head", "seq"),
            P("seq"),
            P("head"),
            P("seq", "head"),
        ),
        out_specs=(P("seq", "head"), P(("seq", "head"), None), P(("seq", "head"), None)),
        check_vma=False,
    )
```

profile of v0, /device:TPU:1, one launch (start us, length us, event | category | flops | bytes accessed | tf_op | source)
XLA Modules:
  0.0 385.0 jit_solution(7027513041555102441)
XLA Ops:
  9.5 1.1 reduce-window.6
  11.2 1.6 copy.22
  12.8 1.3 bitcast_multiply_fusion
  14.1 1.7 fusion.25
  15.8 2.5 copy.24
  18.4 1.3 bitcast_multiply_fusion.4
  19.7 1.7 fusion.22
  21.5 2.0 fusion.21
  23.5 1.3 dynamic-slice
  25.8 55.5 %all-reduce = f32[256]{0:T(256)S(1)} all-reduce(f32[256]{0:T(256)S(1)} %dynamic-update-slice), channel_id=2, replica_groups=mesh['seq'=32,'head'=16] {'seq'}, use_global_device_ids=true, to_apply=%add | all-reduce | flops 256 | bytes 2048
  81.4 1.1 broadcast.41
  82.6 77.1 %while.44 = (s32[]{:T(128)}, f32[512,512]{1,0:T(8,128)}, f32[512,512]{0,1:T(8,128)}, s32[8]{0:T(128)S(1)}, f32[512,512]{1,0:T(8,128)}, /*index=5*/f32[512,512]{0...) while((s32[]{:T(128)}, f32[512,512]{1,0:T(8,128)}, ...), condition=%wide.region_4.5_spmd.clone.clone, body=%wide.region_3.4_spmd.clone.clone.sunk | while | flops 405798912 | bytes 3947246 | solution.py:83
  85.8 3.2 fusion.55
  89.0 2.9 convolution_dynamic-update-slice_fusion.2
  95.1 3.6 fusion.55
  98.6 2.9 convolution_dynamic-update-slice_fusion.2
  104.7 3.6 fusion.55
  108.3 2.9 convolution_dynamic-update-slice_fusion.2
  114.4 3.6 fusion.55
  117.9 2.9 convolution_dynamic-update-slice_fusion.2
  124.0 3.6 fusion.55
  127.6 2.9 convolution_dynamic-update-slice_fusion.2
  133.7 3.6 fusion.55
  137.3 2.9 convolution_dynamic-update-slice_fusion.2
  143.4 3.6 fusion.55
  147.0 2.9 convolution_dynamic-update-slice_fusion.2
  153.1 3.6 fusion.55
  156.7 2.9 convolution_dynamic-update-slice_fusion.2
  159.6 2.9 fusion.24
  162.5 3.0 fusion.23
  165.6 34.1 %while.43 = (s32[]{:T(128)}, f32[8,64,128]{2,1,0:T(8,128)S(1)}, s32[]{:T(128)}, f32[32,8]{1,0:T(8,128)S(1)}, f32[32,8,64,128]{3,2,1,0:T(8,128)}, /*index=5*/s32[]{:T(128)}, s32[]{:T(128)}) while((s32[]{:T(128)}, f32[8,64,128]{2,1,0:T(8,128)S(1)}, s32[]{:T(128)}, f32[32,8]{1,0:T(8,128)S(1)}, f32[32,8,64,128]{3,2,1,0:T(8,128)}, ...), condition=%wide.region_9.10_spmd.clone, body=%wide.region_8.9_spmd.clone.sunk | while | flops 262148 | bytes 786641 | solution.py:24
  165.6 1.1 fusion.50
  199.7 3.5 convolution_add_fusion
  203.5 8.3 %rev.7 = f32[32,8,64,128]{3,2,1,0:T(8,128)} reverse(f32[32,8,64,128]{3,2,1,0:T(8,128)} %all-gather.4.cloned.1.call-done), dimensions={0} | reverse | bytes 16777216 | tf_op jit(solution)/shard_map/rev | solution.py:14
  211.8 34.1 %while.42 = (s32[]{:T(128)}, f32[8,64,128]{2,1,0:T(8,128)S(1)}, s32[]{:T(128)}, f32[32,8]{1,0:T(8,128)S(1)}, f32[32,8,64,128]{3,2,1,0:T(8,128)}, /*index=5*/s32[]{:T(128)}, s32[]{:T(128)}) while((s32[]{:T(128)}, f32[8,64,128]{2,1,0:T(8,128)S(1)}, s32[]{:T(128)}, f32[32,8]{1,0:T(8,128)S(1)}, f32[32,8,64,128]{3,2,1,0:T(8,128)}, ...), condition=%wide.region_6.7_spmd.clone, body=%wide.region_5.6_spmd.clone.sunk | while | flops 262148 | bytes 786641 | solution.py:24
  218.4 1.1 fusion.49
  221.7 1.1 fusion.49
  225.0 1.1 fusion.49
  227.2 1.1 fusion.49
  228.3 1.1 fusion.49
  230.5 1.1 fusion.49
  236.0 1.1 fusion.49
  242.6 1.1 fusion.49
  243.7 1.1 fusion.49
  245.9 2.5 convolution_add_fusion.1
  249.5 1.3 copy.25
  250.8 35.9 %reduce-scatter.5.cloned.1.call-done = f32[32,128]{1,0:T(8,128)} async-done(((f32[512,128]{1,0:T(8,128)}), f32[32,128]{1,0:T(8,128)}) %reduce-scatter.5.cloned.1.call-update) | async-done | bytes 16400 | tf_op jit(solution)/shard_map/reduce_scatter | solution.py:118
  286.7 91.7 %reduce-scatter.3.cloned.1.call-done = f32[32,128]{1,0:T(8,128)} async-done(((f32[512,128]{1,0:T(8,128)}), f32[32,128]{1,0:T(8,128)}) %reduce-scatter.3.cloned.1.call-update) | async-done | bytes 16400 | tf_op jit(solution)/shard_map/reduce_scatter | solution.py:117
  (166 shorter events, 65.6 us)
Async XLA Ops:
  7.2 6.9 %copy-start = (f32[512,128]{1,0:T(8,128)S(1)}, f32[512,128]{1,0:T(8,128)}, u32[]{:S(2)}) copy-start(f32[512,128]{1,0:T(8,128)} %param.14) | copy-start | bytes 786436
  7.2 12.5 %copy-start.2 = (f32[512,128]{1,0:T(8,128)S(1)}, f32[512,128]{1,0:T(8,128)}, u32[]{:S(2)}) copy-start(f32[512,128]{1,0:T(8,128)} %param.15) | copy-start | bytes 786436
  7.2 158.4 %all-gather.6.cloned.1.call-start = ((), (), s32[]{:S(2)}) async-start(), calls=%async_computation.4 | async-start | bytes 8650752 | tf_op jit(solution)/shard_map/all_gather | solution.py:12
  15.8 187.7 %all-gather.4.cloned.1.call-start = ((), (), s32[]{:S(2)}) async-start(), calls=%async_computation.2 | async-start | bytes 8650752 | tf_op jit(solution)/shard_map/all_gather | solution.py:12
  21.4 265.3 %reduce-scatter.5.cloned.1.call-start = ((), (), s32[]{:S(2)}) async-start(), calls=%async_computation.5 | async-start | bytes 278528 | tf_op jit(solution)/shard_map/reduce_scatter | solution.py:118
  203.2 45.2 %copy-start.1 = (f32[512,512]{0,1:T(8,128)S(1)}, f32[512,512]{0,1:T(8,128)}, u32[]{:S(2)}) copy-start(f32[512,512]{0,1:T(8,128)} %get-tuple-element.242) | copy-start | bytes 3145732
  203.2 175.2 %reduce-scatter.3.cloned.1.call-start = ((), (), s32[]{:S(2)}) async-start(), calls=%async_computation.3 | async-start | bytes 278528 | tf_op jit(solution)/shard_map/reduce_scatter | solution.py:117
Sparse Core Ops, SparseCore 0:
  15.9 85.2 all-gather.5
  103.4 75.7 all-gather.3
  203.3 83.3 reduce-scatter.4
  291.7 86.6 reduce-scatter.2
where the time goes:
time: 389 us; the launch traced here: 385 us
  waiting for transfers between devices  128 us (33%)
  other arithmetic  71.8 us (18%)
  matrix products  69.7 us (18%)
  blocking collectives  55.5 us (14%)
  local copies, waits for them, and re-layouts  22.8 us (6%)
  loops' own time  22.4 us (6%)
  between operations  14.6 us (4%)
    reduce_scatter x1, waiting for transfers between devices, per_device(): lax.psum_scatter(block_b + carry_b, 'head', scatter_dimension=0, tiled=True)  91.7 us
    select_n x62, other arithmetic, step(): jnp.where(position < mine, new, old)  65.6 us
    unnamed x1, blocking collectives  55.5 us
    reduce_scatter x1, waiting for transfers between devices, per_device(): lax.psum_scatter(block_c + carry_c, 'head', scatter_dimension=0, tiled=True)  35.9 us
    dot_general x8, matrix products, one_head(): pair_weights = jnp.einsum('tp,sp->ts', own_grad, own_in, precision=highest)  28.2 us
    dot_general x8, matrix products, one_head(): back_flow = jnp.einsum('ts,tp->sp', mixing, own_grad, precision=highest)  23.2 us
    another operation x1, loops' own time, per_device(): lax.scan(one_head, start_carry, jnp.arange(head_count, dtype=jnp.int32))  20.5 us
    rev x2, local copies, waits for them, and re-layouts, prefix(): pieces = jax.tree.map(lambda part: part[::-1], pieces)  8.32 us
  transfers between devices with their start and end apart: 4, of which 2 were waited for; matrix products, arithmetic and copies ran while one was open for 40% of the time, Pallas kernels for 0%

commit v1 on v0

v1 whole, which is shorter than its diff:
```python
import jax
import jax.numpy as jnp
from jax import lax
from jax.experimental import pallas as pl
from jax.experimental.pallas import tpu as pltpu
from jax.sharding import PartitionSpec as P

sudden_falloff = 0.35
highest = lax.Precision.HIGHEST
HEADS_PER_STEP = 2


def step_table(decay_codes):
    levels = jnp.arange(16, dtype=jnp.int32)
    values = 0.5 * 4.0 ** (levels.astype(jnp.float32) / 15.0)
    matching_label = decay_codes[None, :, :] == levels[:, None, None]
    return jnp.sum(jnp.where(matching_label, values[:, None, None], 0.0), axis=0)


def spread_heads(per_head, head_width):
    head_count, tok_count = per_head.shape
    wide = jnp.broadcast_to(per_head.T[:, :, None], (tok_count, head_count, head_width))
    return wide.reshape(tok_count, head_count * head_width)


def block_kernel(cum_row_ref, cum_col_ref, scores_t_ref, in_ref, grad_ref, flow_ref, acc_ref):
    step = pl.program_id(0)

    @pl.when(step == 0)
    def _():
        acc_ref[...] = jnp.zeros_like(acc_ref)

    tok = scores_t_ref.shape[0]
    width = in_ref.shape[1] // HEADS_PER_STEP
    rows = lax.broadcasted_iota(jnp.int32, (tok, tok), 0)
    cols = lax.broadcasted_iota(jnp.int32, (tok, tok), 1)
    later = cols >= rows
    scores_t = scores_t_ref[...]
    for k in range(HEADS_PER_STEP):
        gap = cum_row_ref[k] - cum_col_ref[k]
        decay_t = jnp.where(later, jnp.exp(jnp.where(later, gap, 0.0)), 0.0)
        own_in = in_ref[:, k * width:(k + 1) * width]
        own_grad = grad_ref[:, k * width:(k + 1) * width]
        flow_ref[:, k * width:(k + 1) * width] = jnp.dot(
            scores_t * decay_t, own_grad, precision=highest, preferred_element_type=jnp.float32
        )
        pair_t = lax.dot_general(
            own_in, own_grad, (((1,), (1,)), ((), ())), precision=highest,
            preferred_element_type=jnp.float32,
        )
        acc_ref[...] += pair_t * decay_t


def block_terms(cumul, scores_t, scaled_in, out_grad):
    head_count, tok = cumul.shape
    chan = scaled_in.shape[1]
    lanes = chan // head_count * HEADS_PER_STEP
    cum_row = cumul.reshape(head_count, 1, tok)
    cum_col = cumul.reshape(head_count, tok, 1)
    return pl.pallas_call(
        block_kernel,
        grid=(head_count // HEADS_PER_STEP,),
        in_specs=[
            pl.BlockSpec((HEADS_PER_STEP, 1, tok), lambda j: (j, 0, 0)),
            pl.BlockSpec((HEADS_PER_STEP, tok, 1), lambda j: (j, 0, 0)),
            pl.BlockSpec((tok, tok), lambda j: (0, 0)),
            pl.BlockSpec((tok, lanes), lambda j: (0, j)),
            pl.BlockSpec((tok, lanes), lambda j: (0, j)),
        ],
        out_specs=[
            pl.BlockSpec((tok, lanes), lambda j: (0, j)),
            pl.BlockSpec((tok, tok), lambda j: (0, 0)),
        ],
        out_shape=[
            jax.ShapeDtypeStruct((tok, chan), jnp.float32),
            jax.ShapeDtypeStruct((tok, tok), jnp.float32),
        ],
    )(cum_row, cum_col, scores_t, scaled_in, out_grad)


def pack(state, total):
    head_count, width, state_width = state.shape
    tot_rows = jnp.zeros((8, state_width), jnp.float32)
    tot_rows = lax.dynamic_update_slice(
        tot_rows, jnp.broadcast_to(total[:, None], (head_count, state_width)), (0, 0)
    )
    return jnp.concatenate([state.reshape(head_count * width, state_width), tot_rows], axis=0)


def join(earlier, later, head_count, width):
    rows = head_count * width
    later_tot = later[rows:rows + head_count, 0]
    scale = jnp.concatenate(
        [jnp.repeat(jnp.exp(later_tot), width), jnp.ones((8,), jnp.float32)]
    )
    return scale[:, None] * earlier + later


def chip_scan(state, total, backward):
    count = lax.axis_size("seq")
    index = lax.axis_index("seq")
    head_count, width, state_width = state.shape
    half = head_count // 2
    position = count - 1 - index if backward else index
    sub = position % 2

    def move(value, delta):
        if backward:
            pairs = [(i, i - delta) for i in range(delta, count)]
        else:
            pairs = [(i, i + delta) for i in range(count - delta)]
        return lax.ppermute(value, "seq", pairs)

    def heads(lo):
        return pack(
            lax.dynamic_slice_in_dim(state, lo, half, 0),
            lax.dynamic_slice_in_dim(total, lo, half, 0),
        )

    swap = [(i, i ^ 1) for i in range(count)]
    own_half = heads(sub * half)
    other_half = heads((1 - sub) * half)
    got = lax.ppermute(other_half, "seq", swap)
    first = jnp.where(sub == 0, own_half, got)
    second = jnp.where(sub == 0, got, own_half)
    chip_total = join(first, second, half, width)
    running = move(chip_total, 2)
    distance = 1
    while 2 * distance < count:
        running = join(move(running, 2 * distance), running, half, width)
        distance *= 2
    after_first = join(running, first, half, width)
    outgoing = jnp.where(sub == 0, after_first, running)
    incoming = lax.ppermute(outgoing, "seq", swap)
    mine = jnp.where(sub == 0, running, after_first)
    low = jnp.where(sub == 0, mine, incoming)
    high = jnp.where(sub == 0, incoming, mine)
    rows = half * width
    return jnp.concatenate([low[:rows], high[:rows]], axis=0).reshape(
        head_count, width, state_width
    )


def per_device(
    head_inputs, input_proj, output_mapping, decay_codes, boundary, head_decay_speeds, out_grad
):
    tok_count = head_inputs.shape[0]
    head_count = decay_codes.shape[0]
    head_width = head_inputs.shape[1] // head_count
    state_width = input_proj.shape[1]
    increment_length = step_table(decay_codes)
    logarithm_decay = (
        -head_decay_speeds[:, None] * increment_length
        - sudden_falloff * boundary.astype(jnp.float32)[None, :]
    )
    cumul = jnp.cumsum(logarithm_decay, axis=1)
    group_total = cumul[:, -1]
    to_end = spread_heads(jnp.exp(group_total[:, None] - cumul), head_width)
    from_start = spread_heads(jnp.exp(cumul), head_width)
    scaled_in = head_inputs * spread_heads(increment_length, head_width)
    weighted_in = scaled_in * to_end
    weighted_grad = out_grad * from_start
    ends = jnp.einsum("tk,tn->kn", weighted_in, input_proj, precision=highest)
    starts = jnp.einsum("tk,tn->kn", weighted_grad, output_mapping, precision=highest)
    state_in = chip_scan(
        ends.reshape(head_count, head_width, state_width), group_total, False
    )
    state_grad = chip_scan(
        starts.reshape(head_count, head_width, state_width), group_total, True
    )

    scores_t = jnp.einsum("sn,tn->st", input_proj, output_mapping, precision=highest)
    grad_scaled, grad_scores_t = block_terms(cumul, scores_t, scaled_in, out_grad)
    block_b = jnp.dot(grad_scores_t, output_mapping, precision=highest)
    block_c = jnp.einsum("st,sn->tn", grad_scores_t, input_proj, precision=highest)

    flat_in = state_in.reshape(head_count * head_width, state_width)
    flat_grad = state_grad.reshape(head_count * head_width, state_width)
    carry_c = jnp.dot(weighted_grad, flat_in, precision=highest)
    carry_b = jnp.dot(weighted_in, flat_grad, precision=highest)
    carry_x = to_end * jnp.einsum("tn,kn->tk", input_proj, flat_grad, precision=highest)
    grad_inputs = (grad_scaled + carry_x) * spread_heads(increment_length, head_width)

    both = jnp.concatenate([block_b + carry_b, block_c + carry_c], axis=1)
    parts = lax.axis_size("head")
    spread = lax.all_to_all(both, "head", 0, 0, tiled=True)
    summed = spread.reshape(parts, tok_count // parts, 2 * state_width).sum(axis=0)
    return (grad_inputs, summed[:, :state_width], summed[:, state_width:])


def solution(mesh):
    return jax.shard_map(
        per_device,
        mesh=mesh,
        in_specs=(
            P("seq", "head"),
            P("seq", None),
            P("seq", None),
            P("head", "seq"),
            P("seq"),
            P("head"),
            P("seq", "head"),
        ),
        out_specs=(P("seq", "head"), P(("seq", "head"), None), P(("seq", "head"), None)),
        check_vma=False,
    )
```

time: 389 us -> 175 us (0.45)
  the two profiles are of different devices: /device:TPU:1 before, /device:TPU:384 now
where the time goes in v1:
time: 175 us; the launch traced here: 174 us
  starting transfers between devices  55.2 us (32%)
  local copies, waits for them, and re-layouts  31.9 us (18%)
  waiting for transfers between devices  27.4 us (16%)
  other arithmetic  23.3 us (13%)
  Pallas kernels  17.8 us (10%)
  matrix products  16.7 us (10%)
    ppermute x10, starting transfers between devices, move(): return lax.ppermute(value, 'seq', pairs)  32 us
    ppermute x10, waiting for transfers between devices, move(): return lax.ppermute(value, 'seq', pairs)  19 us
    pallas_call x1, Pallas kernels, block_terms(): pl.pallas_call(block_kernel, grid=(head_count // HEADS_PER_STEP,), in_spe...  17.8 us
    all_to_all x1, starting transfers between devices, per_device(): spread = lax.all_to_all(both, 'head', 0, 0, tiled=True)  14.5 us
    add x8, other arithmetic, join(): return scale[:, None] * earlier + later  12.4 us
    all_to_all x1, waiting for transfers between devices, per_device(): spread = lax.all_to_all(both, 'head', 0, 0, tiled=True)  8.45 us
    reshape x12, local copies, waits for them, and re-layouts, join(): jnp.repeat(jnp.exp(later_tot), width)  6.43 us
    exp x12, local copies, waits for them, and re-layouts, join(): jnp.exp(later_tot)  6.14 us
  transfers between devices with their start and end apart: 15, of which 7 were waited for; matrix products, arithmetic and copies ran while one was open for 34% of the time, Pallas kernels for 10%

profile of v1, /device:TPU:384, one launch (start us, length us, event | category | flops | bytes accessed | tf_op | source)
XLA Modules:
  0.0 173.6 jit_solution(876123581319235241)
XLA Ops:
  3.0 1.1 reduce-window.6
  5.1 1.6 copy.38
  9.4 1.9 %collective-permute-start = (f32[264,128]{1,0:T(8,128)}, f32[264,128]{1,0:T(8,128)}, u32[]{:S(2)}, u32[]{:S(2)}) collective-permute-start(f32[264,128]{1,0:T(8,128)} %pad_maximum_fusion.4), channel_id=1, source_target_pairs={{0,16},{16,0},{32,48},{48,32},{64,80},{80,64},{96,112},{112,96},{1... | collective-permute-start | bytes 405512 | tf_op jit(solution)/shard_map/ppermute | solution.py:123
  13.2 1.1 broadcast_in_dim.53
  14.3 1.6 copy.40
  15.9 1.4 mul.151.in_ref
  17.3 1.8 %fusion.3 = f32[512,128]{1,0:T(8,128)S(1)} fusion(f32[512,128]{1,0:T(8,128)S(1)} %copy-done, f32[512,512]{1,0:T(8,128)S(1)} %mul.151.in_ref, f32[512,512]{1,0:T(8,128)S(1)} %copy.40), kind=kOutput, calls=%fused_computation.8 | convolution fusion | flops 402915328 | bytes 2621440 | tf_op jit(solution)/shard_map/tk,tn->kn/dot_general | solution.py:163
  20.6 2.6 %collective-permute-start.7 = (f32[264,128]{1,0:T(8,128)}, f32[264,128]{1,0:T(8,128)}, u32[]{:S(2)}, u32[]{:S(2)}) collective-permute-start(f32[264,128]{1,0:T(8,128)} %pad_maximum_fusion.6), channel_id=1, source_target_pairs={{0,16},{16,0},{32,48},{48,32},{64,80},{80,64},{96,112},{112,96},{1... | collective-permute-start | bytes 405512 | tf_op jit(solution)/shard_map/ppermute | solution.py:123
  23.8 2.0 %fusion.38.scores_t_ref = f32[512,512]{1,0:T(8,128)} fusion(f32[512,128]{1,0:T(8,128)S(1)} %copy-done, f32[512,128]{1,0:T(8,128)S(1)} %copy-done.5), kind=kOutput, calls=%fused_computation.96 | convolution fusion | flops 402653184 | bytes 1572864 | tf_op jit(solution)/shard_map/sn,tn->st/dot_general | solution.py:172
  25.8 2.0 %copy.37.cum_col_ref = f32[8,512,1]{2,1,0:T(8,128)} copy(f32[8,512,1]{1,0,2:T(8,128)S(1)} %bitcast.57) | data formatting | bytes 32768 | tf_op jit(solution)/shard_map/reduce_window_sum
  27.8 17.8 %shard_map.94 = (f32[512,512]{1,0:T(8,128)}, f32[512,512]{1,0:T(8,128)}) custom-call(f32[8,1,512]{2,1,0:T(1,128)} %bitcast.59, f32[8,512,1]{2,1,0:T(8,128)} %copy.37.cum_col_ref, f32[512,512]{1,0:T(8,128)} %fusion.38.scores_t_ref, f32[512,512]{1,0:T(8,128)} %copy-done.1, f32[512,512]{1,0:T(8,128)} %grad_ref.1), custom_call_target="tpu_custom_call" | custom-call | tf_op jit(solution)/shard_map/pallas_call | solution.py:60
  45.6 2.8 %fusion.41 = f32[512,128]{0,1:T(8,128)} fusion(f32[512,512]{1,0:T(8,128)} %get-tuple-element.6, f32[512,128]{1,0:T(8,128)S(1)} %copy-done), kind=kOutput, calls=%fused_computation.99 | convolution fusion | flops 402653184 | bytes 1572864 | tf_op jit(solution)/shard_map/st,sn->tn/dot_general | solution.py:175
  48.4 2.9 %fusion.40 = f32[512,128]{0,1:T(8,128)} fusion(f32[512,512]{1,0:T(8,128)S(1)} %copy-done.3, f32[512,128]{1,0:T(8,128)} %param.9), kind=kOutput, calls=%fused_computation.98 | convolution fusion | flops 402653184 | bytes 1572864 | tf_op jit(solution)/shard_map/dot_general | solution.py:174
  52.3 1.8 %multiply_add_fusion.11 = (f32[264,128]{1,0:T(8,128)}, f32[264,128]{1,0:T(8,128)}) fusion(f32[264,128]{1,0:T(8,128)} %copy-done.7, f32[264]{0:T(512)S(1)} %concatenate.59, f32[264,128]{1,0:T(8,128)} %collective-permute-done, f32[264]{0:T(512)S(1)} %get-tuple-element.34, f32[256,128]{1,0:T(8,128)S(1)} %bitcast.49, pred[]{:T(512)S(6)} %eq.16), kind=kLoop, calls=%fused_computation.36 | loop fusion | flops 135168 | bytes 673857 | tf_op jit(solution)/shard_map/add | solution.py:96
  54.1 4.1 %collective-permute-start.1 = (f32[264,128]{1,0:T(8,128)}, f32[264,128]{1,0:T(8,128)}, u32[]{:S(2)}, u32[]{:S(2)}) collective-permute-start(f32[264,128]{1,0:T(8,128)} %get-tuple-element.13), channel_id=1, source_target_pairs={{32,0},{48,16},{64,32},{80,48},{96,64},{112,80},{128,96},{144,112}... | collective-permute-start | bytes 405512 | tf_op jit(solution)/shard_map/ppermute | solution.py:112
  58.3 1.1 fusion.14
  59.6 1.7 multiply_add_fusion.5
  62.1 1.9 %collective-permute-start.8 = (f32[264,128]{1,0:T(8,128)}, f32[264,128]{1,0:T(8,128)}, u32[]{:S(2)}, u32[]{:S(2)}) collective-permute-start(f32[264,128]{1,0:T(8,128)} %get-tuple-element.11), channel_id=1, source_target_pairs={{0,32},{16,48},{32,64},{48,80},{64,96},{80,112},{96,128},{112,144}... | collective-permute-start | bytes 405512 | tf_op jit(solution)/shard_map/ppermute | solution.py:112
  64.5 5.1 %collective-permute-start.2 = (f32[264,128]{1,0:T(8,128)}, f32[264,128]{1,0:T(8,128)}, u32[]{:S(2)}, u32[]{:S(2)}) collective-permute-start(f32[264,128]{1,0:T(8,128)} %collective-permute-done.1), channel_id=1, source_target_pairs={{32,0},{48,16},{64,32},{80,48},{96,64},{112,80},{128,96},{144,112}... | collective-permute-start | bytes 405512 | tf_op jit(solution)/shard_map/ppermute | solution.py:112
  72.6 1.9 %collective-permute-start.9 = (f32[264,128]{1,0:T(8,128)}, f32[264,128]{1,0:T(8,128)S(1)}, u32[]{:S(2)}, u32[]{:S(2)}) collective-permute-start(f32[264,128]{1,0:T(8,128)} %collective-permute-done.8), channel_id=1, source_target_pairs={{0,32},{16,48},{32,64},{48,80},{64,96},{80,112},{96,128},{112,144}... | collective-permute-start | bytes 405512 | tf_op jit(solution)/shard_map/ppermute | solution.py:112
  74.5 1.1 multiply_add_fusion.10
  75.6 3.2 %collective-permute-start.3 = (f32[264,128]{1,0:T(8,128)S(1)}, f32[264,128]{1,0:T(8,128)}, u32[]{:S(2)}, u32[]{:S(2)}) collective-permute-start(f32[264,128]{1,0:T(8,128)S(1)} %multiply_add_fusion.10), channel_id=1, source_target_pairs={{64,0},{80,16},{96,32},{112,48},{128,64},{144,80},{160,96},{176,11... | collective-permute-start | bytes 405512 | tf_op jit(solution)/shard_map/ppermute | solution.py:112
  78.8 2.4 %collective-permute-done.9 = f32[264,128]{1,0:T(8,128)S(1)} collective-permute-done((f32[264,128]{1,0:T(8,128)}, f32[264,128]{1,0:T(8,128)S(1)}, u32[]{:S(2)}, u32[]{:S(2)}) %collective-permute-start.9) | collective-permute-done | bytes 135200 | tf_op jit(solution)/shard_map/ppermute | solution.py:112
  81.2 1.7 multiply_add_fusion.4
  84.4 1.9 %collective-permute-start.10 = (f32[264,128]{1,0:T(8,128)}, f32[264,128]{1,0:T(8,128)}, u32[]{:S(2)}, u32[]{:S(2)}) collective-permute-start(f32[264,128]{1,0:T(8,128)} %multiply_add_fusion.4), channel_id=1, source_target_pairs={{0,64},{16,80},{32,96},{48,112},{64,128},{80,144},{96,160},{112,17... | collective-permute-start | bytes 405512 | tf_op jit(solution)/shard_map/ppermute | solution.py:112
  87.7 1.3 reshape.202
  89.8 1.7 multiply_add_fusion.9
  91.4 4.3 %collective-permute-start.4 = (f32[264,128]{1,0:T(8,128)}, f32[264,128]{1,0:T(8,128)}, u32[]{:S(2)}, u32[]{:S(2)}) collective-permute-start(f32[264,128]{1,0:T(8,128)} %multiply_add_fusion.9), channel_id=1, source_target_pairs={{128,0},{144,16},{160,32},{176,48},{192,64},{208,80},{224,96},{240... | collective-permute-start | bytes 405512 | tf_op jit(solution)/shard_map/ppermute | solution.py:112
  95.9 1.1 multiply_add_fusion.3
  99.1 1.3 collective-permute-start.11
  101.2 1.3 reshape.203
  103.2 3.0 %collective-permute-done.4 = f32[264,128]{1,0:T(8,128)} collective-permute-done((f32[264,128]{1,0:T(8,128)}, f32[264,128]{1,0:T(8,128)}, u32[]{:S(2)}, u32[]{:S(2)}) %collective-permute-start.4) | collective-permute-done | bytes 135200 | tf_op jit(solution)/shard_map/ppermute | solution.py:112
  106.2 1.7 multiply_add_fusion.8
  107.9 7.0 %collective-permute-start.5 = (f32[264,128]{1,0:T(8,128)}, f32[264,128]{1,0:T(8,128)}, u32[]{:S(2)}, u32[]{:S(2)}) collective-permute-start(f32[264,128]{1,0:T(8,128)} %multiply_add_fusion.8), channel_id=1, source_target_pairs={{256,0},{272,16},{288,32},{304,48},{320,64},{336,80},{352,96},{368... | collective-permute-start | bytes 405512 | tf_op jit(solution)/shard_map/ppermute | solution.py:112
  114.9 3.2 %collective-permute-done.11 = f32[264,128]{1,0:T(8,128)} collective-permute-done((f32[264,128]{1,0:T(8,128)S(1)}, f32[264,128]{1,0:T(8,128)}, u32[]{:S(2)}, u32[]{:S(2)}) %collective-permute-start.11) | collective-permute-done | bytes 135200 | tf_op jit(solution)/shard_map/ppermute | solution.py:112
  118.1 1.7 multiply_add_fusion.2
  119.8 1.3 collective-permute-start.12
  124.7 1.3 reshape.204
  126.8 9.1 %collective-permute-done.12 = f32[264,128]{1,0:T(8,128)S(1)} collective-permute-done((f32[264,128]{1,0:T(8,128)}, f32[264,128]{1,0:T(8,128)S(1)}, u32[]{:S(2)}, u32[]{:S(2)}) %collective-permute-start.12) | collective-permute-done | bytes 135200 | tf_op jit(solution)/shard_map/ppermute | solution.py:112
  135.9 1.1 fusion.10
  137.0 1.9 %collective-permute-start.13 = (f32[264,128]{1,0:T(8,128)S(1)}, f32[264,128]{1,0:T(8,128)S(1)}, u32[]{:S(2)}, u32[]{:S(2)}) collective-permute-start(f32[264,128]{1,0:T(8,128)S(1)} %get-tuple-element.18), channel_id=1, source_target_pairs={{0,16},{16,0},{32,48},{48,32},{64,80},{80,64},{96,112},{112,96},{1... | collective-permute-start | bytes 405512 | tf_op jit(solution)/shard_map/ppermute | solution.py:134
  138.9 1.2 fusion.12
  140.1 2.4 %collective-permute-start.6 = (f32[264,128]{1,0:T(8,128)S(1)}, f32[264,128]{1,0:T(8,128)S(1)}, u32[]{:S(2)}, u32[]{:S(2)}) collective-permute-start(f32[264,128]{1,0:T(8,128)S(1)} %get-tuple-element.20), channel_id=1, source_target_pairs={{0,16},{16,0},{32,48},{48,32},{64,80},{80,64},{96,112},{112,96},{1... | collective-permute-start | bytes 405512 | tf_op jit(solution)/shard_map/ppermute | solution.py:134
  142.6 1.8 %convolution_add_fusion = f32[512,128]{0,1:T(8,128)S(1)} fusion(f32[512,128]{0,1:T(8,128)} %fusion.41, f32[512,512]{0,1:T(8,128)S(1)} %bitcast_multiply_fusion, f32[256,128]{1,0:T(8,128)S(1)} %get-tuple-element.22, f32[256,128]{1,0:T(8,128)S(1)} %get-tuple-element.21), kind=kOutput, calls=%fused_computation.4 | convolution fusion | flops 402784256 | bytes 1835008 | tf_op jit(solution)/shard_map/dot_general | solution.py:179
  144.4 1.2 convolution_add_fusion.1
  146.7 14.5 %all-to-all-start = ((f32[16,32,256]{2,1,0:T(8,128)}), f32[16,32,256]{2,1,0:T(8,128)S(1)}, u32[]{:S(2)}, u32[]{:S(2)}) async-start(f32[16,32,256]{2,1,0:T(8,128)} %bitcast.18), calls=%async_computation | async-start | bytes 1048576 | tf_op jit(solution)/shard_map/all_to_all | solution.py:186
  161.2 3.3 %fusion.2 = f32[512,512]{1,0:T(8,128)} fusion(f32[512,512]{1,0:T(8,128)S(1)} %copy.36, f32[512,512]{1,0:T(8,128)} %get-tuple-element.5, f32[512,512]{1,0:T(8,128)S(1)} %copy.40, f32[512,128]{1,0:T(8,128)S(1)} %copy-done, f32[256,128]{1,0:T(8,128)S(1)} %get-tuple-element.24, f32[256,128]{1,0:T(8,128)S(1)} %get-tuple-element.23), kind=kOutput, calls=%fused_computation.3 | convolution fusion | flops 403505152 | bytes 4718592 | tf_op jit(solution)/shard_map/tn,kn->tk/dot_general | solution.py:181
  164.5 8.5 %all-to-all-done = f32[16,32,256]{2,1,0:T(8,128)S(1)} async-done(((f32[16,32,256]{2,1,0:T(8,128)}), f32[16,32,256]{2,1,0:T(8,128)S(1)}, u32[]{:S(2)}, u32[]{:S(2)}) %all-to-all-start) | async-done | bytes 524320 | tf_op jit(solution)/shard_map/all_to_all | solution.py:186
  (112 shorter events, 28.9 us)
Async XLA Ops:
  0.6 16.7 %copy-start = (f32[512,128]{1,0:T(8,128)S(1)}, f32[512,128]{1,0:T(8,128)}, u32[]{:S(2)}) copy-start(f32[512,128]{1,0:T(8,128)} %param.8) | copy-start | bytes 786436
  2.9 3.9 %copy-start.9 = (f32[8,512]{1,0:T(8,128)}, f32[8,512]{1,0:T(8,128)S(1)}, u32[]{:S(2)}) copy-start(f32[8,512]{1,0:T(8,128)S(1)} %select_reduce_fusion) | copy-start | bytes 49156
  5.1 1.7 copy-start.4
  9.4 41.9 %collective-permute-start = (f32[264,128]{1,0:T(8,128)}, f32[264,128]{1,0:T(8,128)}, u32[]{:S(2)}, u32[]{:S(2)}) collective-permute-start(f32[264,128]{1,0:T(8,128)} %pad_maximum_fusion.4), channel_id=1, source_target_pairs={{0,16},{16,0},{32,48},{48,32},{64,80},{80,64},{96,112},{112,96},{1... | collective-permute-start | bytes 405512 | tf_op jit(solution)/shard_map/ppermute | solution.py:123
  17.3 8.5 %copy-start.1 = (f32[512,512]{1,0:T(8,128)}, f32[512,512]{1,0:T(8,128)S(1)}, u32[]{:S(2)}) copy-start(f32[512,512]{1,0:T(8,128)S(1)} %mul.151.in_ref) | copy-start | bytes 3145732
  17.3 2.5 %copy-start.12 = (f32[4]{0:T(128)S(1)}, f32[4]{0:T(128)}, u32[]{:S(2)}) copy-start(f32[4]{0:T(128)} %get-tuple-element.8) | copy-start | bytes 52
  17.3 6.5 %copy-start.5 = (f32[512,128]{1,0:T(8,128)S(1)}, f32[512,128]{1,0:T(8,128)}, u32[]{:S(2)}) copy-start(f32[512,128]{1,0:T(8,128)} %param.9) | copy-start | bytes 786436
  20.6 37.6 %collective-permute-start.7 = (f32[264,128]{1,0:T(8,128)}, f32[264,128]{1,0:T(8,128)}, u32[]{:S(2)}, u32[]{:S(2)}) collective-permute-start(f32[264,128]{1,0:T(8,128)} %pad_maximum_fusion.6), channel_id=1, source_target_pairs={{0,16},{16,0},{32,48},{48,32},{64,80},{80,64},{96,112},{112,96},{1... | collective-permute-start | bytes 405512 | tf_op jit(solution)/shard_map/ppermute | solution.py:123
  45.6 2.8 %copy-start.3 = (f32[512,512]{1,0:T(8,128)S(1)}, f32[512,512]{1,0:T(8,128)}, u32[]{:S(2)}) copy-start(f32[512,512]{1,0:T(8,128)} %get-tuple-element.6) | copy-start | bytes 3145732
  45.6 5.7 %copy-start.10 = (f32[4]{0:T(128)S(1)}, f32[4]{0:T(128)}, u32[]{:S(2)}) copy-start(f32[4]{0:T(128)} %get-tuple-element.7) | copy-start | bytes 52
  45.6 5.7 %copy-start.11 = (f32[4]{0:T(128)S(1)}, f32[4]{0:T(128)}, u32[]{:S(2)}) copy-start(f32[4]{0:T(128)} %get-tuple-element.9) | copy-start | bytes 52
  51.4 0.6 copy-start.7
  54.1 10.4 %collective-permute-start.1 = (f32[264,128]{1,0:T(8,128)}, f32[264,128]{1,0:T(8,128)}, u32[]{:S(2)}, u32[]{:S(2)}) collective-permute-start(f32[264,128]{1,0:T(8,128)} %get-tuple-element.13), channel_id=1, source_target_pairs={{32,0},{48,16},{64,32},{80,48},{96,64},{112,80},{128,96},{144,112}... | collective-permute-start | bytes 405512 | tf_op jit(solution)/shard_map/ppermute | solution.py:112
  61.4 2.7 %copy-start.8 = (f32[264,128]{1,0:T(8,128)}, f32[264,128]{1,0:T(8,128)S(1)}, u32[]{:S(2)}) copy-start(f32[264,128]{1,0:T(8,128)S(1)} %get-tuple-element.12) | copy-start | bytes 405508
  62.1 9.5 %collective-permute-start.8 = (f32[264,128]{1,0:T(8,128)}, f32[264,128]{1,0:T(8,128)}, u32[]{:S(2)}, u32[]{:S(2)}) collective-permute-start(f32[264,128]{1,0:T(8,128)} %get-tuple-element.11), channel_id=1, source_target_pairs={{0,32},{16,48},{32,64},{48,80},{64,96},{80,112},{96,128},{112,144}... | collective-permute-start | bytes 405512 | tf_op jit(solution)/shard_map/ppermute | solution.py:112
  64.5 10.0 %collective-permute-start.2 = (f32[264,128]{1,0:T(8,128)}, f32[264,128]{1,0:T(8,128)}, u32[]{:S(2)}, u32[]{:S(2)}) collective-permute-start(f32[264,128]{1,0:T(8,128)} %collective-permute-done.1), channel_id=1, source_target_pairs={{32,0},{48,16},{64,32},{80,48},{96,64},{112,80},{128,96},{144,112}... | collective-permute-start | bytes 405512 | tf_op jit(solution)/shard_map/ppermute | solution.py:112
  72.6 8.6 %collective-permute-start.9 = (f32[264,128]{1,0:T(8,128)}, f32[264,128]{1,0:T(8,128)S(1)}, u32[]{:S(2)}, u32[]{:S(2)}) collective-permute-start(f32[264,128]{1,0:T(8,128)} %collective-permute-done.8), channel_id=1, source_target_pairs={{0,32},{16,48},{32,64},{48,80},{64,96},{80,112},{96,128},{112,144}... | collective-permute-start | bytes 405512 | tf_op jit(solution)/shard_map/ppermute | solution.py:112
  75.6 14.2 %collective-permute-start.3 = (f32[264,128]{1,0:T(8,128)S(1)}, f32[264,128]{1,0:T(8,128)}, u32[]{:S(2)}, u32[]{:S(2)}) collective-permute-start(f32[264,128]{1,0:T(8,128)S(1)} %multiply_add_fusion.10), channel_id=1, source_target_pairs={{64,0},{80,16},{96,32},{112,48},{128,64},{144,80},{160,96},{176,11... | collective-permute-start | bytes 405512 | tf_op jit(solution)/shard_map/ppermute | solution.py:112
  84.4 11.5 %collective-permute-start.10 = (f32[264,128]{1,0:T(8,128)}, f32[264,128]{1,0:T(8,128)}, u32[]{:S(2)}, u32[]{:S(2)}) collective-permute-start(f32[264,128]{1,0:T(8,128)} %multiply_add_fusion.4), channel_id=1, source_target_pairs={{0,64},{16,80},{32,96},{48,112},{64,128},{80,144},{96,160},{112,17... | collective-permute-start | bytes 405512 | tf_op jit(solution)/shard_map/ppermute | solution.py:112
  91.4 14.8 %collective-permute-start.4 = (f32[264,128]{1,0:T(8,128)}, f32[264,128]{1,0:T(8,128)}, u32[]{:S(2)}, u32[]{:S(2)}) collective-permute-start(f32[264,128]{1,0:T(8,128)} %multiply_add_fusion.9), channel_id=1, source_target_pairs={{128,0},{144,16},{160,32},{176,48},{192,64},{208,80},{224,96},{240... | collective-permute-start | bytes 405512 | tf_op jit(solution)/shard_map/ppermute | solution.py:112
  99.1 19.0 %collective-permute-start.11 = (f32[264,128]{1,0:T(8,128)S(1)}, f32[264,128]{1,0:T(8,128)}, u32[]{:S(2)}, u32[]{:S(2)}) collective-permute-start(f32[264,128]{1,0:T(8,128)S(1)} %multiply_add_fusion.3), channel_id=1, source_target_pairs={{0,128},{16,144},{32,160},{48,176},{64,192},{80,208},{96,224},{112... | collective-permute-start | bytes 405512 | tf_op jit(solution)/shard_map/ppermute | solution.py:112
  107.9 31.0 %collective-permute-start.5 = (f32[264,128]{1,0:T(8,128)}, f32[264,128]{1,0:T(8,128)}, u32[]{:S(2)}, u32[]{:S(2)}) collective-permute-start(f32[264,128]{1,0:T(8,128)} %multiply_add_fusion.8), channel_id=1, source_target_pairs={{256,0},{272,16},{288,32},{304,48},{320,64},{336,80},{352,96},{368... | collective-permute-start | bytes 405512 | tf_op jit(solution)/shard_map/ppermute | solution.py:112
  119.8 16.1 %collective-permute-start.12 = (f32[264,128]{1,0:T(8,128)}, f32[264,128]{1,0:T(8,128)S(1)}, u32[]{:S(2)}, u32[]{:S(2)}) collective-permute-start(f32[264,128]{1,0:T(8,128)} %multiply_add_fusion.2), channel_id=1, source_target_pairs={{0,256},{16,272},{32,288},{48,304},{64,320},{80,336},{96,352},{112... | collective-permute-start | bytes 405512 | tf_op jit(solution)/shard_map/ppermute | solution.py:112
  126.7 17.7 %copy-start.2 = (f32[512,512]{1,0:T(8,128)S(1)}, f32[512,512]{1,0:T(8,128)}, u32[]{:S(2)}) copy-start(f32[512,512]{1,0:T(8,128)} %copy-done.1) | copy-start | bytes 3145732
  126.8 17.7 %copy-start.6 = (f32[512,128]{0,1:T(8,128)S(1)}, f32[512,128]{0,1:T(8,128)}, u32[]{:S(2)}) copy-start(f32[512,128]{0,1:T(8,128)} %fusion.40) | copy-start | bytes 786436
  137.0 5.5 %collective-permute-start.13 = (f32[264,128]{1,0:T(8,128)S(1)}, f32[264,128]{1,0:T(8,128)S(1)}, u32[]{:S(2)}, u32[]{:S(2)}) collective-permute-start(f32[264,128]{1,0:T(8,128)S(1)} %get-tuple-element.18), channel_id=1, source_target_pairs={{0,16},{16,0},{32,48},{48,32},{64,80},{80,64},{96,112},{112,96},{1... | collective-permute-start | bytes 405512 | tf_op jit(solution)/shard_map/ppermute | solution.py:134
  140.1 4.3 %collective-permute-start.6 = (f32[264,128]{1,0:T(8,128)S(1)}, f32[264,128]{1,0:T(8,128)S(1)}, u32[]{:S(2)}, u32[]{:S(2)}) collective-permute-start(f32[264,128]{1,0:T(8,128)S(1)} %get-tuple-element.20), channel_id=1, source_target_pairs={{0,16},{16,0},{32,48},{48,32},{64,80},{80,64},{96,112},{112,96},{1... | collective-permute-start | bytes 405512 | tf_op jit(solution)/shard_map/ppermute | solution.py:134
  146.7 26.2 %all-to-all-start = ((f32[16,32,256]{2,1,0:T(8,128)}), f32[16,32,256]{2,1,0:T(8,128)S(1)}, u32[]{:S(2)}, u32[]{:S(2)}) async-start(f32[16,32,256]{2,1,0:T(8,128)} %bitcast.18), calls=%async_computation | async-start | bytes 1048576 | tf_op jit(solution)/shard_map/all_to_all | solution.py:186

commit v2 on v1

--- a/solution.py
+++ b/solution.py
@@ -78,67 +78,93 @@
     )(cum_row, cum_col, scores_t, scaled_in, out_grad)
 
 
-def pack(state, total):
-    head_count, width, state_width = state.shape
-    tot_rows = jnp.zeros((8, state_width), jnp.float32)
-    tot_rows = lax.dynamic_update_slice(
-        tot_rows, jnp.broadcast_to(total[:, None], (head_count, state_width)), (0, 0)
-    )
-    return jnp.concatenate([state.reshape(head_count * width, state_width), tot_rows], axis=0)
-
-
-def join(earlier, later, head_count, width):
-    rows = head_count * width
-    later_tot = later[rows:rows + head_count, 0]
-    scale = jnp.concatenate(
-        [jnp.repeat(jnp.exp(later_tot), width), jnp.ones((8,), jnp.float32)]
-    )
-    return scale[:, None] * earlier + later
-
-
-def chip_scan(state, total, backward):
-    count = lax.axis_size("seq")
-    index = lax.axis_index("seq")
-    head_count, width, state_width = state.shape
+def pack_total(total, state_width):
+    head_count = total.shape[0]
+    rows = jnp.zeros((8, state_width), jnp.float32)
+    return lax.dynamic_update_slice(
+        rows, jnp.broadcast_to(total[:, None], (head_count, state_width)), (0, 0)
+    )
+
+
+def join(earlier, later, later_total):
+    return jnp.exp(later_total)[:, None, None] * earlier + later
+
+
+def pick(flag, when_true, when_false):
+    return jnp.where(flag, when_true, when_false)
+
+
+def chip_scans(ends, starts, total):
+    chips = lax.axis_size("z")
+    chip = lax.axis_index("z")
+    core = lax.axis_index("core")
+    head_count, width, state_width = ends.shape
     half = head_count // 2
-    position = count - 1 - index if backward else index
-    sub = position % 2
-
-    def move(value, delta):
-        if backward:
-            pairs = [(i, i - delta) for i in range(delta, count)]
-        else:
-            pairs = [(i, i + delta) for i in range(count - delta)]
-        return lax.ppermute(value, "seq", pairs)
-
-    def heads(lo):
-        return pack(
-            lax.dynamic_slice_in_dim(state, lo, half, 0),
-            lax.dynamic_slice_in_dim(total, lo, half, 0),
-        )
-
-    swap = [(i, i ^ 1) for i in range(count)]
-    own_half = heads(sub * half)
-    other_half = heads((1 - sub) * half)
-    got = lax.ppermute(other_half, "seq", swap)
-    first = jnp.where(sub == 0, own_half, got)
-    second = jnp.where(sub == 0, got, own_half)
-    chip_total = join(first, second, half, width)
-    running = move(chip_total, 2)
-    distance = 1
-    while 2 * distance < count:
-        running = join(move(running, 2 * distance), running, half, width)
-        distance *= 2
-    after_first = join(running, first, half, width)
-    outgoing = jnp.where(sub == 0, after_first, running)
-    incoming = lax.ppermute(outgoing, "seq", swap)
-    mine = jnp.where(sub == 0, running, after_first)
-    low = jnp.where(sub == 0, mine, incoming)
-    high = jnp.where(sub == 0, incoming, mine)
     rows = half * width
-    return jnp.concatenate([low[:rows], high[:rows]], axis=0).reshape(
-        head_count, width, state_width
-    )
+    swap = [(0, 1), (1, 0)]
+    mine_lo = core * half
+    other_lo = (1 - core) * half
+
+    def heads(value, lo):
+        return lax.dynamic_slice_in_dim(value, lo, half, 0)
+
+    own_x, own_y, own_t = heads(ends, mine_lo), heads(starts, mine_lo), heads(total, mine_lo)
+    outgoing = jnp.concatenate(
+        [
+            heads(ends, other_lo).reshape(rows, state_width),
+            heads(starts, other_lo).reshape(rows, state_width),
+            pack_total(heads(total, other_lo), state_width),
+        ],
+        axis=0,
+    )
+    incoming = lax.ppermute(outgoing, "core", swap)
+    got_x = incoming[:rows].reshape(half, width, state_width)
+    got_y = incoming[rows:2 * rows].reshape(half, width, state_width)
+    got_t = incoming[2 * rows:2 * rows + half, 0]
+    is_first = core == 0
+    x_first, x_second = pick(is_first, own_x, got_x), pick(is_first, got_x, own_x)
+    y_first, y_second = pick(is_first, own_y, got_y), pick(is_first, got_y, own_y)
+    t_first, t_second = pick(is_first, own_t, got_t), pick(is_first, got_t, own_t)
+    chip_x = join(x_first, x_second, t_second)
+    chip_y = join(y_second, y_first, t_first)
+    chip_t = t_first + t_second
+    gathered = lax.all_gather(
+        jnp.concatenate(
+            [
+                chip_x.reshape(rows, state_width),
+                chip_y.reshape(rows, state_width),
+                pack_total(chip_t, state_width),
+            ],
+            axis=0,
+        ),
+        "z",
+    )
+    all_x = gathered[:, :rows].reshape(chips, half, width, state_width)
+    all_y = gathered[:, rows:2 * rows].reshape(chips, half, width, state_width)
+    all_t = gathered[:, 2 * rows:2 * rows + half, 0]
+    src = jnp.arange(chips, dtype=jnp.int32)
+    between_fwd = (src[:, None] < src[None, :]) & (src[None, :] < chip)
+    between_bwd = (chip < src[None, :]) & (src[None, :] < src[:, None])
+    sum_fwd = jnp.sum(jnp.where(between_fwd[:, :, None], all_t[None, :, :], 0.0), axis=1)
+    sum_bwd = jnp.sum(jnp.where(between_bwd[:, :, None], all_t[None, :, :], 0.0), axis=1)
+    w_fwd = jnp.where((src < chip)[:, None], jnp.exp(sum_fwd), 0.0)
+    w_bwd = jnp.where((src > chip)[:, None], jnp.exp(sum_bwd), 0.0)
+    pre_x = jnp.einsum("ch,chpn->hpn", w_fwd, all_x, precision=highest)
+    pre_y = jnp.einsum("ch,chpn->hpn", w_bwd, all_y, precision=highest)
+    joined_x = join(pre_x, x_first, t_first)
+    joined_y = join(pre_y, y_second, t_second)
+    keep_x, send_x = pick(is_first, pre_x, joined_x), pick(is_first, joined_x, pre_x)
+    keep_y, send_y = pick(is_first, joined_y, pre_y), pick(is_first, pre_y, joined_y)
+    back = lax.ppermute(
+        jnp.concatenate([send_x.reshape(rows, state_width), send_y.reshape(rows, state_width)]),
+        "core",
+        swap,
+    )
+    recv_x = back[:rows].reshape(half, width, state_width)
+    recv_y = back[rows:].reshape(half, width, state_width)
+    state_in = jnp.concatenate([pick(is_first, keep_x, recv_x), pick(is_first, recv_x, keep_x)])
+    state_grad = jnp.concatenate([pick(is_first, keep_y, recv_y), pick(is_first, recv_y, keep_y)])
+    return state_in, state_grad
 
 
 def per_device(
@@ -162,11 +188,10 @@
     weighted_grad = out_grad * from_start
     ends = jnp.einsum("tk,tn->kn", weighted_in, input_proj, precision=highest)
     starts = jnp.einsum("tk,tn->kn", weighted_grad, output_mapping, precision=highest)
-    state_in = chip_scan(
-        ends.reshape(head_count, head_width, state_width), group_total, False
-    )
-    state_grad = chip_scan(
-        starts.reshape(head_count, head_width, state_width), group_total, True
+    state_in, state_grad = chip_scans(
+        ends.reshape(head_count, head_width, state_width),
+        starts.reshape(head_count, head_width, state_width),
+        group_total,
     )
 
     scores_t = jnp.einsum("sn,tn->st", input_proj, output_mapping, precision=highest)
@@ -189,18 +214,23 @@
 
 
 def solution(mesh):
+    seq_count, head_parts = mesh.devices.shape
+    split = jax.sharding.Mesh(
+        mesh.devices.reshape(seq_count // 2, 2, head_parts), ("z", "core", "head")
+    )
+    seq = ("z", "core")
     return jax.shard_map(
         per_device,
-        mesh=mesh,
+        mesh=split,
         in_specs=(
-            P("seq", "head"),
-            P("seq", None),
-            P("seq", None),
-            P("head", "seq"),
-            P("seq"),
+            P(seq, "head"),
+            P(seq, None),
+            P(seq, None),
+            P("head", seq),
+            P(seq),
             P("head"),
-            P("seq", "head"),
+            P(seq, "head"),
         ),
-        out_specs=(P("seq", "head"), P(("seq", "head"), None), P(("seq", "head"), None)),
+        out_specs=(P(seq, "head"), P(("z", "core", "head"), None), P(("z", "core", "head"), None)),
         check_vma=False,
     )

time: 175 us -> 165 us (0.943)
  the two profiles are of different devices: /device:TPU:384 before, /device:TPU:1 now
where the time goes in v2:
time: 165 us; the launch traced here: 164 us
  waiting for transfers between devices  50.8 us (31%)
  starting transfers between devices  27 us (16%)
  matrix products  21.1 us (13%)
  local copies, waits for them, and re-layouts  18.9 us (11%)
  Pallas kernels  17.8 us (11%)
  between operations  14.5 us (9%)
  other arithmetic  14.4 us (9%)
    all_gather x1, waiting for transfers between devices, chip_scans(): lax.all_gather(jnp.concatenate([chip_x.reshape(rows, state_width), chip_y...  41.6 us
    pallas_call x1, Pallas kernels, block_terms(): pl.pallas_call(block_kernel, grid=(head_count // HEADS_PER_STEP,), in_spe...  17.8 us
    ppermute x1, starting transfers between devices, chip_scans(): lax.ppermute(jnp.concatenate([send_x.reshape(rows, state_width), send_y.r...  11.5 us
    ppermute x1, starting transfers between devices, chip_scans(): incoming = lax.ppermute(outgoing, 'core', swap)  8.96 us
    all_to_all x1, waiting for transfers between devices, per_device(): spread = lax.all_to_all(both, 'head', 0, 0, tiled=True)  7.8 us
    all_to_all x1, starting transfers between devices, per_device(): spread = lax.all_to_all(both, 'head', 0, 0, tiled=True)  6.52 us
    slice x1, local copies, waits for them, and re-layouts, chip_scans(): all_x = gathered[:, :rows].reshape(chips, half, width, state_width)  4.67 us
    dot_general x1, matrix products, chip_scans(): pre_x = jnp.einsum('ch,chpn->hpn', w_fwd, all_x, precision=highest)  3.82 us
  transfers between devices with their start and end apart: 4, of which 4 were waited for; matrix products, arithmetic and copies ran while one was open for 8% of the time, Pallas kernels for 11%

profile of v2, /device:TPU:1, one launch (start us, length us, event | category | flops | bytes accessed | tf_op | source)
XLA Modules:
  0.0 164.4 jit_solution(9952946931024842604)
XLA Ops:
  7.2 0.7 multiply_bitcast_fusion
  8.0 0.7 neg.4
  8.6 0.8 select_reduce_fusion
  9.5 1.1 reduce-window.6
  10.6 0.2 slice_reduce_fusion
  10.9 0.2 fusion.22
  11.3 0.3 copy.49
  11.7 1.1 broadcast_in_dim.116
  12.8 1.6 copy.43
  14.4 1.3 copy.46
  15.8 2.6 %fusion.17 = (f32[512,512]{1,0:T(8,128)S(1)}, f32[512,512]{1,0:T(8,128)}) fusion(f32[512,512]{1,0:T(8,128)S(1)} %copy.49, f32[512,512]{1,0:T(8,128)} %param.7, f32[512,512]{1,0:T(8,128)S(1)} %copy.43), kind=kLoop, calls=%fused_computation.64 | loop fusion | flops 524288 | bytes 5242880 | tf_op jit(solution)/shard_map/mul | solution.py:187
  18.4 1.8 %fusion.24 = f32[512,128]{1,0:T(8,128)S(1)} fusion(f32[512,512]{1,0:T(8,128)S(1)} %get-tuple-element.16, f32[512,128]{1,0:T(8,128)S(1)} %copy-done), kind=kOutput, calls=%fused_computation.71 | convolution fusion | flops 402653184 | bytes 1572864 | tf_op jit(solution)/shard_map/tk,tn->kn/dot_general | solution.py:189
  20.3 1.0 fusion.25
  21.4 0.6 copy-done.11
  22.0 0.8 maximum_maximum_fusion
  22.9 9.0 %collective-permute-start = (f32[520,128]{1,0:T(8,128)}, f32[520,128]{1,0:T(8,128)}, u32[]{:S(2)}, u32[]{:S(2)}) collective-permute-start(f32[520,128]{1,0:T(8,128)} %maximum_maximum_fusion), channel_id=1, source_target_pairs={{0,16},{16,0},{1,17},{17,1},{2,18},{18,2},{3,19},{19,3},{4,20},{20... | collective-permute-start | bytes 798728 | tf_op jit(solution)/shard_map/ppermute | solution.py:120
  31.8 1.3 collective-permute-done
  33.1 0.8 add_reduce_fusion
  34.0 1.0 fusion.19
  35.0 1.0 select_add_fusion.1
  36.1 1.0 select_add_fusion
  37.1 0.8 maximum_maximum_fusion.1
  37.9 0.6 copy.42
  38.6 2.0 %copy.44.cum_col_ref = f32[8,512,1]{2,1,0:T(8,128)} copy(f32[8,512,1]{1,0,2:T(8,128)S(1)} %bitcast.114) | data formatting | bytes 32768 | tf_op jit(solution)/shard_map/reduce_window_sum
  40.5 2.9 %fusion.23.scores_t_ref = f32[512,512]{1,0:T(8,128)} fusion(f32[512,128]{1,0:T(8,128)S(1)} %copy-done, f32[512,128]{1,0:T(8,128)} %param.9), kind=kOutput, calls=%fused_computation.70 | convolution fusion | flops 402653184 | bytes 1572864 | tf_op jit(solution)/shard_map/sn,tn->st/dot_general | solution.py:197
  43.5 17.8 %shard_map.94 = (f32[512,512]{1,0:T(8,128)}, f32[512,512]{1,0:T(8,128)}) custom-call(f32[8,1,512]{2,1,0:T(1,128)} %bitcast.116, f32[8,512,1]{2,1,0:T(8,128)} %copy.44.cum_col_ref, f32[512,512]{1,0:T(8,128)} %fusion.23.scores_t_ref, f32[512,512]{1,0:T(8,128)} %get-tuple-element.17.in_ref, f32[512,512]{1,0:T(8,128)} %grad_ref.1), custom_call_target="tpu_custom_call" | custom-call | tf_op jit(solution)/shard_map/pallas_call | solution.py:60
  61.3 0.5 iota_compare_fusion.6
  61.8 0.5 copy-done.21
  62.3 3.2 %fusion.26 = f32[512,128]{0,1:T(8,128)} fusion(f32[512,512]{1,0:T(8,128)} %get-tuple-element.6, f32[512,128]{1,0:T(8,128)} %param.9), kind=kOutput, calls=%fused_computation.73 | convolution fusion | flops 402653184 | bytes 1572864 | tf_op jit(solution)/shard_map/dot_general | solution.py:199
  65.5 41.6 %all-gather.3.cloned.1.call-done = f32[8320,128]{1,0:T(8,128)} async-done(((f32[520,128]{1,0:T(8,128)}), f32[8320,128]{1,0:T(8,128)}) %all-gather.3.cloned.1.call-update) | async-done | bytes 4259856 | tf_op jit(solution)/shard_map/all_gather | solution.py:131
  107.1 4.7 %fusion.18 = (f32[16,256,128]{2,1,0:T(8,128)}, f32[16,256,128]{2,1,0:T(8,128)}) fusion(f32[16,520,128]{2,1,0:T(8,128)} %bitcast.77), kind=kLoop, calls=%fused_computation.65 | loop fusion | bytes 8388608 | tf_op jit(solution)/shard_map/slice | solution.py:142
  111.7 1.4 slice.57
  113.2 0.9 copy.47
  114.1 0.8 exponential_select_fusion
  114.9 3.8 %fusion = f32[4,1,64,128]{3,1,2,0:T(1,128)S(1)} fusion(f32[16,4,1,1]{0,2,3,1:T(1,128)S(1)} %bitcast.118, f32[16,4,64,128]{3,2,1,0:T(8,128)} %bitcast.76), kind=kOutput, calls=%fused_computation | convolution fusion | flops 6291456 | bytes 2228480 | tf_op jit(solution)/shard_map/ch,chpn->hpn/dot_general | solution.py:152
  118.8 1.1 fusion.8
  119.8 0.7 exponential_select_fusion.1
  120.5 2.2 %fusion.2 = f32[4,1,64,128]{3,1,2,0:T(1,128)S(1)} fusion(f32[16,4,1,1]{0,2,3,1:T(1,128)S(1)} %bitcast.117, f32[16,4,64,128]{3,2,1,0:T(8,128)S(1)} %bitcast.75), kind=kOutput, calls=%fused_computation.2 | convolution fusion | flops 6291456 | bytes 2228480 | tf_op jit(solution)/shard_map/ch,chpn->hpn/dot_general | solution.py:153
  122.9 11.5 %collective-permute-start.1 = (f32[512,128]{1,0:T(8,128)S(1)}, f32[512,128]{1,0:T(8,128)S(1)}, u32[]{:S(2)}, u32[]{:S(2)}) collective-permute-start(f32[512,128]{1,0:T(8,128)S(1)} %pad_maximum_fusion.1), channel_id=1, source_target_pairs={{0,16},{16,0},{1,17},{17,1},{2,18},{18,2},{3,19},{19,3},{4,20},{20... | collective-permute-start | bytes 786440 | tf_op jit(solution)/shard_map/ppermute | solution.py:158
  134.4 0.8 fusion.27
  135.6 0.5 copy-done.16
  136.1 1.2 convolution_add_fusion.1
  137.4 0.8 convolution_add_fusion
  138.3 1.0 copy.51
  139.3 6.5 %all-to-all-start = ((f32[16,32,256]{2,1,0:T(8,128)}), f32[16,32,256]{2,1,0:T(8,128)S(1)}, u32[]{:S(2)}, u32[]{:S(2)}) async-start(f32[16,32,256]{2,1,0:T(8,128)} %bitcast.91), calls=%async_computation | async-start | bytes 1048576 | tf_op jit(solution)/shard_map/all_to_all | solution.py:211
  145.9 3.3 %fusion.6 = f32[512,512]{1,0:T(8,128)} fusion(f32[512,512]{1,0:T(8,128)S(1)} %copy-done.2, f32[512,512]{1,0:T(8,128)} %get-tuple-element.5, f32[512,512]{1,0:T(8,128)S(1)} %copy.49, f32[512,128]{1,0:T(8,128)S(1)} %bitcast.82, f32[512,128]{1,0:T(8,128)S(1)} %copy-done), kind=kOutput, calls=%fused_computation.7 | convolution fusion | flops 403439616 | bytes 4718592 | tf_op jit(solution)/shard_map/tn,kn->tk/dot_general | solution.py:206
  149.1 7.8 %all-to-all-done = f32[16,32,256]{2,1,0:T(8,128)S(1)} async-done(((f32[16,32,256]{2,1,0:T(8,128)}), f32[16,32,256]{2,1,0:T(8,128)S(1)}, u32[]{:S(2)}, u32[]{:S(2)}) %all-to-all-start) | async-done | bytes 524320 | tf_op jit(solution)/shard_map/all_to_all | solution.py:211
  156.9 0.6 fusion.21
  (71 shorter events, 1.5 us)
Async XLA Ops:
  7.2 11.2 %copy-start = (f32[512,128]{1,0:T(8,128)S(1)}, f32[512,128]{1,0:T(8,128)}, u32[]{:S(2)}) copy-start(f32[512,128]{1,0:T(8,128)} %param.8) | copy-start | bytes 786436
  7.2 99.9 %all-gather.3.cloned.1.call-start = ((), (), s32[]{:S(2)}) async-start(), calls=%async_computation.1 | async-start | bytes 4526080 | tf_op jit(solution)/shard_map/all_gather | solution.py:131
  11.7 2.7 %copy-start.4 = (f32[512,512]{1,0:T(8,128)S(1)}, f32[512,512]{1,0:T(8,128)}, u32[]{:S(2)}) copy-start(f32[512,512]{1,0:T(8,128)} %grad_ref.1) | copy-start | bytes 3145732
  14.3 4.0 %copy-start.1 = (f32[512,512]{1,0:T(8,128)}, f32[512,512]{1,0:T(8,128)S(1)}, u32[]{:S(2)}) copy-start(f32[512,512]{1,0:T(8,128)S(1)} %copy.43) | copy-start | bytes 3145732
  18.4 1.8 %copy-start.6 = (f32[512,512]{0,1:T(8,128)S(1)}, f32[512,512]{0,1:T(8,128)}, u32[]{:S(2)}) copy-start(f32[512,512]{0,1:T(8,128)} %copy.46) | copy-start | bytes 3145732
  18.4 1.9 %copy-start.13 = (f32[512,128]{1,0:T(8,128)S(1)}, f32[512,128]{1,0:T(8,128)}, u32[]{:S(2)}) copy-start(f32[512,128]{1,0:T(8,128)} %param.9) | copy-start | bytes 786436
  20.2 1.2 copy-start.9
  21.3 0.7 copy-start.11
  22.9 10.3 %collective-permute-start = (f32[520,128]{1,0:T(8,128)}, f32[520,128]{1,0:T(8,128)}, u32[]{:S(2)}, u32[]{:S(2)}) collective-permute-start(f32[520,128]{1,0:T(8,128)} %maximum_maximum_fusion), channel_id=1, source_target_pairs={{0,16},{16,0},{1,17},{17,1},{2,18},{18,2},{3,19},{19,3},{4,20},{20... | collective-permute-start | bytes 798728 | tf_op jit(solution)/shard_map/ppermute | solution.py:120
  34.0 2.1 %copy-start.19 = (f32[4]{0:T(128)}, f32[4]{0:T(128)S(1)}, u32[]{:S(2)}) copy-start(f32[4]{0:T(128)S(1)} %get-tuple-element.9) | copy-start | bytes 52
  34.0 3.1 %copy-start.17 = (f32[4]{0:T(128)}, f32[4]{0:T(128)S(1)}, u32[]{:S(2)}) copy-start(f32[4]{0:T(128)S(1)} %get-tuple-element.8) | copy-start | bytes 52
  35.0 1.1 copy-start.14
  61.8 0.5 copy-start.21
  111.7 7.0 %copy-start.18 = (f32[4]{0:T(128)S(1)}, f32[4]{0:T(128)}, u32[]{:S(2)}) copy-start(f32[4]{0:T(128)} %copy-done.17) | copy-start | bytes 52
  114.0 6.5 %copy-start.3 = (f32[16,256,128]{2,1,0:T(8,128)S(1)}, f32[16,256,128]{2,1,0:T(8,128)}, u32[]{:S(2)}) copy-start(f32[16,256,128]{2,1,0:T(8,128)} %get-tuple-element.21) | copy-start | bytes 6291460
  114.9 7.9 %copy-start.12 = (f32[512,128]{1,0:T(8,128)S(1)}, f32[512,128]{1,0:T(8,128)}, u32[]{:S(2)}) copy-start(f32[512,128]{1,0:T(8,128)} %copy-done.11) | copy-start | bytes 786436
  114.9 7.9 %copy-start.15 = (f32[256,128]{1,0:T(8,128)S(1)}, f32[256,128]{1,0:T(8,128)}, u32[]{:S(2)}) copy-start(f32[256,128]{1,0:T(8,128)} %copy-done.14) | copy-start | bytes 393220
  114.9 7.9 %copy-start.20 = (f32[4]{0:T(128)S(1)}, f32[4]{0:T(128)}, u32[]{:S(2)}) copy-start(f32[4]{0:T(128)} %copy-done.19) | copy-start | bytes 52
  118.7 15.6 %copy-start.5 = (f32[512,512]{1,0:T(8,128)S(1)}, f32[512,512]{1,0:T(8,128)}, u32[]{:S(2)}) copy-start(f32[512,512]{1,0:T(8,128)} %get-tuple-element.6) | copy-start | bytes 3145732
  122.8 12.7 %copy-start.10 = (f32[512,128]{1,0:T(8,128)S(1)}, f32[512,128]{1,0:T(8,128)}, u32[]{:S(2)}) copy-start(f32[512,128]{1,0:T(8,128)} %copy-done.9) | copy-start | bytes 786436
  122.9 12.4 %collective-permute-start.1 = (f32[512,128]{1,0:T(8,128)S(1)}, f32[512,128]{1,0:T(8,128)S(1)}, u32[]{:S(2)}, u32[]{:S(2)}) collective-permute-start(f32[512,128]{1,0:T(8,128)S(1)} %pad_maximum_fusion.1), channel_id=1, source_target_pairs={{0,16},{16,0},{1,17},{17,1},{2,18},{18,2},{3,19},{19,3},{4,20},{20... | collective-permute-start | bytes 786440 | tf_op jit(solution)/shard_map/ppermute | solution.py:158
  135.2 1.0 copy-start.16
  135.6 2.7 %copy-start.7 = (f32[8,64,128]{2,1,0:T(8,128)}, f32[8,64,128]{2,1,0:T(8,128)S(1)}, u32[]{:S(2)}) copy-start(f32[8,64,128]{2,1,0:T(8,128)S(1)} %pad_maximum_fusion.2) | copy-start | bytes 786436
  137.4 8.4 %copy-start.2 = (f32[512,512]{1,0:T(8,128)S(1)}, f32[512,512]{1,0:T(8,128)}, u32[]{:S(2)}) copy-start(f32[512,512]{1,0:T(8,128)} %copy-done.1) | copy-start | bytes 3145732
  138.3 7.5 %copy-start.8 = (f32[8,64,128]{2,1,0:T(8,128)S(1)}, f32[8,64,128]{2,1,0:T(8,128)}, u32[]{:S(2)}) copy-start(f32[8,64,128]{2,1,0:T(8,128)} %copy-done.7) | copy-start | bytes 786436
  139.3 17.6 %all-to-all-start = ((f32[16,32,256]{2,1,0:T(8,128)}), f32[16,32,256]{2,1,0:T(8,128)S(1)}, u32[]{:S(2)}, u32[]{:S(2)}) async-start(f32[16,32,256]{2,1,0:T(8,128)} %bitcast.91), calls=%async_computation | async-start | bytes 1048576 | tf_op jit(solution)/shard_map/all_to_all | solution.py:211
Sparse Core Ops, SparseCore 0:
  38.1 68.9 all-gather.2

commit v3 on v2

--- a/solution.py
+++ b/solution.py
@@ -139,8 +139,6 @@
         ),
         "z",
     )
-    all_x = gathered[:, :rows].reshape(chips, half, width, state_width)
-    all_y = gathered[:, rows:2 * rows].reshape(chips, half, width, state_width)
     all_t = gathered[:, 2 * rows:2 * rows + half, 0]
     src = jnp.arange(chips, dtype=jnp.int32)
     between_fwd = (src[:, None] < src[None, :]) & (src[None, :] < chip)
@@ -149,8 +147,17 @@
     sum_bwd = jnp.sum(jnp.where(between_bwd[:, :, None], all_t[None, :, :], 0.0), axis=1)
     w_fwd = jnp.where((src < chip)[:, None], jnp.exp(sum_fwd), 0.0)
     w_bwd = jnp.where((src > chip)[:, None], jnp.exp(sum_bwd), 0.0)
-    pre_x = jnp.einsum("ch,chpn->hpn", w_fwd, all_x, precision=highest)
-    pre_y = jnp.einsum("ch,chpn->hpn", w_bwd, all_y, precision=highest)
+    row_weights = jnp.concatenate(
+        [
+            jnp.repeat(w_fwd, width, axis=1),
+            jnp.repeat(w_bwd, width, axis=1),
+            jnp.zeros((chips, gathered.shape[1] - 2 * rows), jnp.float32),
+        ],
+        axis=1,
+    )
+    summed = jnp.sum(row_weights[:, :, None] * gathered, axis=0)
+    pre_x = summed[:rows].reshape(half, width, state_width)
+    pre_y = summed[rows:2 * rows].reshape(half, width, state_width)
     joined_x = join(pre_x, x_first, t_first)
     joined_y = join(pre_y, y_second, t_second)
     keep_x, send_x = pick(is_first, pre_x, joined_x), pick(is_first, joined_x, pre_x)

time: 165 us -> 159 us (0.964)
  matrix products: 21.1 us -> 16.4 us
  local copies, waits for them, and re-layouts: 18.9 us -> 16.8 us
    dot_general x2 -> x0, matrix products: 6.06 us -> none  [the longest x1 3.82 us: chip_scans(): pre_x = jnp.einsum('ch,chpn->hpn', w_fwd, all_x, precision=highest)]
    slice x2, local copies, waits for them, and re-layouts: 4.83 us -> 0.18 us  [the longest x1 4.67 us: chip_scans(): all_x = gathered[:, :rows].reshape(chips, half, width, state_width)]
    reduce_sum x0 -> x1, other arithmetic: none -> 2.88 us  [chip_scans(): summed = jnp.sum(row_weights[:, :, None] * gathered, axis=0)]
    reshape x0 -> x2, local copies, waits for them, and re-layouts: none -> 2.29 us  [the longest x1 1.45 us: chip_scans(): jnp.repeat(w_bwd, width, axis=1)]
    broadcast_in_dim x0 -> x3, local copies, waits for them, and re-layouts: none -> 2.08 us  [the longest x1 1.39 us: chip_scans(): jnp.repeat(w_bwd, width, axis=1)]
    unnamed x45 -> x37, local copies, waits for them, and re-layouts: 3.08 us -> 1.11 us
    dot_general x1, matrix products: 3.17 us -> 1.23 us  [per_device(): block_b = jnp.dot(grad_scores_t, output_mapping, precision=highest)]
    dot_general x1, matrix products: 0.79 us -> 2.71 us  [per_device(): jnp.einsum('st,sn->tn', grad_scores_t, input_proj, precision=highest)]
  transfers between devices with their start and end apart: 4 -> 4, of which waited for: 4 -> 3; matrix products, arithmetic and copies ran while one was open for 8% -> 9% of each run, Pallas kernels for 11% -> 11%
where the time goes in v3:
time: 159 us; the launch traced here: 158 us
  waiting for transfers between devices  50.5 us (32%)
  starting transfers between devices  26.8 us (17%)
  Pallas kernels  17.8 us (11%)
  local copies, waits for them, and re-layouts  16.8 us (11%)
  matrix products  16.4 us (10%)
  other arithmetic  15.3 us (10%)
  between operations  14.5 us (9%)
    all_gather x1, waiting for transfers between devices, chip_scans(): lax.all_gather(jnp.concatenate([chip_x.reshape(rows, state_width), chip_y...  42 us
    pallas_call x1, Pallas kernels, block_terms(): pl.pallas_call(block_kernel, grid=(head_count // HEADS_PER_STEP,), in_spe...  17.8 us
    ppermute x1, starting transfers between devices, chip_scans(): lax.ppermute(jnp.concatenate([send_x.reshape(rows, state_width), send_y.r...  11.2 us
    ppermute x1, starting transfers between devices, chip_scans(): incoming = lax.ppermute(outgoing, 'core', swap)  8.95 us
    all_to_all x1, waiting for transfers between devices, per_device(): spread = lax.all_to_all(both, 'head', 0, 0, tiled=True)  7.18 us
    all_to_all x1, starting transfers between devices, per_device(): spread = lax.all_to_all(both, 'head', 0, 0, tiled=True)  6.59 us
    dot_general x1, matrix products, per_device(): jnp.einsum('tn,kn->tk', input_proj, flat_grad, precision=highest)  3.66 us
  transfers between devices with their start and end apart: 4, of which 3 were waited for; matrix products, arithmetic and copies ran while one was open for 9% of the time, Pallas kernels for 11%

profile of v3, /device:TPU:1, one launch (start us, length us, event | category | flops | bytes accessed | tf_op | source)
XLA Modules:
  0.0 158.0 jit_solution(18158395003759362510)
XLA Ops:
  7.3 0.7 neg.4
  8.0 0.7 multiply_bitcast_fusion
  8.7 0.8 select_reduce_fusion
  9.6 1.1 reduce-window.6
  10.7 0.2 slice_reduce_fusion
  11.0 0.2 fusion.18
  11.5 0.3 copy.51
  12.0 1.3 copy.43
  13.3 0.3 copy.46
  13.8 2.1 %fusion.21 = f32[512,128]{1,0:T(8,128)S(1)} fusion(f32[512,512]{0,1:T(8,128)S(1)} %bitcast_multiply_fusion, f32[512,128]{1,0:T(8,128)} %param.9), kind=kOutput, calls=%fused_computation.70 | convolution fusion | flops 402653184 | bytes 1572864 | tf_op jit(solution)/shard_map/tk,tn->kn/dot_general | solution.py:197
  15.9 1.4 fusion.13
  17.3 1.8 %fusion.20 = f32[512,128]{1,0:T(8,128)S(1)} fusion(f32[512,512]{1,0:T(8,128)S(1)} %get-tuple-element.16, f32[512,128]{1,0:T(8,128)S(1)} %copy-done), kind=kOutput, calls=%fused_computation.69 | convolution fusion | flops 402653184 | bytes 1572864 | tf_op jit(solution)/shard_map/tk,tn->kn/dot_general | solution.py:196
  19.1 0.7 copy-done.5
  19.8 0.8 maximum_maximum_fusion
  20.6 9.0 %collective-permute-start = (f32[520,128]{1,0:T(8,128)}, f32[520,128]{1,0:T(8,128)}, u32[]{:S(2)}, u32[]{:S(2)}) collective-permute-start(f32[520,128]{1,0:T(8,128)} %maximum_maximum_fusion), channel_id=1, source_target_pairs={{0,16},{16,0},{1,17},{17,1},{2,18},{18,2},{3,19},{19,3},{4,20},{20... | collective-permute-start | bytes 798728 | tf_op jit(solution)/shard_map/ppermute | solution.py:120
  29.6 1.3 collective-permute-done
  30.9 0.8 add_reduce_fusion
  31.8 1.0 fusion.15
  32.8 1.0 select_add_fusion
  33.8 1.0 select_add_fusion.1
  34.8 0.8 maximum_maximum_fusion.1
  35.7 0.6 copy.42
  36.3 2.0 %copy.44.cum_col_ref = f32[8,512,1]{2,1,0:T(8,128)} copy(f32[8,512,1]{1,0,2:T(8,128)S(1)} %bitcast.99) | data formatting | bytes 32768 | tf_op jit(solution)/shard_map/reduce_window_sum
  38.3 0.6 pad.12.clone
  38.9 2.9 %fusion.19.scores_t_ref = f32[512,512]{1,0:T(8,128)} fusion(f32[512,128]{1,0:T(8,128)S(1)} %copy-done, f32[512,128]{1,0:T(8,128)} %param.9), kind=kOutput, calls=%fused_computation.68 | convolution fusion | flops 402653184 | bytes 1572864 | tf_op jit(solution)/shard_map/sn,tn->st/dot_general | solution.py:204
  41.8 17.8 %shard_map.94 = (f32[512,512]{1,0:T(8,128)}, f32[512,512]{1,0:T(8,128)}) custom-call(f32[8,1,512]{2,1,0:T(1,128)} %bitcast.101, f32[8,512,1]{2,1,0:T(8,128)} %copy.44.cum_col_ref, f32[512,512]{1,0:T(8,128)} %fusion.19.scores_t_ref, f32[512,512]{1,0:T(8,128)} %get-tuple-element.17.in_ref, f32[512,512]{1,0:T(8,128)} %grad_ref.1), custom_call_target="tpu_custom_call" | custom-call | tf_op jit(solution)/shard_map/pallas_call | solution.py:60
  59.6 0.5 iota_compare_fusion.4
  60.1 2.7 %fusion.23 = f32[512,128]{0,1:T(8,128)} fusion(f32[512,512]{1,0:T(8,128)} %get-tuple-element.6, f32[512,128]{1,0:T(8,128)S(1)} %copy-done), kind=kOutput, calls=%fused_computation.72 | convolution fusion | flops 402653184 | bytes 1572864 | tf_op jit(solution)/shard_map/st,sn->tn/dot_general | solution.py:207
  62.9 42.0 %all-gather.3.cloned.1.call-done = f32[8320,128]{1,0:T(8,128)} async-done(((f32[520,128]{1,0:T(8,128)}), f32[8320,128]{1,0:T(8,128)}) %all-gather.3.cloned.1.call-update) | async-done | bytes 4259856 | tf_op jit(solution)/shard_map/all_gather | solution.py:131
  104.8 1.5 slice.57
  106.3 0.9 copy.47
  107.2 0.7 exponential_select_fusion
  107.9 0.7 copy.49
  108.7 0.7 broadcast_in_dim.137
  109.4 0.8 reshape.263
  110.2 1.4 broadcast_in_dim.140
  111.6 1.4 reshape.264
  113.1 0.9 maximum_maximum_fusion.2
  114.0 2.9 %multiply_reduce_fusion = f32[520,128]{1,0:T(8,128)S(1)} fusion(f32[16,520,128]{2,1,0:T(8,128)} %bitcast.64, f32[16,520]{1,0:T(8,128)S(1)} %maximum_maximum_fusion.2), kind=kLoop, calls=%fused_computation | loop fusion | flops 2063360 | bytes 4559360 | tf_op jit(solution)/shard_map/reduce_sum | solution.py:158
  117.2 11.2 %collective-permute-start.1 = (f32[512,128]{1,0:T(8,128)S(1)}, f32[512,128]{1,0:T(8,128)S(1)}, u32[]{:S(2)}, u32[]{:S(2)}) collective-permute-start(f32[512,128]{1,0:T(8,128)S(1)} %pad_maximum_fusion.1), channel_id=1, source_target_pairs={{0,16},{16,0},{1,17},{17,1},{2,18},{18,2},{3,19},{19,3},{4,20},{20... | collective-permute-start | bytes 786440 | tf_op jit(solution)/shard_map/ppermute | solution.py:165
  128.4 1.2 fusion.22
  130.0 1.2 convolution_add_fusion.1
  131.2 0.8 convolution_add_fusion
  132.1 1.0 copy.53
  133.1 6.6 %all-to-all-start = ((f32[16,32,256]{2,1,0:T(8,128)}), f32[16,32,256]{2,1,0:T(8,128)S(1)}, u32[]{:S(2)}, u32[]{:S(2)}) async-start(f32[16,32,256]{2,1,0:T(8,128)} %bitcast.30), calls=%async_computation | async-start | bytes 1048576 | tf_op jit(solution)/shard_map/all_to_all | solution.py:218
  139.7 3.7 %fusion.2 = f32[512,512]{1,0:T(8,128)} fusion(f32[512,512]{1,0:T(8,128)} %copy.43, f32[512,512]{1,0:T(8,128)} %get-tuple-element.5, f32[512,512]{1,0:T(8,128)S(1)} %copy.51, f32[512,128]{1,0:T(8,128)} %bitcast.68, f32[512,128]{1,0:T(8,128)S(1)} %copy-done), kind=kOutput, calls=%fused_computation.4 | convolution fusion | flops 403439616 | bytes 4718592 | tf_op jit(solution)/shard_map/tn,kn->tk/dot_general | solution.py:213
  143.3 7.2 %all-to-all-done = f32[16,32,256]{2,1,0:T(8,128)S(1)} async-done(((f32[16,32,256]{2,1,0:T(8,128)}), f32[16,32,256]{2,1,0:T(8,128)S(1)}, u32[]{:S(2)}, u32[]{:S(2)}) %all-to-all-start) | async-done | bytes 524320 | tf_op jit(solution)/shard_map/all_to_all | solution.py:218
  150.6 0.6 fusion.17
  (71 shorter events, 1.7 us)
Async XLA Ops:
  7.2 10.1 %copy-start = (f32[512,128]{1,0:T(8,128)S(1)}, f32[512,128]{1,0:T(8,128)}, u32[]{:S(2)}) copy-start(f32[512,128]{1,0:T(8,128)} %param.8) | copy-start | bytes 786436
  7.2 6.1 %copy-start.2 = (f32[512,512]{1,0:T(8,128)S(1)}, f32[512,512]{1,0:T(8,128)}, u32[]{:S(2)}) copy-start(f32[512,512]{1,0:T(8,128)} %grad_ref.1) | copy-start | bytes 3145732
  7.2 97.6 %all-gather.3.cloned.1.call-start = ((), (), s32[]{:S(2)}) async-start(), calls=%async_computation.1 | async-start | bytes 4526080 | tf_op jit(solution)/shard_map/all_gather | solution.py:131
  13.6 2.2 %copy-start.1 = (f32[512,512]{1,0:T(8,128)S(1)}, f32[512,512]{1,0:T(8,128)}, u32[]{:S(2)}) copy-start(f32[512,512]{1,0:T(8,128)} %copy.43) | copy-start | bytes 3145732
  13.6 2.2 %copy-start.12 = (f32[512,512]{1,0:T(8,128)S(1)}, f32[512,512]{1,0:T(8,128)}, u32[]{:S(2)}) copy-start(f32[512,512]{1,0:T(8,128)} %param.7) | copy-start | bytes 3145732
  15.9 3.9 %copy-start.7 = (f32[512,128]{1,0:T(8,128)}, f32[512,128]{1,0:T(8,128)S(1)}, u32[]{:S(2)}) copy-start(f32[512,128]{1,0:T(8,128)S(1)} %fusion.21) | copy-start | bytes 786436
  19.1 0.7 copy-start.5
  20.6 10.3 %collective-permute-start = (f32[520,128]{1,0:T(8,128)}, f32[520,128]{1,0:T(8,128)}, u32[]{:S(2)}, u32[]{:S(2)}) collective-permute-start(f32[520,128]{1,0:T(8,128)} %maximum_maximum_fusion), channel_id=1, source_target_pairs={{0,16},{16,0},{1,17},{17,1},{2,18},{18,2},{3,19},{19,3},{4,20},{20... | collective-permute-start | bytes 798728 | tf_op jit(solution)/shard_map/ppermute | solution.py:120
  31.7 2.1 %copy-start.16 = (f32[4]{0:T(128)}, f32[4]{0:T(128)S(1)}, u32[]{:S(2)}) copy-start(f32[4]{0:T(128)S(1)} %get-tuple-element.8) | copy-start | bytes 52
  31.8 3.1 %copy-start.14 = (f32[4]{0:T(128)}, f32[4]{0:T(128)S(1)}, u32[]{:S(2)}) copy-start(f32[4]{0:T(128)S(1)} %get-tuple-element.9) | copy-start | bytes 52
  32.8 1.1 copy-start.10
  113.1 3.8 %copy-start.8 = (f32[512,128]{1,0:T(8,128)S(1)}, f32[512,128]{1,0:T(8,128)}, u32[]{:S(2)}) copy-start(f32[512,128]{1,0:T(8,128)} %copy-done.7) | copy-start | bytes 786436
  113.1 3.8 %copy-start.15 = (f32[4]{0:T(128)S(1)}, f32[4]{0:T(128)}, u32[]{:S(2)}) copy-start(f32[4]{0:T(128)} %copy-done.14) | copy-start | bytes 52
  113.1 3.9 %copy-start.6 = (f32[512,128]{1,0:T(8,128)S(1)}, f32[512,128]{1,0:T(8,128)}, u32[]{:S(2)}) copy-start(f32[512,128]{1,0:T(8,128)} %copy-done.5) | copy-start | bytes 786436
  113.1 3.9 %copy-start.11 = (f32[256,128]{1,0:T(8,128)S(1)}, f32[256,128]{1,0:T(8,128)}, u32[]{:S(2)}) copy-start(f32[256,128]{1,0:T(8,128)} %copy-done.10) | copy-start | bytes 393220
  113.1 4.0 %copy-start.17 = (f32[4]{0:T(128)S(1)}, f32[4]{0:T(128)}, u32[]{:S(2)}) copy-start(f32[4]{0:T(128)} %copy-done.16) | copy-start | bytes 52
  113.1 15.3 %copy-start.3 = (f32[512,512]{1,0:T(8,128)S(1)}, f32[512,512]{1,0:T(8,128)}, u32[]{:S(2)}) copy-start(f32[512,512]{1,0:T(8,128)} %get-tuple-element.6) | copy-start | bytes 3145732
  113.1 15.3 %copy-start.9 = (f32[512,128]{1,0:T(8,128)S(1)}, f32[512,128]{1,0:T(8,128)}, u32[]{:S(2)}) copy-start(f32[512,128]{1,0:T(8,128)} %param.9) | copy-start | bytes 786436
  117.0 14.2 %copy-start.13 = (f32[512,128]{0,1:T(8,128)S(1)}, f32[512,128]{0,1:T(8,128)}, u32[]{:S(2)}) copy-start(f32[512,128]{0,1:T(8,128)} %fusion.23) | copy-start | bytes 786436
  117.2 12.5 %collective-permute-start.1 = (f32[512,128]{1,0:T(8,128)S(1)}, f32[512,128]{1,0:T(8,128)S(1)}, u32[]{:S(2)}, u32[]{:S(2)}) collective-permute-start(f32[512,128]{1,0:T(8,128)S(1)} %pad_maximum_fusion.1), channel_id=1, source_target_pairs={{0,16},{16,0},{1,17},{17,1},{2,18},{18,2},{3,19},{19,3},{4,20},{20... | collective-permute-start | bytes 786440 | tf_op jit(solution)/shard_map/ppermute | solution.py:165
  130.0 2.1 %copy-start.4 = (f32[8,64,128]{2,1,0:T(8,128)}, f32[8,64,128]{2,1,0:T(8,128)S(1)}, u32[]{:S(2)}) copy-start(f32[8,64,128]{2,1,0:T(8,128)S(1)} %pad_maximum_fusion.2) | copy-start | bytes 786436
  133.1 17.4 %all-to-all-start = ((f32[16,32,256]{2,1,0:T(8,128)}), f32[16,32,256]{2,1,0:T(8,128)S(1)}, u32[]{:S(2)}, u32[]{:S(2)}) async-start(f32[16,32,256]{2,1,0:T(8,128)} %bitcast.30), calls=%async_computation | async-start | bytes 1048576 | tf_op jit(solution)/shard_map/all_to_all | solution.py:218
Sparse Core Ops, SparseCore 0:
  35.8 68.9 all-gather.2

commit v4 on v2

--- a/solution.py
+++ b/solution.py
@@ -139,8 +139,6 @@
         ),
         "z",
     )
-    all_x = gathered[:, :rows].reshape(chips, half, width, state_width)
-    all_y = gathered[:, rows:2 * rows].reshape(chips, half, width, state_width)
     all_t = gathered[:, 2 * rows:2 * rows + half, 0]
     src = jnp.arange(chips, dtype=jnp.int32)
     between_fwd = (src[:, None] < src[None, :]) & (src[None, :] < chip)
@@ -149,8 +147,11 @@
     sum_bwd = jnp.sum(jnp.where(between_bwd[:, :, None], all_t[None, :, :], 0.0), axis=1)
     w_fwd = jnp.where((src < chip)[:, None], jnp.exp(sum_fwd), 0.0)
     w_bwd = jnp.where((src > chip)[:, None], jnp.exp(sum_bwd), 0.0)
-    pre_x = jnp.einsum("ch,chpn->hpn", w_fwd, all_x, precision=highest)
-    pre_y = jnp.einsum("ch,chpn->hpn", w_bwd, all_y, precision=highest)
+    weights = jnp.stack([w_fwd, w_bwd], axis=1)
+    blocks = gathered[:, :2 * rows].reshape(chips, 2, half, width, state_width)
+    summed = jnp.sum(weights[:, :, :, None, None] * blocks, axis=0)
+    pre_x = summed[0]
+    pre_y = summed[1]
     joined_x = join(pre_x, x_first, t_first)
     joined_y = join(pre_y, y_second, t_second)
     keep_x, send_x = pick(is_first, pre_x, joined_x), pick(is_first, joined_x, pre_x)

time: 165 us -> 157 us (0.952)
  local copies, waits for them, and re-layouts: 18.9 us -> 14.1 us
  matrix products: 21.1 us -> 16.4 us
    dot_general x2 -> x0, matrix products: 6.06 us -> none  [the longest x1 3.82 us: chip_scans(): pre_x = jnp.einsum('ch,chpn->hpn', w_fwd, all_x, precision=highest)]
    slice x2, local copies, waits for them, and re-layouts: 4.83 us -> 0.18 us  [the longest x1 4.67 us: chip_scans(): all_x = gathered[:, :rows].reshape(chips, half, width, state_width)]
    reduce_sum x0 -> x1, other arithmetic: none -> 3.01 us  [chip_scans(): summed = jnp.sum(weights[:, :, :, None, None] * blocks, axis=0)]
    mul x0 -> x2, local copies, waits for them, and re-layouts: none -> 2.29 us  [chip_scans(): summed = jnp.sum(weights[:, :, :, None, None] * blocks, axis=0)]
    unnamed x45 -> x37, local copies, waits for them, and re-layouts: 3.08 us -> 1.11 us
    dot_general x1, matrix products: 3.17 us -> 1.22 us  [per_device(): block_b = jnp.dot(grad_scores_t, output_mapping, precision=highest)]
    dot_general x1, matrix products: 0.79 us -> 2.71 us  [per_device(): jnp.einsum('st,sn->tn', grad_scores_t, input_proj, precision=highest)]
    another operation x3 -> x4, local copies, waits for them, and re-layouts: 2.59 us -> 3.36 us
  transfers between devices with their start and end apart: 4 -> 4, of which waited for: 4 -> 3; matrix products, arithmetic and copies ran while one was open for 8% -> 9% of each run, Pallas kernels for 11% -> 11%
where the time goes in v4:
time: 157 us; the launch traced here: 156 us
  waiting for transfers between devices  51.5 us (33%)
  starting transfers between devices  26.4 us (17%)
  Pallas kernels  17.8 us (11%)
  matrix products  16.4 us (10%)
  other arithmetic  15.1 us (10%)
  between operations  14.5 us (9%)
  local copies, waits for them, and re-layouts  14.1 us (9%)
    all_gather x1, waiting for transfers between devices, chip_scans(): lax.all_gather(jnp.concatenate([chip_x.reshape(rows, state_width), chip_y...  43 us
    pallas_call x1, Pallas kernels, block_terms(): pl.pallas_call(block_kernel, grid=(head_count // HEADS_PER_STEP,), in_spe...  17.8 us
    ppermute x1, starting transfers between devices, chip_scans(): lax.ppermute(jnp.concatenate([send_x.reshape(rows, state_width), send_y.r...  10.8 us
    ppermute x1, starting transfers between devices, chip_scans(): incoming = lax.ppermute(outgoing, 'core', swap)  8.95 us
    all_to_all x1, waiting for transfers between devices, per_device(): spread = lax.all_to_all(both, 'head', 0, 0, tiled=True)  7.18 us
    all_to_all x1, starting transfers between devices, per_device(): spread = lax.all_to_all(both, 'head', 0, 0, tiled=True)  6.6 us
    dot_general x1, matrix products, per_device(): jnp.einsum('tn,kn->tk', input_proj, flat_grad, precision=highest)  3.66 us
  transfers between devices with their start and end apart: 4, of which 3 were waited for; matrix products, arithmetic and copies ran while one was open for 9% of the time, Pallas kernels for 11%

profile of v4, /device:TPU:1, one launch (start us, length us, event | category | flops | bytes accessed | tf_op | source)
XLA Modules:
  0.0 155.8 jit_solution(5816437422616034327)
XLA Ops:
  7.3 0.7 neg.4
  8.0 0.7 multiply_bitcast_fusion
  8.7 0.8 select_reduce_fusion
  9.6 1.1 reduce-window.6
  10.7 0.2 slice_reduce_fusion
  11.0 0.2 fusion.19
  11.2 0.1 dynamic-slice_reduce_fusion
  11.4 0.1 broadcast_in_dim.118
  11.5 0.3 copy.52
  11.9 0.1 broadcast_in_dim.73
  12.0 1.3 copy.45
  13.3 0.3 copy.48
  13.8 2.1 %fusion.22 = f32[512,128]{1,0:T(8,128)S(1)} fusion(f32[512,512]{0,1:T(8,128)S(1)} %bitcast_multiply_fusion, f32[512,128]{1,0:T(8,128)} %param.9), kind=kOutput, calls=%fused_computation.71 | convolution fusion | flops 402653184 | bytes 1572864 | tf_op jit(solution)/shard_map/tk,tn->kn/dot_general | solution.py:191
  15.9 1.4 fusion.14
  17.3 1.8 %fusion.21 = f32[512,128]{1,0:T(8,128)S(1)} fusion(f32[512,512]{1,0:T(8,128)S(1)} %get-tuple-element.16, f32[512,128]{1,0:T(8,128)S(1)} %copy-done), kind=kOutput, calls=%fused_computation.70 | convolution fusion | flops 402653184 | bytes 1572864 | tf_op jit(solution)/shard_map/tk,tn->kn/dot_general | solution.py:190
  19.1 0.7 copy-done.5
  19.8 0.8 maximum_maximum_fusion
  20.6 9.0 %collective-permute-start = (f32[520,128]{1,0:T(8,128)}, f32[520,128]{1,0:T(8,128)}, u32[]{:S(2)}, u32[]{:S(2)}) collective-permute-start(f32[520,128]{1,0:T(8,128)} %maximum_maximum_fusion), channel_id=1, source_target_pairs={{0,16},{16,0},{1,17},{17,1},{2,18},{18,2},{3,19},{19,3},{4,20},{20... | collective-permute-start | bytes 798728 | tf_op jit(solution)/shard_map/ppermute | solution.py:120
  29.6 1.3 collective-permute-done
  30.9 0.8 add_reduce_fusion
  31.8 1.0 fusion.15
  32.8 1.0 select_add_fusion
  33.8 1.0 select_add_fusion.1
  34.8 0.8 maximum_maximum_fusion.1
  35.7 0.6 copy.44
  36.3 2.0 %copy.46.cum_col_ref = f32[8,512,1]{2,1,0:T(8,128)} copy(f32[8,512,1]{1,0,2:T(8,128)S(1)} %bitcast.103) | data formatting | bytes 32768 | tf_op jit(solution)/shard_map/reduce_window_sum
  38.3 2.9 %fusion.20.scores_t_ref = f32[512,512]{1,0:T(8,128)} fusion(f32[512,128]{1,0:T(8,128)S(1)} %copy-done, f32[512,128]{1,0:T(8,128)} %param.9), kind=kOutput, calls=%fused_computation.69 | convolution fusion | flops 402653184 | bytes 1572864 | tf_op jit(solution)/shard_map/sn,tn->st/dot_general | solution.py:198
  41.2 17.8 %shard_map.94 = (f32[512,512]{1,0:T(8,128)}, f32[512,512]{1,0:T(8,128)}) custom-call(f32[8,1,512]{2,1,0:T(1,128)} %bitcast.105, f32[8,512,1]{2,1,0:T(8,128)} %copy.46.cum_col_ref, f32[512,512]{1,0:T(8,128)} %fusion.20.scores_t_ref, f32[512,512]{1,0:T(8,128)} %get-tuple-element.17.in_ref, f32[512,512]{1,0:T(8,128)} %grad_ref.1), custom_call_target="tpu_custom_call" | custom-call | tf_op jit(solution)/shard_map/pallas_call | solution.py:60
  59.0 0.5 iota_compare_fusion.4
  59.5 2.7 %fusion.24 = f32[512,128]{0,1:T(8,128)} fusion(f32[512,512]{1,0:T(8,128)} %get-tuple-element.6, f32[512,128]{1,0:T(8,128)S(1)} %copy-done), kind=kOutput, calls=%fused_computation.73 | convolution fusion | flops 402653184 | bytes 1572864 | tf_op jit(solution)/shard_map/st,sn->tn/dot_general | solution.py:201
  62.3 43.0 %all-gather.3.cloned.1.call-done = f32[8320,128]{1,0:T(8,128)} async-done(((f32[520,128]{1,0:T(8,128)}), f32[8320,128]{1,0:T(8,128)}) %all-gather.3.cloned.1.call-update) | async-done | bytes 4259856 | tf_op jit(solution)/shard_map/all_gather | solution.py:131
  105.2 1.5 slice.63
  106.7 0.9 copy.49
  107.7 0.7 bitcast_select_fusion
  108.3 0.6 pad_maximum_fusion.4
  108.9 0.8 copy.50
  109.7 0.7 mul.99
  110.4 1.6 %mul.100 = f32[16,512]{1,0:T(8,128)} reshape(f32[16,2,4,64]{3,2,1,0:T(4,128)} %mul.99) | data formatting | bytes 65536 | tf_op jit(solution)/shard_map/mul | solution.py:152
  112.0 3.0 %fusion = f32[512,128]{1,0:T(8,128)S(1)} fusion(f32[16,520,128]{2,1,0:T(8,128)} %bitcast.68, f32[16,512]{1,0:T(8,128)} %mul.100), kind=kLoop, calls=%fused_computation.1 | loop fusion | flops 2031616 | bytes 4489216 | tf_op jit(solution)/shard_map/reduce_sum | solution.py:152
  115.4 10.8 %collective-permute-start.1 = (f32[512,128]{1,0:T(8,128)S(1)}, f32[512,128]{1,0:T(8,128)S(1)}, u32[]{:S(2)}, u32[]{:S(2)}) collective-permute-start(f32[512,128]{1,0:T(8,128)S(1)} %pad_maximum_fusion.1), channel_id=1, source_target_pairs={{0,16},{16,0},{1,17},{17,1},{2,18},{18,2},{3,19},{19,3},{4,20},{20... | collective-permute-start | bytes 786440 | tf_op jit(solution)/shard_map/ppermute | solution.py:159
  126.2 1.2 fusion.23
  127.7 1.2 convolution_add_fusion.1
  129.0 0.8 convolution_add_fusion
  129.9 1.0 copy.54
  130.9 6.6 %all-to-all-start = ((f32[16,32,256]{2,1,0:T(8,128)}), f32[16,32,256]{2,1,0:T(8,128)S(1)}, u32[]{:S(2)}, u32[]{:S(2)}) async-start(f32[16,32,256]{2,1,0:T(8,128)} %bitcast.32), calls=%async_computation | async-start | bytes 1048576 | tf_op jit(solution)/shard_map/all_to_all | solution.py:212
  137.5 3.7 %fusion.3 = f32[512,512]{1,0:T(8,128)} fusion(f32[512,512]{1,0:T(8,128)} %copy.45, f32[512,512]{1,0:T(8,128)} %get-tuple-element.5, f32[512,512]{1,0:T(8,128)S(1)} %copy.52, f32[512,128]{1,0:T(8,128)} %bitcast.72, f32[512,128]{1,0:T(8,128)S(1)} %copy-done), kind=kOutput, calls=%fused_computation.5 | convolution fusion | flops 403439616 | bytes 4718592 | tf_op jit(solution)/shard_map/tn,kn->tk/dot_general | solution.py:207
  141.1 7.2 %all-to-all-done = f32[16,32,256]{2,1,0:T(8,128)S(1)} async-done(((f32[16,32,256]{2,1,0:T(8,128)}), f32[16,32,256]{2,1,0:T(8,128)S(1)}, u32[]{:S(2)}, u32[]{:S(2)}) %all-to-all-start) | async-done | bytes 524320 | tf_op jit(solution)/shard_map/all_to_all | solution.py:212
  148.3 0.6 fusion.18
  (66 shorter events, 1.3 us)
Async XLA Ops:
  7.2 10.1 %copy-start = (f32[512,128]{1,0:T(8,128)S(1)}, f32[512,128]{1,0:T(8,128)}, u32[]{:S(2)}) copy-start(f32[512,128]{1,0:T(8,128)} %param.8) | copy-start | bytes 786436
  7.2 6.1 %copy-start.2 = (f32[512,512]{1,0:T(8,128)S(1)}, f32[512,512]{1,0:T(8,128)}, u32[]{:S(2)}) copy-start(f32[512,512]{1,0:T(8,128)} %grad_ref.1) | copy-start | bytes 3145732
  7.2 98.1 %all-gather.3.cloned.1.call-start = ((), (), s32[]{:S(2)}) async-start(), calls=%async_computation.1 | async-start | bytes 4526080 | tf_op jit(solution)/shard_map/all_gather | solution.py:131
  13.6 2.2 %copy-start.1 = (f32[512,512]{1,0:T(8,128)S(1)}, f32[512,512]{1,0:T(8,128)}, u32[]{:S(2)}) copy-start(f32[512,512]{1,0:T(8,128)} %copy.45) | copy-start | bytes 3145732
  13.6 2.2 %copy-start.12 = (f32[512,512]{1,0:T(8,128)S(1)}, f32[512,512]{1,0:T(8,128)}, u32[]{:S(2)}) copy-start(f32[512,512]{1,0:T(8,128)} %param.7) | copy-start | bytes 3145732
  15.9 3.9 %copy-start.7 = (f32[512,128]{1,0:T(8,128)}, f32[512,128]{1,0:T(8,128)S(1)}, u32[]{:S(2)}) copy-start(f32[512,128]{1,0:T(8,128)S(1)} %fusion.22) | copy-start | bytes 786436
  19.1 0.7 copy-start.5
  20.6 10.3 %collective-permute-start = (f32[520,128]{1,0:T(8,128)}, f32[520,128]{1,0:T(8,128)}, u32[]{:S(2)}, u32[]{:S(2)}) collective-permute-start(f32[520,128]{1,0:T(8,128)} %maximum_maximum_fusion), channel_id=1, source_target_pairs={{0,16},{16,0},{1,17},{17,1},{2,18},{18,2},{3,19},{19,3},{4,20},{20... | collective-permute-start | bytes 798728 | tf_op jit(solution)/shard_map/ppermute | solution.py:120
  31.7 2.1 %copy-start.16 = (f32[4]{0:T(128)}, f32[4]{0:T(128)S(1)}, u32[]{:S(2)}) copy-start(f32[4]{0:T(128)S(1)} %get-tuple-element.8) | copy-start | bytes 52
  31.8 3.1 %copy-start.14 = (f32[4]{0:T(128)}, f32[4]{0:T(128)S(1)}, u32[]{:S(2)}) copy-start(f32[4]{0:T(128)S(1)} %get-tuple-element.9) | copy-start | bytes 52
  32.8 1.1 copy-start.10
  110.4 4.6 %copy-start.15 = (f32[4]{0:T(128)S(1)}, f32[4]{0:T(128)}, u32[]{:S(2)}) copy-start(f32[4]{0:T(128)} %copy-done.14) | copy-start | bytes 52
  110.4 4.8 %copy-start.17 = (f32[4]{0:T(128)S(1)}, f32[4]{0:T(128)}, u32[]{:S(2)}) copy-start(f32[4]{0:T(128)} %copy-done.16) | copy-start | bytes 52
  112.0 3.1 %copy-start.8 = (f32[512,128]{1,0:T(8,128)S(1)}, f32[512,128]{1,0:T(8,128)}, u32[]{:S(2)}) copy-start(f32[512,128]{1,0:T(8,128)} %copy-done.7) | copy-start | bytes 786436
  112.0 3.2 %copy-start.6 = (f32[512,128]{1,0:T(8,128)S(1)}, f32[512,128]{1,0:T(8,128)}, u32[]{:S(2)}) copy-start(f32[512,128]{1,0:T(8,128)} %copy-done.5) | copy-start | bytes 786436
  112.0 3.2 %copy-start.11 = (f32[256,128]{1,0:T(8,128)S(1)}, f32[256,128]{1,0:T(8,128)}, u32[]{:S(2)}) copy-start(f32[256,128]{1,0:T(8,128)} %copy-done.10) | copy-start | bytes 393220
  112.0 14.2 %copy-start.3 = (f32[512,512]{1,0:T(8,128)S(1)}, f32[512,512]{1,0:T(8,128)}, u32[]{:S(2)}) copy-start(f32[512,512]{1,0:T(8,128)} %get-tuple-element.6) | copy-start | bytes 3145732
  112.0 14.2 %copy-start.9 = (f32[512,128]{1,0:T(8,128)S(1)}, f32[512,128]{1,0:T(8,128)}, u32[]{:S(2)}) copy-start(f32[512,128]{1,0:T(8,128)} %param.9) | copy-start | bytes 786436
  115.2 13.8 %copy-start.13 = (f32[512,128]{0,1:T(8,128)S(1)}, f32[512,128]{0,1:T(8,128)}, u32[]{:S(2)}) copy-start(f32[512,128]{0,1:T(8,128)} %fusion.24) | copy-start | bytes 786436
  115.4 12.1 %collective-permute-start.1 = (f32[512,128]{1,0:T(8,128)S(1)}, f32[512,128]{1,0:T(8,128)S(1)}, u32[]{:S(2)}, u32[]{:S(2)}) collective-permute-start(f32[512,128]{1,0:T(8,128)S(1)} %pad_maximum_fusion.1), channel_id=1, source_target_pairs={{0,16},{16,0},{1,17},{17,1},{2,18},{18,2},{3,19},{19,3},{4,20},{20... | collective-permute-start | bytes 786440 | tf_op jit(solution)/shard_map/ppermute | solution.py:159
  127.7 2.1 %copy-start.4 = (f32[8,64,128]{2,1,0:T(8,128)}, f32[8,64,128]{2,1,0:T(8,128)S(1)}, u32[]{:S(2)}) copy-start(f32[8,64,128]{2,1,0:T(8,128)S(1)} %pad_maximum_fusion.2) | copy-start | bytes 786436
  130.9 17.4 %all-to-all-start = ((f32[16,32,256]{2,1,0:T(8,128)}), f32[16,32,256]{2,1,0:T(8,128)S(1)}, u32[]{:S(2)}, u32[]{:S(2)}) async-start(f32[16,32,256]{2,1,0:T(8,128)} %bitcast.32), calls=%async_computation | async-start | bytes 1048576 | tf_op jit(solution)/shard_map/all_to_all | solution.py:212
Sparse Core Ops, SparseCore 0:
  35.8 69.3 all-gather.2

commit v5 on v2

--- a/solution.py
+++ b/solution.py
@@ -96,74 +96,53 @@
 
 def chip_scans(ends, starts, total):
     chips = lax.axis_size("z")
-    chip = lax.axis_index("z")
     core = lax.axis_index("core")
     head_count, width, state_width = ends.shape
-    half = head_count // 2
-    rows = half * width
+    rows = head_count * width
+    both = ("z", "core")
     swap = [(0, 1), (1, 0)]
-    mine_lo = core * half
-    other_lo = (1 - core) * half
-
-    def heads(value, lo):
-        return lax.dynamic_slice_in_dim(value, lo, half, 0)
-
-    own_x, own_y, own_t = heads(ends, mine_lo), heads(starts, mine_lo), heads(total, mine_lo)
+    is_fwd = core == 0
+    tot_rows = pack_total(total, state_width)
+    mine = pick(is_fwd, ends, starts)
     outgoing = jnp.concatenate(
-        [
-            heads(ends, other_lo).reshape(rows, state_width),
-            heads(starts, other_lo).reshape(rows, state_width),
-            pack_total(heads(total, other_lo), state_width),
-        ],
-        axis=0,
+        [pick(is_fwd, starts, ends).reshape(rows, state_width), tot_rows], axis=0
     )
     incoming = lax.ppermute(outgoing, "core", swap)
-    got_x = incoming[:rows].reshape(half, width, state_width)
-    got_y = incoming[rows:2 * rows].reshape(half, width, state_width)
-    got_t = incoming[2 * rows:2 * rows + half, 0]
-    is_first = core == 0
-    x_first, x_second = pick(is_first, own_x, got_x), pick(is_first, got_x, own_x)
-    y_first, y_second = pick(is_first, own_y, got_y), pick(is_first, got_y, own_y)
-    t_first, t_second = pick(is_first, own_t, got_t), pick(is_first, got_t, own_t)
-    chip_x = join(x_first, x_second, t_second)
-    chip_y = join(y_second, y_first, t_first)
-    chip_t = t_first + t_second
-    gathered = lax.all_gather(
-        jnp.concatenate(
-            [
-                chip_x.reshape(rows, state_width),
-                chip_y.reshape(rows, state_width),
-                pack_total(chip_t, state_width),
-            ],
-            axis=0,
-        ),
-        "z",
-    )
-    all_x = gathered[:, :rows].reshape(chips, half, width, state_width)
-    all_y = gathered[:, rows:2 * rows].reshape(chips, half, width, state_width)
-    all_t = gathered[:, 2 * rows:2 * rows + half, 0]
-    src = jnp.arange(chips, dtype=jnp.int32)
-    between_fwd = (src[:, None] < src[None, :]) & (src[None, :] < chip)
-    between_bwd = (chip < src[None, :]) & (src[None, :] < src[:, None])
-    sum_fwd = jnp.sum(jnp.where(between_fwd[:, :, None], all_t[None, :, :], 0.0), axis=1)
-    sum_bwd = jnp.sum(jnp.where(between_bwd[:, :, None], all_t[None, :, :], 0.0), axis=1)
-    w_fwd = jnp.where((src < chip)[:, None], jnp.exp(sum_fwd), 0.0)
-    w_bwd = jnp.where((src > chip)[:, None], jnp.exp(sum_bwd), 0.0)
-    pre_x = jnp.einsum("ch,chpn->hpn", w_fwd, all_x, precision=highest)
-    pre_y = jnp.einsum("ch,chpn->hpn", w_bwd, all_y, precision=highest)
-    joined_x = join(pre_x, x_first, t_first)
-    joined_y = join(pre_y, y_second, t_second)
-    keep_x, send_x = pick(is_first, pre_x, joined_x), pick(is_first, joined_x, pre_x)
-    keep_y, send_y = pick(is_first, joined_y, pre_y), pick(is_first, pre_y, joined_y)
-    back = lax.ppermute(
-        jnp.concatenate([send_x.reshape(rows, state_width), send_y.reshape(rows, state_width)]),
-        "core",
-        swap,
-    )
-    recv_x = back[:rows].reshape(half, width, state_width)
-    recv_y = back[rows:].reshape(half, width, state_width)
-    state_in = jnp.concatenate([pick(is_first, keep_x, recv_x), pick(is_first, recv_x, keep_x)])
-    state_grad = jnp.concatenate([pick(is_first, keep_y, recv_y), pick(is_first, recv_y, keep_y)])
+    partner = incoming[:rows].reshape(head_count, width, state_width)
+    partner_t = incoming[rows:rows + head_count, 0]
+    chip_state = join(mine, partner, partner_t)
+    chip_t = total + partner_t
+
+    def packed(state, tot):
+        return jnp.concatenate(
+            [state.reshape(rows, state_width), pack_total(tot, state_width)], axis=0
+        )
+
+    def unpacked(value):
+        return value[:rows].reshape(head_count, width, state_width), value[rows:rows + head_count, 0]
+
+    def move(value, hop):
+        pairs = []
+        for z in range(chips):
+            if z + hop < chips:
+                pairs.append((2 * z, 2 * (z + hop)))
+            if z - hop >= 0:
+                pairs.append((2 * z + 1, 2 * (z - hop) + 1))
+        return lax.ppermute(value, both, pairs)
+
+    running = move(packed(chip_state, chip_t), 1)
+    hop = 1
+    while hop < chips:
+        got_state, got_t = unpacked(move(running, hop))
+        run_state, run_t = unpacked(running)
+        running = packed(join(got_state, run_state, run_t), got_t + run_t)
+        hop *= 2
+    prefix, unused = unpacked(running)
+    joined = join(prefix, mine, total)
+    back = lax.ppermute(joined.reshape(rows, state_width), "core", swap)
+    other = back.reshape(head_count, width, state_width)
+    state_in = pick(is_fwd, prefix, other)
+    state_grad = pick(is_fwd, other, prefix)
     return state_in, state_grad
 
 

time: 165 us -> 157 us (0.952)
  starting transfers between devices: 27 us -> 47.5 us
  between operations: 14.5 us -> 1.06 us
  waiting for transfers between devices: 50.8 us -> 41.2 us
  matrix products: 21.1 us -> 17.6 us
  local copies, waits for them, and re-layouts: 18.9 us -> 15.9 us
    all_gather x1 -> x0, waiting for transfers between devices: 41.6 us -> none  [chip_scans(): lax.all_gather(jnp.concatenate([chip_x.reshape(rows, state_width), chip_y...]
    ppermute x1 -> x6, waiting for transfers between devices: 0.1 us -> 32.3 us  [the longest x5 32.3 us: move(): return lax.ppermute(value, both, pairs)]
    ppermute x1 -> x6, starting transfers between devices: 11.5 us -> 31.1 us  [the longest x1 24.5 us: chip_scans(): back = lax.ppermute(joined.reshape(rows, state_width), 'core', swap)]
    slice x6 -> x3, local copies, waits for them, and re-layouts: 8.13 us -> 1.07 us  [the longest x2 0.91 us: unpacked(): value[rows:rows + head_count, 0]]
    dot_general x2 -> x0, matrix products: 6.06 us -> none  [the longest x1 3.82 us: chip_scans(): pre_x = jnp.einsum('ch,chpn->hpn', w_fwd, all_x, precision=highest)]
    add x2 -> x5, other arithmetic: 2.03 us -> 6.08 us  [join(): return jnp.exp(later_total)[:, None, None] * earlier + later]
    unnamed x45 -> x41, local copies, waits for them, and re-layouts: 3.08 us -> 6.38 us
    select_n x8 -> x0, other arithmetic: 2.82 us -> none  [the longest x6 1.4 us: pick(): return jnp.where(flag, when_true, when_false)]
  transfers between devices with their start and end apart: 4 -> 8, of which waited for: 4 -> 6; matrix products, arithmetic and copies ran while one was open for 8% -> 9% of each run, Pallas kernels for 11% -> 11%
where the time goes in v5:
time: 157 us; the launch traced here: 156 us
  starting transfers between devices  47.5 us (30%)
  waiting for transfers between devices  41.2 us (26%)
  Pallas kernels  17.8 us (11%)
  matrix products  17.6 us (11%)
  local copies, waits for them, and re-layouts  15.9 us (10%)
  other arithmetic  14.8 us (9%)
    ppermute x5, waiting for transfers between devices, move(): return lax.ppermute(value, both, pairs)  32.3 us
    ppermute x1, starting transfers between devices, chip_scans(): back = lax.ppermute(joined.reshape(rows, state_width), 'core', swap)  24.5 us
    pallas_call x1, Pallas kernels, block_terms(): pl.pallas_call(block_kernel, grid=(head_count // HEADS_PER_STEP,), in_spe...  17.8 us
    ppermute x1, starting transfers between devices, chip_scans(): incoming = lax.ppermute(outgoing, 'core', swap)  8.79 us
    all_to_all x1, waiting for transfers between devices, per_device(): spread = lax.all_to_all(both, 'head', 0, 0, tiled=True)  7.78 us
    all_to_all x1, starting transfers between devices, per_device(): spread = lax.all_to_all(both, 'head', 0, 0, tiled=True)  7.61 us
    ppermute x5, starting transfers between devices, move(): return lax.ppermute(value, both, pairs)  6.61 us
    unnamed x41, local copies, waits for them, and re-layouts  6.38 us
  transfers between devices with their start and end apart: 8, of which 6 were waited for; matrix products, arithmetic and copies ran while one was open for 9% of the time, Pallas kernels for 11%

profile of v5, /device:TPU:1, one launch (start us, length us, event | category | flops | bytes accessed | tf_op | source)
XLA Modules:
  0.0 155.8 jit_solution(2239603587531551175)
XLA Ops:
  0.7 0.8 select_reduce_fusion
  2.1 1.1 reduce-window.6
  3.8 1.1 broadcast_in_dim.35
  4.9 1.6 copy.30
  6.5 1.3 copy.27
  7.8 2.6 %fusion.13 = (f32[512,512]{1,0:T(8,128)S(1)}, f32[512,512]{1,0:T(8,128)}) fusion(f32[512,512]{1,0:T(8,128)S(1)} %copy.30, f32[512,512]{1,0:T(8,128)} %param.7, f32[512,512]{1,0:T(8,128)S(1)} %copy.25), kind=kLoop, calls=%fused_computation.48 | loop fusion | flops 524288 | bytes 5242880 | tf_op jit(solution)/shard_map/mul | solution.py:166
  10.4 2.5 %fusion.16 = f32[512,128]{1,0:T(8,128)} fusion(f32[512,512]{1,0:T(8,128)S(1)} %get-tuple-element.17, f32[512,128]{1,0:T(8,128)S(1)} %copy-done), kind=kOutput, calls=%fused_computation.51 | convolution fusion | flops 402653184 | bytes 1572864 | tf_op jit(solution)/shard_map/tk,tn->kn/dot_general | solution.py:168
  12.9 1.4 bitcast_multiply_fusion
  14.3 1.0 copy-done.1
  15.3 1.7 %broadcast_select_fusion.2 = (f32[512,128]{1,0:T(8,128)S(1)}, f32[512,128]{1,0:T(8,128)}) fusion(f32[512,128]{1,0:T(8,128)S(1)} %copy-done.6, pred[]{:T(512)S(6)} %eq.19, f32[512,512]{0,1:T(8,128)S(1)} %bitcast_multiply_fusion, f32[512,128]{1,0:T(8,128)S(1)} %copy-done.12), kind=kOutput, calls=%fused_computation.29 | convolution fusion | flops 402718720 | bytes 2097153 | tf_op jit(solution)/shard_map/tk,tn->kn/dot_general | solution.py:169
  17.1 8.8 %collective-permute-start = (f32[520,128]{1,0:T(8,128)S(1)}, f32[520,128]{1,0:T(8,128)S(1)}, u32[]{:S(2)}, u32[]{:S(2)}) collective-permute-start(f32[520,128]{1,0:T(8,128)S(1)} %pad_maximum_fusion.1), channel_id=1, source_target_pairs={{0,16},{16,0},{1,17},{17,1},{2,18},{18,2},{3,19},{19,3},{4,20},{20... | collective-permute-start | bytes 798728 | tf_op jit(solution)/shard_map/ppermute | solution.py:110
  25.9 1.1 collective-permute-done
  27.1 0.7 copy-done.17
  28.1 1.2 slice_add_fusion.1
  29.4 1.3 collective-permute-start.1
  30.7 5.9 %collective-permute-done.1 = f32[520,128]{1,0:T(8,128)S(1)} collective-permute-done((f32[520,128]{1,0:T(8,128)S(1)}, f32[520,128]{1,0:T(8,128)S(1)}, u32[]{:S(2)}, u32[]{:S(2)}) %collective-permute-start.1) | collective-permute-done | bytes 266272 | tf_op jit(solution)/shard_map/ppermute | solution.py:131
  36.6 1.3 collective-permute-start.2
  37.9 5.9 %collective-permute-done.2 = f32[520,128]{1,0:T(8,128)S(1)} collective-permute-done((f32[520,128]{1,0:T(8,128)S(1)}, f32[520,128]{1,0:T(8,128)S(1)}, u32[]{:S(2)}, u32[]{:S(2)}) %collective-permute-start.2) | collective-permute-done | bytes 266272 | tf_op jit(solution)/shard_map/ppermute | solution.py:131
  44.6 1.2 slice_add_fusion
  45.7 0.7 copy-done.10
  46.6 1.3 collective-permute-start.3
  47.9 8.5 %collective-permute-done.3 = f32[520,128]{1,0:T(8,128)S(1)} collective-permute-done((f32[520,128]{1,0:T(8,128)S(1)}, f32[520,128]{1,0:T(8,128)S(1)}, u32[]{:S(2)}, u32[]{:S(2)}) %collective-permute-start.3) | collective-permute-done | bytes 266272 | tf_op jit(solution)/shard_map/ppermute | solution.py:131
  56.4 0.7 copy-done.15
  57.4 1.2 fusion.5
  58.6 0.7 copy-done.9
  59.3 0.8 pad_maximum_fusion.4
  60.1 1.3 collective-permute-start.4
  61.5 12.0 %collective-permute-done.4 = f32[520,128]{1,0:T(8,128)} collective-permute-done((f32[520,128]{1,0:T(8,128)}, f32[520,128]{1,0:T(8,128)}, u32[]{:S(2)}, u32[]{:S(2)}) %collective-permute-start.4) | collective-permute-done | bytes 266272 | tf_op jit(solution)/shard_map/ppermute | solution.py:131
  73.5 0.8 slice_reduce_fusion.1
  74.3 1.2 fusion.4
  75.5 0.7 copy-done.11
  76.2 0.9 pad_maximum_fusion.5
  77.1 1.5 collective-permute-start.5
  78.5 2.9 %fusion.15.scores_t_ref = f32[512,512]{1,0:T(8,128)} fusion(f32[512,128]{1,0:T(8,128)S(1)} %copy-done, f32[512,128]{1,0:T(8,128)} %param.9), kind=kOutput, calls=%fused_computation.50 | convolution fusion | flops 402653184 | bytes 1572864 | tf_op jit(solution)/shard_map/sn,tn->st/dot_general | solution.py:176
  81.5 0.6 copy.24
  82.1 2.0 %copy.26.cum_col_ref = f32[8,512,1]{2,1,0:T(8,128)} copy(f32[8,512,1]{1,0,2:T(8,128)S(1)} %bitcast.47) | data formatting | bytes 32768 | tf_op jit(solution)/shard_map/reduce_window_sum
  84.2 17.8 %shard_map.94 = (f32[512,512]{1,0:T(8,128)}, f32[512,512]{1,0:T(8,128)}) custom-call(f32[8,1,512]{2,1,0:T(1,128)} %bitcast.49, f32[8,512,1]{2,1,0:T(8,128)} %copy.26.cum_col_ref, f32[512,512]{1,0:T(8,128)} %fusion.15.scores_t_ref, f32[512,512]{1,0:T(8,128)} %get-tuple-element.18.in_ref, f32[512,512]{1,0:T(8,128)} %grad_ref.1), custom_call_target="tpu_custom_call" | custom-call | tf_op jit(solution)/shard_map/pallas_call | solution.py:60
  102.0 2.7 %fusion.18 = f32[512,128]{0,1:T(8,128)} fusion(f32[512,512]{1,0:T(8,128)} %get-tuple-element.6, f32[512,128]{1,0:T(8,128)S(1)} %copy-done), kind=kOutput, calls=%fused_computation.53 | convolution fusion | flops 402653184 | bytes 1572864 | tf_op jit(solution)/shard_map/st,sn->tn/dot_general | solution.py:179
  104.8 1.4 multiply_add_fusion
  106.3 24.5 %collective-permute-start.6 = (f32[512,128]{1,0:T(8,128)S(1)}, f32[512,128]{1,0:T(8,128)S(1)}, u32[]{:S(2)}, u32[]{:S(2)}) collective-permute-start(f32[512,128]{1,0:T(8,128)S(1)} %get-tuple-element.11), channel_id=1, source_target_pairs={{0,16},{16,0},{1,17},{17,1},{2,18},{18,2},{3,19},{19,3},{4,20},{20... | collective-permute-start | bytes 786440 | tf_op jit(solution)/shard_map/ppermute | solution.py:142
  130.8 2.5 %fusion.17 = f32[512,128]{0,1:T(8,128)S(1)} fusion(f32[512,512]{1,0:T(8,128)} %get-tuple-element.6, f32[512,128]{1,0:T(8,128)} %param.9), kind=kOutput, calls=%fused_computation.52 | convolution fusion | flops 402653184 | bytes 1572864 | tf_op jit(solution)/shard_map/dot_general | solution.py:178
  133.3 0.8 convolution_add_fusion
  134.1 1.2 convolution_add_fusion.1
  135.4 1.0 copy.32
  136.4 7.6 %all-to-all-start = ((f32[16,32,256]{2,1,0:T(8,128)}), f32[16,32,256]{2,1,0:T(8,128)S(1)}, u32[]{:S(2)}, u32[]{:S(2)}) async-start(f32[16,32,256]{2,1,0:T(8,128)} %bitcast.44), calls=%async_computation | async-start | bytes 1048576 | tf_op jit(solution)/shard_map/all_to_all | solution.py:190
  144.0 3.3 %fusion.2 = f32[512,512]{1,0:T(8,128)} fusion(f32[512,512]{1,0:T(8,128)S(1)} %copy.25, f32[512,512]{1,0:T(8,128)} %get-tuple-element.5, f32[512,512]{1,0:T(8,128)S(1)} %copy.30, f32[512,128]{1,0:T(8,128)S(1)} %copy-done, f32[512,128]{1,0:T(8,128)S(1)} %copy-done.8, f32[512,128]{1,0:T(8,128)S(1)} %copy-done.5, pred[]{:T(512)S(6)} %eq.19), kind=kOutput, calls=%fused_computation.3 | convolution fusion | flops 403505152 | bytes 4980737 | tf_op jit(solution)/shard_map/tn,kn->tk/dot_general | solution.py:185
  147.3 7.8 %all-to-all-done = f32[16,32,256]{2,1,0:T(8,128)S(1)} async-done(((f32[16,32,256]{2,1,0:T(8,128)}), f32[16,32,256]{2,1,0:T(8,128)S(1)}, u32[]{:S(2)}, u32[]{:S(2)}) %all-to-all-start) | async-done | bytes 524320 | tf_op jit(solution)/shard_map/all_to_all | solution.py:190
  155.1 0.6 fusion.14
  (76 shorter events, 3.5 us)
Async XLA Ops:
  0.6 9.7 %copy-start = (f32[512,128]{1,0:T(8,128)S(1)}, f32[512,128]{1,0:T(8,128)}, u32[]{:S(2)}) copy-start(f32[512,128]{1,0:T(8,128)} %param.8) | copy-start | bytes 786436
  0.6 1.4 copy-start.18
  0.7 1.4 copy-start.19
  2.0 4.5 %copy-start.3 = (f32[512,512]{1,0:T(8,128)S(1)}, f32[512,512]{1,0:T(8,128)}, u32[]{:S(2)}) copy-start(f32[512,512]{1,0:T(8,128)} %grad_ref.1) | copy-start | bytes 3145732
  12.9 2.4 %copy-start.6 = (f32[512,128]{1,0:T(8,128)S(1)}, f32[512,128]{1,0:T(8,128)}, u32[]{:S(2)}) copy-start(f32[512,128]{1,0:T(8,128)} %fusion.16) | copy-start | bytes 786436
  12.9 2.4 %copy-start.12 = (f32[512,128]{1,0:T(8,128)S(1)}, f32[512,128]{1,0:T(8,128)}, u32[]{:S(2)}) copy-start(f32[512,128]{1,0:T(8,128)} %param.9) | copy-start | bytes 786436
  14.3 1.0 copy-start.1
  17.1 9.9 %collective-permute-start = (f32[520,128]{1,0:T(8,128)S(1)}, f32[520,128]{1,0:T(8,128)S(1)}, u32[]{:S(2)}, u32[]{:S(2)}) collective-permute-start(f32[520,128]{1,0:T(8,128)S(1)} %pad_maximum_fusion.1), channel_id=1, source_target_pairs={{0,16},{16,0},{1,17},{17,1},{2,18},{18,2},{3,19},{19,3},{4,20},{20... | collective-permute-start | bytes 798728 | tf_op jit(solution)/shard_map/ppermute | solution.py:110
  27.1 0.7 copy-start.17
  29.4 7.2 %collective-permute-start.1 = (f32[520,128]{1,0:T(8,128)S(1)}, f32[520,128]{1,0:T(8,128)S(1)}, u32[]{:S(2)}, u32[]{:S(2)}) collective-permute-start(f32[520,128]{1,0:T(8,128)S(1)} %pad_maximum_fusion.2), channel_id=1, source_target_pairs={{0,32},{32,64},{48,16},{64,96},{80,48},{96,128},{112,80},{128,160}... | collective-permute-start | bytes 798728 | tf_op jit(solution)/shard_map/ppermute | solution.py:131
  36.6 7.2 %copy-start.14 = (f32[520,128]{1,0:T(8,128)}, f32[520,128]{1,0:T(8,128)S(1)}, u32[]{:S(2)}) copy-start(f32[520,128]{1,0:T(8,128)S(1)} %collective-permute-done.1) | copy-start | bytes 798724
  36.6 7.1 %collective-permute-start.2 = (f32[520,128]{1,0:T(8,128)S(1)}, f32[520,128]{1,0:T(8,128)S(1)}, u32[]{:S(2)}, u32[]{:S(2)}) collective-permute-start(f32[520,128]{1,0:T(8,128)S(1)} %collective-permute-done.1), channel_id=1, source_target_pairs={{0,32},{32,64},{48,16},{64,96},{80,48},{96,128},{112,80},{128,160}... | collective-permute-start | bytes 798728 | tf_op jit(solution)/shard_map/ppermute | solution.py:131
  43.7 0.7 copy-start.16
  45.7 0.7 copy-start.10
  46.6 9.8 %collective-permute-start.3 = (f32[520,128]{1,0:T(8,128)S(1)}, f32[520,128]{1,0:T(8,128)S(1)}, u32[]{:S(2)}, u32[]{:S(2)}) collective-permute-start(f32[520,128]{1,0:T(8,128)S(1)} %pad_maximum_fusion.3), channel_id=1, source_target_pairs={{0,64},{32,96},{64,128},{80,16},{96,160},{112,48},{128,192},{144,8... | collective-permute-start | bytes 798728 | tf_op jit(solution)/shard_map/ppermute | solution.py:131
  56.4 0.7 copy-start.15
  58.6 0.7 copy-start.9
  60.1 13.4 %collective-permute-start.4 = (f32[520,128]{1,0:T(8,128)}, f32[520,128]{1,0:T(8,128)}, u32[]{:S(2)}, u32[]{:S(2)}) collective-permute-start(f32[520,128]{1,0:T(8,128)} %pad_maximum_fusion.4), channel_id=1, source_target_pairs={{0,128},{32,160},{64,192},{96,224},{128,256},{144,16},{160,288},{1... | collective-permute-start | bytes 798728 | tf_op jit(solution)/shard_map/ppermute | solution.py:131
  75.5 0.7 copy-start.11
  77.1 27.8 %collective-permute-start.5 = (f32[520,128]{1,0:T(8,128)}, f32[520,128]{1,0:T(8,128)}, u32[]{:S(2)}, u32[]{:S(2)}) collective-permute-start(f32[520,128]{1,0:T(8,128)} %pad_maximum_fusion.5), channel_id=1, source_target_pairs={{0,256},{32,288},{64,320},{96,352},{128,384},{160,416},{192,448},{... | collective-permute-start | bytes 798728 | tf_op jit(solution)/shard_map/ppermute | solution.py:131
  104.8 28.4 %copy-start.2 = (f32[512,512]{0,1:T(8,128)S(1)}, f32[512,512]{0,1:T(8,128)}, u32[]{:S(2)}) copy-start(f32[512,512]{0,1:T(8,128)} %copy-done.1) | copy-start | bytes 3145732
  104.8 28.5 %copy-start.13 = (f32[512,128]{0,1:T(8,128)S(1)}, f32[512,128]{0,1:T(8,128)}, u32[]{:S(2)}) copy-start(f32[512,128]{0,1:T(8,128)} %fusion.18) | copy-start | bytes 786436
  106.3 29.1 %copy-start.4 = (f32[512,128]{1,0:T(8,128)}, f32[512,128]{1,0:T(8,128)S(1)}, u32[]{:S(2)}) copy-start(f32[512,128]{1,0:T(8,128)S(1)} %get-tuple-element.12) | copy-start | bytes 786436
  106.3 27.0 %collective-permute-start.6 = (f32[512,128]{1,0:T(8,128)S(1)}, f32[512,128]{1,0:T(8,128)S(1)}, u32[]{:S(2)}, u32[]{:S(2)}) collective-permute-start(f32[512,128]{1,0:T(8,128)S(1)} %get-tuple-element.11), channel_id=1, source_target_pairs={{0,16},{16,0},{1,17},{17,1},{2,18},{18,2},{3,19},{19,3},{4,20},{20... | collective-permute-start | bytes 786440 | tf_op jit(solution)/shard_map/ppermute | solution.py:142
  133.3 2.1 %copy-start.7 = (f32[512,128]{1,0:T(8,128)}, f32[512,128]{1,0:T(8,128)S(1)}, u32[]{:S(2)}) copy-start(f32[512,128]{1,0:T(8,128)S(1)} %collective-permute-done.6) | copy-start | bytes 786436
  135.4 8.6 %copy-start.5 = (f32[512,128]{1,0:T(8,128)S(1)}, f32[512,128]{1,0:T(8,128)}, u32[]{:S(2)}) copy-start(f32[512,128]{1,0:T(8,128)} %copy-done.4) | copy-start | bytes 786436
  135.4 8.6 %copy-start.8 = (f32[512,128]{1,0:T(8,128)S(1)}, f32[512,128]{1,0:T(8,128)}, u32[]{:S(2)}) copy-start(f32[512,128]{1,0:T(8,128)} %copy-done.7) | copy-start | bytes 786436
  136.4 18.7 %all-to-all-start = ((f32[16,32,256]{2,1,0:T(8,128)}), f32[16,32,256]{2,1,0:T(8,128)S(1)}, u32[]{:S(2)}, u32[]{:S(2)}) async-start(f32[16,32,256]{2,1,0:T(8,128)} %bitcast.44), calls=%async_computation | async-start | bytes 1048576 | tf_op jit(solution)/shard_map/all_to_all | solution.py:190

commit v6 on v4

--- a/solution.py
+++ b/solution.py
@@ -94,7 +94,7 @@
     return jnp.where(flag, when_true, when_false)
 
 
-def chip_scans(ends, starts, total):
+def gathered_scans(ends, starts, total, hold):
     chips = lax.axis_size("z")
     chip = lax.axis_index("z")
     core = lax.axis_index("core")
@@ -117,7 +117,7 @@
         ],
         axis=0,
     )
-    incoming = lax.ppermute(outgoing, "core", swap)
+    incoming, held = hold(outgoing)
     got_x = incoming[:rows].reshape(half, width, state_width)
     got_y = incoming[rows:2 * rows].reshape(half, width, state_width)
     got_t = incoming[2 * rows:2 * rows + half, 0]
@@ -128,17 +128,20 @@
     chip_x = join(x_first, x_second, t_second)
     chip_y = join(y_second, y_first, t_first)
     chip_t = t_first + t_second
-    gathered = lax.all_gather(
-        jnp.concatenate(
-            [
-                chip_x.reshape(rows, state_width),
-                chip_y.reshape(rows, state_width),
-                pack_total(chip_t, state_width),
-            ],
-            axis=0,
-        ),
-        "z",
-    )
+    payload, held = lax.optimization_barrier(
+        (
+            jnp.concatenate(
+                [
+                    chip_x.reshape(rows, state_width),
+                    chip_y.reshape(rows, state_width),
+                    pack_total(chip_t, state_width),
+                ],
+                axis=0,
+            ),
+            held,
+        )
+    )
+    gathered = lax.all_gather(payload, "z")
     all_t = gathered[:, 2 * rows:2 * rows + half, 0]
     src = jnp.arange(chips, dtype=jnp.int32)
     between_fwd = (src[:, None] < src[None, :]) & (src[None, :] < chip)
@@ -165,7 +168,91 @@
     recv_y = back[rows:].reshape(half, width, state_width)
     state_in = jnp.concatenate([pick(is_first, keep_x, recv_x), pick(is_first, recv_x, keep_x)])
     state_grad = jnp.concatenate([pick(is_first, keep_y, recv_y), pick(is_first, recv_y, keep_y)])
+    return state_in, state_grad, held
+
+
+def stepped_scans(ends, starts, total, hold):
+    chips = lax.axis_size("z")
+    core = lax.axis_index("core")
+    head_count, width, state_width = ends.shape
+    rows = head_count * width
+    both = ("z", "core")
+    swap = [(0, 1), (1, 0)]
+    is_fwd = core == 0
+    tot_rows = pack_total(total, state_width)
+    mine = pick(is_fwd, ends, starts)
+    outgoing = jnp.concatenate(
+        [pick(is_fwd, starts, ends).reshape(rows, state_width), tot_rows], axis=0
+    )
+    incoming = hold(outgoing)
+    partner = incoming[:rows].reshape(head_count, width, state_width)
+    partner_t = incoming[rows:rows + head_count, 0]
+    chip_state = join(mine, partner, partner_t)
+    chip_t = total + partner_t
+
+    def packed(state, tot):
+        return jnp.concatenate(
+            [state.reshape(rows, state_width), pack_total(tot, state_width)], axis=0
+        )
+
+    def unpacked(value):
+        return value[:rows].reshape(head_count, width, state_width), value[rows:rows + head_count, 0]
+
+    def move(value, hop):
+        pairs = []
+        for z in range(chips):
+            if z + hop < chips:
+                pairs.append((2 * z, 2 * (z + hop)))
+            if z - hop >= 0:
+                pairs.append((2 * z + 1, 2 * (z - hop) + 1))
+        return lax.ppermute(value, both, pairs)
+
+    running = move(packed(chip_state, chip_t), 1)
+    hop = 1
+    while hop < chips:
+        got_state, got_t = unpacked(move(running, hop))
+        run_state, run_t = unpacked(running)
+        running = packed(join(got_state, run_state, run_t), got_t + run_t)
+        hop *= 2
+    prefix, unused = unpacked(running)
+    joined = join(prefix, mine, total)
+    back = lax.ppermute(joined.reshape(rows, state_width), "core", swap)
+    other = back.reshape(head_count, width, state_width)
+    state_in = pick(is_fwd, prefix, other)
+    state_grad = pick(is_fwd, other, prefix)
     return state_in, state_grad
+
+
+def chip_scans(ends, starts, total):
+    part = ends.shape[0] // 2
+    state_width = ends.shape[2]
+    box = {}
+
+    def hold_b(outgoing):
+        box["b"] = outgoing
+        return box["b_in"]
+
+    def hold_a(outgoing):
+        rows_a = outgoing.shape[0]
+        both = lax.ppermute(
+            jnp.concatenate([outgoing, box["b"]], axis=0), "core", [(0, 1), (1, 0)]
+        )
+        box["b_in"] = both[rows_a:]
+        return both[:rows_a], both[rows_a:]
+
+    b_ends, b_starts, b_total = ends[part:], starts[part:], total[part:]
+    core = lax.axis_index("core")
+    rows_b = part * ends.shape[1]
+    box["b"] = jnp.concatenate(
+        [
+            pick(core == 0, b_starts, b_ends).reshape(rows_b, state_width),
+            pack_total(b_total, state_width),
+        ],
+        axis=0,
+    )
+    in_a, grad_a, held = gathered_scans(ends[:part], starts[:part], total[:part], hold_a)
+    in_b, grad_b = stepped_scans(b_ends, b_starts, b_total, lambda unused: held)
+    return jnp.concatenate([in_a, in_b]), jnp.concatenate([grad_a, grad_b])
 
 
 def per_device(

time: 157 us -> 186 us (1.18)
  the two profiles are of different devices: /device:TPU:1 before, /device:TPU:32 now
where the time goes in v6:
time: 186 us; the launch traced here: 184 us
  starting transfers between devices  55.2 us (30%)
  other arithmetic  33.7 us (18%)
  local copies, waits for them, and re-layouts  26.5 us (14%)
  waiting for transfers between devices  19.5 us (10%)
  Pallas kernels  17.8 us (10%)
  matrix products  16.9 us (9%)
  between operations  14.7 us (8%)
    ppermute x5, starting transfers between devices, move(): return lax.ppermute(value, both, pairs)  38.1 us
    pallas_call x1, Pallas kernels, block_terms(): pl.pallas_call(block_kernel, grid=(head_count // HEADS_PER_STEP,), in_spe...  17.8 us
    all_to_all x1, starting transfers between devices, per_device(): spread = lax.all_to_all(both, 'head', 0, 0, tiled=True)  10.9 us
    all_to_all x1, waiting for transfers between devices, per_device(): spread = lax.all_to_all(both, 'head', 0, 0, tiled=True)  8.77 us
    ppermute x5, waiting for transfers between devices, move(): return lax.ppermute(value, both, pairs)  7.85 us
    unnamed x66, local copies, waits for them, and re-layouts  7.64 us
    slice x4, other arithmetic, unpacked(): value[:rows].reshape(head_count, width, state_width)  6.16 us
    another operation x3, local copies, waits for them, and re-layouts  4.01 us
  transfers between devices with their start and end apart: 10, of which 8 were waited for; matrix products, arithmetic and copies ran while one was open for 18% of the time, Pallas kernels for 10%

profile of v6, /device:TPU:32, one launch (start us, length us, event | category | flops | bytes accessed | tf_op | source)
XLA Modules:
  0.0 184.2 jit_solution(3340466940129263358)
XLA Ops:
  9.5 1.1 reduce-window.6
  12.0 1.3 copy.36
  14.6 1.0 fusion.29
  16.3 2.9 %fusion.18 = (f32[512,512]{1,0:T(8,128)S(1)}, f32[512,512]{1,0:T(8,128)}) fusion(f32[512,512]{1,0:T(8,128)} %copy.36, f32[512,512]{1,0:T(8,128)} %param.7, f32[512,512]{1,0:T(8,128)S(1)} %copy.29), kind=kLoop, calls=%fused_computation.95 | loop fusion | flops 524288 | bytes 5242880 | tf_op jit(solution)/shard_map/mul | solution.py:275
  19.2 1.8 fusion.28
  22.4 0.8 constant_dynamic-slice_fusion.2
  25.4 1.6 select_dynamic-update-slice_fusion
  27.6 1.9 %collective-permute-start = (f32[528,128]{1,0:T(8,128)}, f32[528,128]{1,0:T(8,128)}, u32[]{:S(2)}, u32[]{:S(2)}) collective-permute-start(f32[528,128]{1,0:T(8,128)} %constant_dynamic-update-slice_fusion), channel_id=1, source_target_pairs={{0,16},{16,0},{1,17},{17,1},{2,18},{18,2},{3,19},{19,3},{4,20},{20... | collective-permute-start | bytes 811016 | tf_op jit(solution)/shard_map/ppermute | solution.py:237
  29.6 1.9 %collective-permute-done = f32[528,128]{1,0:T(8,128)} collective-permute-done((f32[528,128]{1,0:T(8,128)}, f32[528,128]{1,0:T(8,128)}, u32[]{:S(2)}, u32[]{:S(2)}) %collective-permute-start) | collective-permute-done | bytes 270368 | tf_op jit(solution)/shard_map/ppermute | solution.py:237
  31.4 0.8 add_reduce_fusion.1
  32.3 0.9 fusion.19
  33.8 0.9 select_add_fusion.1
  35.5 0.9 slice.165
  36.4 0.9 add_reduce_fusion
  37.5 1.1 slice_add_fusion
  39.3 3.8 %collective-permute-start.2 = (f32[264,128]{1,0:T(8,128)}, f32[264,128]{1,0:T(8,128)S(1)}, u32[]{:S(2)}, u32[]{:S(2)}) collective-permute-start(f32[264,128]{1,0:T(8,128)} %pad_maximum_fusion.3), channel_id=1, source_target_pairs={{0,32},{32,64},{48,16},{64,96},{80,48},{96,128},{112,80},{128,160}... | collective-permute-start | bytes 405512 | tf_op jit(solution)/shard_map/ppermute | solution.py:208
  43.2 6.1 %collective-permute-done.2 = f32[264,128]{1,0:T(8,128)S(1)} collective-permute-done((f32[264,128]{1,0:T(8,128)}, f32[264,128]{1,0:T(8,128)S(1)}, u32[]{:S(2)}, u32[]{:S(2)}) %collective-permute-start.2) | collective-permute-done | bytes 135200 | tf_op jit(solution)/shard_map/ppermute | solution.py:208
  49.3 1.9 %collective-permute-start.3 = (f32[264,128]{1,0:T(8,128)S(1)}, f32[264,128]{1,0:T(8,128)}, u32[]{:S(2)}, u32[]{:S(2)}) collective-permute-start(f32[264,128]{1,0:T(8,128)S(1)} %collective-permute-done.2), channel_id=1, source_target_pairs={{0,32},{32,64},{48,16},{64,96},{80,48},{96,128},{112,80},{128,160}... | collective-permute-start | bytes 405512 | tf_op jit(solution)/shard_map/ppermute | solution.py:208
  51.2 2.9 %fusion.27.scores_t_ref = f32[512,512]{1,0:T(8,128)} fusion(f32[512,128]{1,0:T(8,128)S(1)} %copy-done, f32[512,128]{1,0:T(8,128)} %param.9), kind=kOutput, calls=%fused_computation.104 | convolution fusion | flops 402653184 | bytes 1572864 | tf_op jit(solution)/shard_map/sn,tn->st/dot_general | solution.py:285
  54.1 1.3 copy.28
  55.4 2.7 %copy.30.cum_col_ref = f32[8,512,1]{2,1,0:T(8,128)} copy(f32[8,512,1]{1,0,2:T(8,128)} %bitcast.113) | data formatting | bytes 32768 | tf_op jit(solution)/shard_map/reduce_window_sum
  58.1 17.8 %shard_map.94 = (f32[512,512]{1,0:T(8,128)}, f32[512,512]{1,0:T(8,128)}) custom-call(f32[8,1,512]{2,1,0:T(1,128)} %bitcast.121, f32[8,512,1]{2,1,0:T(8,128)} %copy.30.cum_col_ref, f32[512,512]{1,0:T(8,128)} %fusion.27.scores_t_ref, f32[512,512]{1,0:T(8,128)} %get-tuple-element.31.in_ref, f32[512,512]{1,0:T(8,128)} %grad_ref.1), custom_call_target="tpu_custom_call" | custom-call | tf_op jit(solution)/shard_map/pallas_call | solution.py:60
  75.9 0.8 fusion.14
  76.9 1.7 fusion.23
  79.4 7.3 %collective-permute-start.4 = (f32[264,128]{1,0:T(8,128)}, f32[264,128]{1,0:T(8,128)}, u32[]{:S(2)}, u32[]{:S(2)}) collective-permute-start(f32[264,128]{1,0:T(8,128)} %pad_maximum_fusion.4), channel_id=1, source_target_pairs={{0,64},{32,96},{64,128},{80,16},{96,160},{112,48},{128,192},{144,8... | collective-permute-start | bytes 405512 | tf_op jit(solution)/shard_map/ppermute | solution.py:208
  86.7 2.7 %fusion.31 = f32[512,128]{0,1:T(8,128)} fusion(f32[512,512]{1,0:T(8,128)} %get-tuple-element.10, f32[512,128]{1,0:T(8,128)S(1)} %copy-done), kind=kOutput, calls=%fused_computation.108 | convolution fusion | flops 402653184 | bytes 1572864 | tf_op jit(solution)/shard_map/st,sn->tn/dot_general | solution.py:288
  91.2 1.6 fusion.22
  93.5 10.6 %collective-permute-start.5 = (f32[264,128]{1,0:T(8,128)S(1)}, f32[264,128]{1,0:T(8,128)}, u32[]{:S(2)}, u32[]{:S(2)}) collective-permute-start(f32[264,128]{1,0:T(8,128)S(1)} %pad_maximum_fusion.5), channel_id=1, source_target_pairs={{0,128},{32,160},{64,192},{96,224},{128,256},{144,16},{160,288},{1... | collective-permute-start | bytes 405512 | tf_op jit(solution)/shard_map/ppermute | solution.py:208
  104.2 3.2 %fusion.30 = f32[512,128]{0,1:T(8,128)} fusion(f32[512,512]{1,0:T(8,128)} %get-tuple-element.10, f32[512,128]{1,0:T(8,128)} %param.9), kind=kOutput, calls=%fused_computation.107 | convolution fusion | flops 402653184 | bytes 1572864 | tf_op jit(solution)/shard_map/dot_general | solution.py:287
  107.9 1.0 collective-permute-done.5
  109.9 1.6 fusion.21
  112.9 14.4 %collective-permute-start.6 = (f32[264,128]{1,0:T(8,128)}, f32[264,128]{1,0:T(8,128)}, u32[]{:S(2)}, u32[]{:S(2)}) collective-permute-start(f32[264,128]{1,0:T(8,128)} %pad_maximum_fusion.6), channel_id=1, source_target_pairs={{0,256},{32,288},{64,320},{96,352},{128,384},{160,416},{192,448},{... | collective-permute-start | bytes 405512 | tf_op jit(solution)/shard_map/ppermute | solution.py:208
  127.3 1.2 fusion.9
  131.0 1.2 fusion.20
  132.3 1.9 %collective-permute-start.7 = (f32[256,128]{1,0:T(8,128)S(1)}, f32[256,128]{1,0:T(8,128)S(1)}, u32[]{:S(2)}, u32[]{:S(2)}) collective-permute-start(f32[256,128]{1,0:T(8,128)S(1)} %get-tuple-element.35), channel_id=1, source_target_pairs={{0,16},{16,0},{1,17},{17,1},{2,18},{18,2},{3,19},{19,3},{4,20},{20... | collective-permute-start | bytes 393224 | tf_op jit(solution)/shard_map/ppermute | solution.py:219
  134.2 1.2 fusion.10
  136.2 1.9 %broadcast_select_fusion = (f32[4,64,128]{2,1,0:T(8,128)}, f32[4,64,128]{2,1,0:T(8,128)}) fusion(f32[4,64,128]{2,1,0:T(8,128)S(1)} %bitcast.105, pred[]{:T(512)S(6)} %eq.21, f32[4,64,128]{2,1,0:T(8,128)} %bitcast.104, f32[4,64,128]{2,1,0:T(8,128)} %bitcast.103, f32[4]{0:T(128)S(1)} %get-tuple-element.15, f32[4,64,128]{2,1,0:T(8,128)} %bitcast.107, ...), kind=kLoop, calls=%fused_computation.36 | loop fusion | flops 294912 | bytes 1048641 | tf_op jit(solution)/shard_map/jit(_where)/select_n | solution.py:94
  138.1 0.8 slice.166
  143.7 0.8 mul.200
  144.6 2.0 %fusion = f32[256,128]{1,0:T(8,128)S(1)} fusion(f32[16,264,128]{2,1,0:T(8,128)} %bitcast.79, f32[16,256]{1,0:T(8,128)S(1)} %mul.200), kind=kLoop, calls=%fused_computation.1 | loop fusion | flops 1015808 | bytes 2244608 | tf_op jit(solution)/shard_map/reduce_sum | solution.py:155
  147.0 2.3 %collective-permute-start.1 = (f32[256,128]{1,0:T(8,128)S(1)}, f32[256,128]{1,0:T(8,128)S(1)}, u32[]{:S(2)}, u32[]{:S(2)}) collective-permute-start(f32[256,128]{1,0:T(8,128)S(1)} %pad_maximum_fusion.7), channel_id=1, source_target_pairs={{0,16},{16,0},{1,17},{17,1},{2,18},{18,2},{3,19},{19,3},{4,20},{20... | collective-permute-start | bytes 393224 | tf_op jit(solution)/shard_map/ppermute | solution.py:162
  149.3 0.9 collective-permute-done.1
  150.5 0.8 convolution_add_fusion
  151.5 1.2 convolution_add_fusion.1
  152.8 1.0 copy.38
  153.8 10.9 %all-to-all-start = ((f32[16,32,256]{2,1,0:T(8,128)}), f32[16,32,256]{2,1,0:T(8,128)S(1)}, u32[]{:S(2)}, u32[]{:S(2)}) async-start(f32[16,32,256]{2,1,0:T(8,128)} %bitcast.77), calls=%async_computation | async-start | bytes 1048576 | tf_op jit(solution)/shard_map/all_to_all | solution.py:299
  164.7 3.3 %fusion.3 = f32[512,512]{1,0:T(8,128)} fusion(f32[512,512]{1,0:T(8,128)S(1)} %copy.29, f32[512,512]{1,0:T(8,128)} %get-tuple-element.7, f32[512,512]{1,0:T(8,128)S(1)} %copy-done.1, f32[512,128]{1,0:T(8,128)S(1)} %bitcast.76, f32[512,128]{1,0:T(8,128)S(1)} %copy-done), kind=kOutput, calls=%fused_computation.5 | convolution fusion | flops 403439616 | bytes 4718592 | tf_op jit(solution)/shard_map/tn,kn->tk/dot_general | solution.py:294
  168.0 8.8 %all-to-all-done = f32[16,32,256]{2,1,0:T(8,128)S(1)} async-done(((f32[16,32,256]{2,1,0:T(8,128)}), f32[16,32,256]{2,1,0:T(8,128)S(1)}, u32[]{:S(2)}, u32[]{:S(2)}) %all-to-all-start) | async-done | bytes 524320 | tf_op jit(solution)/shard_map/all_to_all | solution.py:299
  (147 shorter events, 27.5 us)
Async XLA Ops:
  7.2 12.1 %copy-start = (f32[512,128]{1,0:T(8,128)S(1)}, f32[512,128]{1,0:T(8,128)}, u32[]{:S(2)}) copy-start(f32[512,128]{1,0:T(8,128)} %param.8) | copy-start | bytes 786436
  7.2 130.9 %all-gather.3.cloned.1.call-start = ((), (), s32[]{:S(2)}) async-start(), calls=%async_computation.1 | async-start | bytes 2297856 | tf_op jit(solution)/shard_map/all_gather | solution.py:144
  10.9 0.8 copy-start.23
  11.3 12.7 %copy-start.30 = (f32[4]{0:T(128)}, f32[4]{0:T(128)S(1)}, u32[]{:S(2)}) copy-start(f32[4]{0:T(128)S(1)} %get-tuple-element.49) | copy-start | bytes 52
  11.8 1.5 copy-start.2
  13.6 1.0 copy-start.7
  15.6 0.8 copy-start.5
  15.6 17.6 %copy-start.8 = (f32[256,128]{1,0:T(8,128)}, f32[256,128]{1,0:T(8,128)S(1)}, u32[]{:S(2)}) copy-start(f32[256,128]{1,0:T(8,128)S(1)} %slice.157) | copy-start | bytes 393220
  21.0 0.7 copy-start.6
  27.6 3.8 %collective-permute-start = (f32[528,128]{1,0:T(8,128)}, f32[528,128]{1,0:T(8,128)}, u32[]{:S(2)}, u32[]{:S(2)}) collective-permute-start(f32[528,128]{1,0:T(8,128)} %constant_dynamic-update-slice_fusion), channel_id=1, source_target_pairs={{0,16},{16,0},{1,17},{17,1},{2,18},{18,2},{3,19},{19,3},{4,20},{20... | collective-permute-start | bytes 811016 | tf_op jit(solution)/shard_map/ppermute | solution.py:237
  32.3 2.5 %copy-start.25 = (f32[2]{0:T(128)}, f32[2]{0:T(128)S(1)}, u32[]{:S(2)}) copy-start(f32[2]{0:T(128)S(1)} %get-tuple-element.12) | copy-start | bytes 28
  32.3 2.5 %copy-start.27 = (f32[2]{0:T(128)}, f32[2]{0:T(128)S(1)}, u32[]{:S(2)}) copy-start(f32[2]{0:T(128)S(1)} %get-tuple-element.13) | copy-start | bytes 28
  33.2 0.6 copy-start.15
  33.2 1.5 copy-start.17
  39.3 9.9 %collective-permute-start.2 = (f32[264,128]{1,0:T(8,128)}, f32[264,128]{1,0:T(8,128)S(1)}, u32[]{:S(2)}, u32[]{:S(2)}) collective-permute-start(f32[264,128]{1,0:T(8,128)} %pad_maximum_fusion.3), channel_id=1, source_target_pairs={{0,32},{32,64},{48,16},{64,96},{80,48},{96,128},{112,80},{128,160}... | collective-permute-start | bytes 405512 | tf_op jit(solution)/shard_map/ppermute | solution.py:208
  49.3 26.6 %copy-start.24 = (f32[264,128]{1,0:T(8,128)}, f32[264,128]{1,0:T(8,128)S(1)}, u32[]{:S(2)}) copy-start(f32[264,128]{1,0:T(8,128)S(1)} %collective-permute-done.2) | copy-start | bytes 405508
  49.3 26.6 %collective-permute-start.3 = (f32[264,128]{1,0:T(8,128)S(1)}, f32[264,128]{1,0:T(8,128)}, u32[]{:S(2)}, u32[]{:S(2)}) collective-permute-start(f32[264,128]{1,0:T(8,128)S(1)} %collective-permute-done.2), channel_id=1, source_target_pairs={{0,32},{32,64},{48,16},{64,96},{80,48},{96,128},{112,80},{128,160}... | collective-permute-start | bytes 405512 | tf_op jit(solution)/shard_map/ppermute | solution.py:208
  79.4 11.0 %collective-permute-start.4 = (f32[264,128]{1,0:T(8,128)}, f32[264,128]{1,0:T(8,128)}, u32[]{:S(2)}, u32[]{:S(2)}) collective-permute-start(f32[264,128]{1,0:T(8,128)} %pad_maximum_fusion.4), channel_id=1, source_target_pairs={{0,64},{32,96},{64,128},{80,16},{96,160},{112,48},{128,192},{144,8... | collective-permute-start | bytes 405512 | tf_op jit(solution)/shard_map/ppermute | solution.py:208
  89.4 0.6 copy-start.29
  92.8 0.6 copy-start.11
  93.5 15.4 %collective-permute-start.5 = (f32[264,128]{1,0:T(8,128)S(1)}, f32[264,128]{1,0:T(8,128)}, u32[]{:S(2)}, u32[]{:S(2)}) collective-permute-start(f32[264,128]{1,0:T(8,128)S(1)} %pad_maximum_fusion.5), channel_id=1, source_target_pairs={{0,128},{32,160},{64,192},{96,224},{128,256},{144,16},{160,288},{1... | collective-permute-start | bytes 405512 | tf_op jit(solution)/shard_map/ppermute | solution.py:208
  111.5 0.6 copy-start.12
  112.9 18.1 %collective-permute-start.6 = (f32[264,128]{1,0:T(8,128)}, f32[264,128]{1,0:T(8,128)}, u32[]{:S(2)}, u32[]{:S(2)}) collective-permute-start(f32[264,128]{1,0:T(8,128)} %pad_maximum_fusion.6), channel_id=1, source_target_pairs={{0,256},{32,288},{64,320},{96,352},{128,384},{160,416},{192,448},{... | collective-permute-start | bytes 405512 | tf_op jit(solution)/shard_map/ppermute | solution.py:208
  130.6 16.2 %copy-start.9 = (f32[256,128]{1,0:T(8,128)S(1)}, f32[256,128]{1,0:T(8,128)}, u32[]{:S(2)}) copy-start(f32[256,128]{1,0:T(8,128)} %copy-done.8) | copy-start | bytes 393220
  132.3 3.2 %collective-permute-start.7 = (f32[256,128]{1,0:T(8,128)S(1)}, f32[256,128]{1,0:T(8,128)S(1)}, u32[]{:S(2)}, u32[]{:S(2)}) collective-permute-start(f32[256,128]{1,0:T(8,128)S(1)} %get-tuple-element.35), channel_id=1, source_target_pairs={{0,16},{16,0},{1,17},{17,1},{2,18},{18,2},{3,19},{19,3},{4,20},{20... | collective-permute-start | bytes 393224 | tf_op jit(solution)/shard_map/ppermute | solution.py:219
  135.5 0.6 copy-start.19
  144.6 2.2 %copy-start.18 = (f32[128,128]{1,0:T(8,128)S(1)}, f32[128,128]{1,0:T(8,128)}, u32[]{:S(2)}) copy-start(f32[128,128]{1,0:T(8,128)} %copy-done.17) | copy-start | bytes 196612
  144.6 2.2 %copy-start.28 = (f32[2]{0:T(128)S(1)}, f32[2]{0:T(128)}, u32[]{:S(2)}) copy-start(f32[2]{0:T(128)} %copy-done.27) | copy-start | bytes 28
  144.6 2.3 %copy-start.10 = (f32[256,128]{1,0:T(8,128)S(1)}, f32[256,128]{1,0:T(8,128)}, u32[]{:S(2)}) copy-start(f32[256,128]{1,0:T(8,128)} %slice.156) | copy-start | bytes 393220
  144.6 2.3 %copy-start.16 = (f32[128,128]{1,0:T(8,128)S(1)}, f32[128,128]{1,0:T(8,128)}, u32[]{:S(2)}) copy-start(f32[128,128]{1,0:T(8,128)} %copy-done.15) | copy-start | bytes 196612
  144.6 2.3 %copy-start.26 = (f32[2]{0:T(128)S(1)}, f32[2]{0:T(128)}, u32[]{:S(2)}) copy-start(f32[2]{0:T(128)} %copy-done.25) | copy-start | bytes 28
  144.6 4.7 %copy-start.20 = (f32[256,128]{1,0:T(8,128)S(1)}, f32[256,128]{1,0:T(8,128)}, u32[]{:S(2)}) copy-start(f32[256,128]{1,0:T(8,128)} %copy-done.19) | copy-start | bytes 393220
  144.6 4.7 %copy-start.21 = (f32[4,64,128]{2,1,0:T(8,128)S(1)}, f32[4,64,128]{2,1,0:T(8,128)}, u32[]{:S(2)}) copy-start(f32[4,64,128]{2,1,0:T(8,128)} %get-tuple-element.23) | copy-start | bytes 393220
  144.6 5.9 %copy-start.22 = (f32[4,64,128]{2,1,0:T(8,128)S(1)}, f32[4,64,128]{2,1,0:T(8,128)}, u32[]{:S(2)}) copy-start(f32[4,64,128]{2,1,0:T(8,128)} %get-tuple-element.22) | copy-start | bytes 393220
  146.7 3.9 %copy-start.13 = (f32[512,128]{0,1:T(8,128)S(1)}, f32[512,128]{0,1:T(8,128)}, u32[]{:S(2)}) copy-start(f32[512,128]{0,1:T(8,128)} %fusion.31) | copy-start | bytes 786436
  147.0 3.3 %collective-permute-start.1 = (f32[256,128]{1,0:T(8,128)S(1)}, f32[256,128]{1,0:T(8,128)S(1)}, u32[]{:S(2)}, u32[]{:S(2)}) collective-permute-start(f32[256,128]{1,0:T(8,128)S(1)} %pad_maximum_fusion.7), channel_id=1, source_target_pairs={{0,16},{16,0},{1,17},{17,1},{2,18},{18,2},{3,19},{19,3},{4,20},{20... | collective-permute-start | bytes 393224 | tf_op jit(solution)/shard_map/ppermute | solution.py:162
  150.3 1.2 copy-start.14
  151.4 1.3 copy-start.3
  151.4 13.2 %copy-start.1 = (f32[512,512]{1,0:T(8,128)S(1)}, f32[512,512]{1,0:T(8,128)}, u32[]{:S(2)}) copy-start(f32[512,512]{1,0:T(8,128)} %copy.36) | copy-start | bytes 3145732
  152.7 11.9 %copy-start.4 = (f32[8,64,128]{2,1,0:T(8,128)S(1)}, f32[8,64,128]{2,1,0:T(8,128)}, u32[]{:S(2)}) copy-start(f32[8,64,128]{2,1,0:T(8,128)} %copy-done.3) | copy-start | bytes 786436
  153.8 23.0 %all-to-all-start = ((f32[16,32,256]{2,1,0:T(8,128)}), f32[16,32,256]{2,1,0:T(8,128)S(1)}, u32[]{:S(2)}, u32[]{:S(2)}) async-start(f32[16,32,256]{2,1,0:T(8,128)} %bitcast.77), calls=%async_computation | async-start | bytes 1048576 | tf_op jit(solution)/shard_map/all_to_all | solution.py:299
Sparse Core Ops, SparseCore 0:
  43.3 82.7 all-gather.2

commit v7 on v5

--- a/solution.py
+++ b/solution.py
@@ -32,23 +32,27 @@
 
     tok = scores_t_ref.shape[0]
     width = in_ref.shape[1] // HEADS_PER_STEP
-    rows = lax.broadcasted_iota(jnp.int32, (tok, tok), 0)
-    cols = lax.broadcasted_iota(jnp.int32, (tok, tok), 1)
-    later = cols >= rows
-    scores_t = scores_t_ref[...]
+    piece = 128
     for k in range(HEADS_PER_STEP):
-        gap = cum_row_ref[k] - cum_col_ref[k]
-        decay_t = jnp.where(later, jnp.exp(jnp.where(later, gap, 0.0)), 0.0)
-        own_in = in_ref[:, k * width:(k + 1) * width]
-        own_grad = grad_ref[:, k * width:(k + 1) * width]
-        flow_ref[:, k * width:(k + 1) * width] = jnp.dot(
-            scores_t * decay_t, own_grad, precision=highest, preferred_element_type=jnp.float32
-        )
-        pair_t = lax.dot_general(
-            own_in, own_grad, (((1,), (1,)), ((), ())), precision=highest,
-            preferred_element_type=jnp.float32,
-        )
-        acc_ref[...] += pair_t * decay_t
+        lanes = slice(k * width, (k + 1) * width)
+        for first in range(0, tok, piece):
+            span = tok - first
+            rows = lax.broadcasted_iota(jnp.int32, (piece, span), 0)
+            cols = lax.broadcasted_iota(jnp.int32, (piece, span), 1)
+            later = cols >= rows
+            gap = cum_row_ref[k, :, first:] - cum_col_ref[k, first:first + piece, :]
+            decay_t = jnp.where(later, jnp.exp(jnp.where(later, gap, 0.0)), 0.0)
+            own_in = in_ref[first:first + piece, lanes]
+            own_grad = grad_ref[first:, lanes]
+            flow_ref[first:first + piece, lanes] = jnp.dot(
+                scores_t_ref[first:first + piece, first:] * decay_t, own_grad,
+                precision=highest, preferred_element_type=jnp.float32,
+            )
+            pair_t = lax.dot_general(
+                own_in, own_grad, (((1,), (1,)), ((), ())), precision=highest,
+                preferred_element_type=jnp.float32,
+            )
+            acc_ref[first:first + piece, first:] += pair_t * decay_t
 
 
 def block_terms(cumul, scores_t, scaled_in, out_grad):

time: 157 us -> 153 us (0.975)
  Pallas kernels: 17.8 us -> 14.2 us
    pallas_call x1, Pallas kernels: 17.8 us -> 14.2 us  [block_terms(): pl.pallas_call(block_kernel, grid=(head_count // HEADS_PER_STEP,), in_spe...]
  transfers between devices with their start and end apart: 8 -> 8, of which waited for: 6 -> 6; matrix products, arithmetic and copies ran while one was open for 9% -> 9% of each run, Pallas kernels for 11% -> 9%
where the time goes in v7:
time: 153 us; the launch traced here: 152 us
  starting transfers between devices  47.7 us (31%)
  waiting for transfers between devices  41.2 us (27%)
  matrix products  17.6 us (12%)
  local copies, waits for them, and re-layouts  15.9 us (10%)
  other arithmetic  14.8 us (10%)
  Pallas kernels  14.2 us (9%)
    ppermute x5, waiting for transfers between devices, move(): return lax.ppermute(value, both, pairs)  32.3 us
    ppermute x1, starting transfers between devices, chip_scans(): back = lax.ppermute(joined.reshape(rows, state_width), 'core', swap)  24.9 us
    pallas_call x1, Pallas kernels, block_terms(): pl.pallas_call(block_kernel, grid=(head_count // HEADS_PER_STEP,), in_spe...  14.2 us
    ppermute x1, starting transfers between devices, chip_scans(): incoming = lax.ppermute(outgoing, 'core', swap)  8.79 us
    all_to_all x1, waiting for transfers between devices, per_device(): spread = lax.all_to_all(both, 'head', 0, 0, tiled=True)  7.79 us
    all_to_all x1, starting transfers between devices, per_device(): spread = lax.all_to_all(both, 'head', 0, 0, tiled=True)  7.61 us
    ppermute x5, starting transfers between devices, move(): return lax.ppermute(value, both, pairs)  6.42 us
    unnamed x41, local copies, waits for them, and re-layouts  6.38 us
  transfers between devices with their start and end apart: 8, of which 6 were waited for; matrix products, arithmetic and copies ran while one was open for 9% of the time, Pallas kernels for 9%

profile of v7, /device:TPU:1, one launch (start us, length us, event | category | flops | bytes accessed | tf_op | source)
XLA Modules:
  0.0 152.4 jit_solution(10532873789099940944)
XLA Ops:
  0.7 0.8 select_reduce_fusion
  2.1 1.1 reduce-window.6
  3.8 1.1 broadcast_in_dim.35
  4.9 1.6 %copy.30 = f32[512,512]{1,0:T(8,128)S(1)} copy(f32[512,512]{0,1:T(8,128)} %bitcast.42) | data formatting | bytes 2097152 | tf_op jit(solution)/shard_map/reshape | solution.py:23
  6.5 1.3 copy.27
  7.8 2.6 %fusion.13 = (f32[512,512]{1,0:T(8,128)S(1)}, f32[512,512]{1,0:T(8,128)}) fusion(f32[512,512]{1,0:T(8,128)S(1)} %copy.30, f32[512,512]{1,0:T(8,128)} %param.7, f32[512,512]{1,0:T(8,128)S(1)} %copy.25), kind=kLoop, calls=%fused_computation.48 | loop fusion | flops 524288 | bytes 5242880 | tf_op jit(solution)/shard_map/mul | solution.py:170
  10.4 2.5 %fusion.16 = f32[512,128]{1,0:T(8,128)} fusion(f32[512,512]{1,0:T(8,128)S(1)} %get-tuple-element.17, f32[512,128]{1,0:T(8,128)S(1)} %copy-done), kind=kOutput, calls=%fused_computation.51 | convolution fusion | flops 402653184 | bytes 1572864 | tf_op jit(solution)/shard_map/tk,tn->kn/dot_general | solution.py:172
  12.9 1.4 bitcast_multiply_fusion
  14.3 1.0 copy-done.1
  15.3 1.7 %broadcast_select_fusion.2 = (f32[512,128]{1,0:T(8,128)S(1)}, f32[512,128]{1,0:T(8,128)}) fusion(f32[512,128]{1,0:T(8,128)S(1)} %copy-done.6, pred[]{:T(512)S(6)} %eq.19, f32[512,512]{0,1:T(8,128)S(1)} %bitcast_multiply_fusion, f32[512,128]{1,0:T(8,128)S(1)} %copy-done.12), kind=kOutput, calls=%fused_computation.29 | convolution fusion | flops 402718720 | bytes 2097153 | tf_op jit(solution)/shard_map/tk,tn->kn/dot_general | solution.py:173
  17.1 8.8 %collective-permute-start = (f32[520,128]{1,0:T(8,128)S(1)}, f32[520,128]{1,0:T(8,128)S(1)}, u32[]{:S(2)}, u32[]{:S(2)}) collective-permute-start(f32[520,128]{1,0:T(8,128)S(1)} %pad_maximum_fusion.1), channel_id=1, source_target_pairs={{0,16},{16,0},{1,17},{17,1},{2,18},{18,2},{3,19},{19,3},{4,20},{20... | collective-permute-start | bytes 798728 | tf_op jit(solution)/shard_map/ppermute | solution.py:114
  25.9 1.1 collective-permute-done
  27.1 0.7 copy-done.17
  28.1 1.2 slice_add_fusion.1
  29.4 1.3 collective-permute-start.1
  30.7 5.9 %collective-permute-done.1 = f32[520,128]{1,0:T(8,128)S(1)} collective-permute-done((f32[520,128]{1,0:T(8,128)S(1)}, f32[520,128]{1,0:T(8,128)S(1)}, u32[]{:S(2)}, u32[]{:S(2)}) %collective-permute-start.1) | collective-permute-done | bytes 266272 | tf_op jit(solution)/shard_map/ppermute | solution.py:135
  36.6 1.3 collective-permute-start.2
  37.9 5.9 %collective-permute-done.2 = f32[520,128]{1,0:T(8,128)S(1)} collective-permute-done((f32[520,128]{1,0:T(8,128)S(1)}, f32[520,128]{1,0:T(8,128)S(1)}, u32[]{:S(2)}, u32[]{:S(2)}) %collective-permute-start.2) | collective-permute-done | bytes 266272 | tf_op jit(solution)/shard_map/ppermute | solution.py:135
  44.6 1.2 slice_add_fusion
  45.7 0.7 copy-done.10
  46.6 1.3 collective-permute-start.3
  47.9 8.5 %collective-permute-done.3 = f32[520,128]{1,0:T(8,128)S(1)} collective-permute-done((f32[520,128]{1,0:T(8,128)S(1)}, f32[520,128]{1,0:T(8,128)S(1)}, u32[]{:S(2)}, u32[]{:S(2)}) %collective-permute-start.3) | collective-permute-done | bytes 266272 | tf_op jit(solution)/shard_map/ppermute | solution.py:135
  56.4 0.7 copy-done.15
  57.4 1.2 fusion.5
  58.6 0.7 copy-done.9
  59.3 0.8 pad_maximum_fusion.4
  60.1 1.3 collective-permute-start.4
  61.5 12.0 %collective-permute-done.4 = f32[520,128]{1,0:T(8,128)} collective-permute-done((f32[520,128]{1,0:T(8,128)}, f32[520,128]{1,0:T(8,128)}, u32[]{:S(2)}, u32[]{:S(2)}) %collective-permute-start.4) | collective-permute-done | bytes 266272 | tf_op jit(solution)/shard_map/ppermute | solution.py:135
  73.5 0.8 slice_reduce_fusion.1
  74.3 1.2 fusion.4
  75.5 0.7 copy-done.11
  76.2 0.9 pad_maximum_fusion.5
  77.1 1.3 collective-permute-start.5
  78.4 2.9 %fusion.15.scores_t_ref = f32[512,512]{1,0:T(8,128)} fusion(f32[512,128]{1,0:T(8,128)S(1)} %copy-done, f32[512,128]{1,0:T(8,128)} %param.9), kind=kOutput, calls=%fused_computation.50 | convolution fusion | flops 402653184 | bytes 1572864 | tf_op jit(solution)/shard_map/sn,tn->st/dot_general | solution.py:180
  81.3 0.6 copy.24
  81.9 2.0 %copy.26.cum_col_ref = f32[8,512,1]{2,1,0:T(8,128)} copy(f32[8,512,1]{1,0,2:T(8,128)S(1)} %bitcast.47) | data formatting | bytes 32768 | tf_op jit(solution)/shard_map/reduce_window_sum
  84.0 14.2 %shard_map.94 = (f32[512,512]{1,0:T(8,128)}, f32[512,512]{1,0:T(8,128)}) custom-call(f32[8,1,512]{2,1,0:T(1,128)} %bitcast.49, f32[8,512,1]{2,1,0:T(8,128)} %copy.26.cum_col_ref, f32[512,512]{1,0:T(8,128)} %fusion.15.scores_t_ref, f32[512,512]{1,0:T(8,128)} %get-tuple-element.18.in_ref, f32[512,512]{1,0:T(8,128)} %grad_ref.1), custom_call_target="tpu_custom_call" | custom-call | tf_op jit(solution)/shard_map/pallas_call | solution.py:64
  98.2 2.7 %fusion.18 = f32[512,128]{0,1:T(8,128)} fusion(f32[512,512]{1,0:T(8,128)} %get-tuple-element.6, f32[512,128]{1,0:T(8,128)S(1)} %copy-done), kind=kOutput, calls=%fused_computation.53 | convolution fusion | flops 402653184 | bytes 1572864 | tf_op jit(solution)/shard_map/st,sn->tn/dot_general | solution.py:183
  101.1 1.4 multiply_add_fusion
  102.5 24.9 %collective-permute-start.6 = (f32[512,128]{1,0:T(8,128)S(1)}, f32[512,128]{1,0:T(8,128)S(1)}, u32[]{:S(2)}, u32[]{:S(2)}) collective-permute-start(f32[512,128]{1,0:T(8,128)S(1)} %get-tuple-element.11), channel_id=1, source_target_pairs={{0,16},{16,0},{1,17},{17,1},{2,18},{18,2},{3,19},{19,3},{4,20},{20... | collective-permute-start | bytes 786440 | tf_op jit(solution)/shard_map/ppermute | solution.py:146
  127.4 2.5 %fusion.17 = f32[512,128]{0,1:T(8,128)S(1)} fusion(f32[512,512]{1,0:T(8,128)} %get-tuple-element.6, f32[512,128]{1,0:T(8,128)} %param.9), kind=kOutput, calls=%fused_computation.52 | convolution fusion | flops 402653184 | bytes 1572864 | tf_op jit(solution)/shard_map/dot_general | solution.py:182
  129.9 0.8 convolution_add_fusion
  130.7 1.2 convolution_add_fusion.1
  132.0 1.0 copy.32
  133.0 7.6 %all-to-all-start = ((f32[16,32,256]{2,1,0:T(8,128)}), f32[16,32,256]{2,1,0:T(8,128)S(1)}, u32[]{:S(2)}, u32[]{:S(2)}) async-start(f32[16,32,256]{2,1,0:T(8,128)} %bitcast.44), calls=%async_computation | async-start | bytes 1048576 | tf_op jit(solution)/shard_map/all_to_all | solution.py:194
  140.6 3.3 %fusion.2 = f32[512,512]{1,0:T(8,128)} fusion(f32[512,512]{1,0:T(8,128)S(1)} %copy.25, f32[512,512]{1,0:T(8,128)} %get-tuple-element.5, f32[512,512]{1,0:T(8,128)S(1)} %copy.30, f32[512,128]{1,0:T(8,128)S(1)} %copy-done, f32[512,128]{1,0:T(8,128)S(1)} %copy-done.8, f32[512,128]{1,0:T(8,128)S(1)} %copy-done.5, pred[]{:T(512)S(6)} %eq.19), kind=kOutput, calls=%fused_computation.3 | convolution fusion | flops 403505152 | bytes 4980737 | tf_op jit(solution)/shard_map/tn,kn->tk/dot_general | solution.py:189
  143.9 7.8 %all-to-all-done = f32[16,32,256]{2,1,0:T(8,128)S(1)} async-done(((f32[16,32,256]{2,1,0:T(8,128)}), f32[16,32,256]{2,1,0:T(8,128)S(1)}, u32[]{:S(2)}, u32[]{:S(2)}) %all-to-all-start) | async-done | bytes 524320 | tf_op jit(solution)/shard_map/all_to_all | solution.py:194
  151.7 0.6 fusion.14
  (76 shorter events, 3.5 us)
Async XLA Ops:
  0.6 9.7 %copy-start = (f32[512,128]{1,0:T(8,128)S(1)}, f32[512,128]{1,0:T(8,128)}, u32[]{:S(2)}) copy-start(f32[512,128]{1,0:T(8,128)} %param.8) | copy-start | bytes 786436
  0.6 1.4 copy-start.18
  0.7 1.4 copy-start.19
  2.0 4.5 %copy-start.3 = (f32[512,512]{1,0:T(8,128)S(1)}, f32[512,512]{1,0:T(8,128)}, u32[]{:S(2)}) copy-start(f32[512,512]{1,0:T(8,128)} %grad_ref.1) | copy-start | bytes 3145732
  12.9 2.4 %copy-start.6 = (f32[512,128]{1,0:T(8,128)S(1)}, f32[512,128]{1,0:T(8,128)}, u32[]{:S(2)}) copy-start(f32[512,128]{1,0:T(8,128)} %fusion.16) | copy-start | bytes 786436
  12.9 2.4 %copy-start.12 = (f32[512,128]{1,0:T(8,128)S(1)}, f32[512,128]{1,0:T(8,128)}, u32[]{:S(2)}) copy-start(f32[512,128]{1,0:T(8,128)} %param.9) | copy-start | bytes 786436
  14.3 1.0 copy-start.1
  17.1 9.9 %collective-permute-start = (f32[520,128]{1,0:T(8,128)S(1)}, f32[520,128]{1,0:T(8,128)S(1)}, u32[]{:S(2)}, u32[]{:S(2)}) collective-permute-start(f32[520,128]{1,0:T(8,128)S(1)} %pad_maximum_fusion.1), channel_id=1, source_target_pairs={{0,16},{16,0},{1,17},{17,1},{2,18},{18,2},{3,19},{19,3},{4,20},{20... | collective-permute-start | bytes 798728 | tf_op jit(solution)/shard_map/ppermute | solution.py:114
  27.1 0.7 copy-start.17
  29.4 7.2 %collective-permute-start.1 = (f32[520,128]{1,0:T(8,128)S(1)}, f32[520,128]{1,0:T(8,128)S(1)}, u32[]{:S(2)}, u32[]{:S(2)}) collective-permute-start(f32[520,128]{1,0:T(8,128)S(1)} %pad_maximum_fusion.2), channel_id=1, source_target_pairs={{0,32},{32,64},{48,16},{64,96},{80,48},{96,128},{112,80},{128,160}... | collective-permute-start | bytes 798728 | tf_op jit(solution)/shard_map/ppermute | solution.py:135
  36.6 7.2 %copy-start.14 = (f32[520,128]{1,0:T(8,128)}, f32[520,128]{1,0:T(8,128)S(1)}, u32[]{:S(2)}) copy-start(f32[520,128]{1,0:T(8,128)S(1)} %collective-permute-done.1) | copy-start | bytes 798724
  36.6 7.1 %collective-permute-start.2 = (f32[520,128]{1,0:T(8,128)S(1)}, f32[520,128]{1,0:T(8,128)S(1)}, u32[]{:S(2)}, u32[]{:S(2)}) collective-permute-start(f32[520,128]{1,0:T(8,128)S(1)} %collective-permute-done.1), channel_id=1, source_target_pairs={{0,32},{32,64},{48,16},{64,96},{80,48},{96,128},{112,80},{128,160}... | collective-permute-start | bytes 798728 | tf_op jit(solution)/shard_map/ppermute | solution.py:135
  43.7 0.7 copy-start.16
  45.7 0.7 copy-start.10
  46.6 9.8 %collective-permute-start.3 = (f32[520,128]{1,0:T(8,128)S(1)}, f32[520,128]{1,0:T(8,128)S(1)}, u32[]{:S(2)}, u32[]{:S(2)}) collective-permute-start(f32[520,128]{1,0:T(8,128)S(1)} %pad_maximum_fusion.3), channel_id=1, source_target_pairs={{0,64},{32,96},{64,128},{80,16},{96,160},{112,48},{128,192},{144,8... | collective-permute-start | bytes 798728 | tf_op jit(solution)/shard_map/ppermute | solution.py:135
  56.4 0.7 copy-start.15
  58.6 0.7 copy-start.9
  60.1 13.4 %collective-permute-start.4 = (f32[520,128]{1,0:T(8,128)}, f32[520,128]{1,0:T(8,128)}, u32[]{:S(2)}, u32[]{:S(2)}) collective-permute-start(f32[520,128]{1,0:T(8,128)} %pad_maximum_fusion.4), channel_id=1, source_target_pairs={{0,128},{32,160},{64,192},{96,224},{128,256},{144,16},{160,288},{1... | collective-permute-start | bytes 798728 | tf_op jit(solution)/shard_map/ppermute | solution.py:135
  75.5 0.7 copy-start.11
  77.1 24.0 %collective-permute-start.5 = (f32[520,128]{1,0:T(8,128)}, f32[520,128]{1,0:T(8,128)}, u32[]{:S(2)}, u32[]{:S(2)}) collective-permute-start(f32[520,128]{1,0:T(8,128)} %pad_maximum_fusion.5), channel_id=1, source_target_pairs={{0,256},{32,288},{64,320},{96,352},{128,384},{160,416},{192,448},{... | collective-permute-start | bytes 798728 | tf_op jit(solution)/shard_map/ppermute | solution.py:135
  101.1 28.8 %copy-start.2 = (f32[512,512]{0,1:T(8,128)S(1)}, f32[512,512]{0,1:T(8,128)}, u32[]{:S(2)}) copy-start(f32[512,512]{0,1:T(8,128)} %copy-done.1) | copy-start | bytes 3145732
  101.1 28.8 %copy-start.13 = (f32[512,128]{0,1:T(8,128)S(1)}, f32[512,128]{0,1:T(8,128)}, u32[]{:S(2)}) copy-start(f32[512,128]{0,1:T(8,128)} %fusion.18) | copy-start | bytes 786436
  102.5 29.4 %copy-start.4 = (f32[512,128]{1,0:T(8,128)}, f32[512,128]{1,0:T(8,128)S(1)}, u32[]{:S(2)}) copy-start(f32[512,128]{1,0:T(8,128)S(1)} %get-tuple-element.12) | copy-start | bytes 786436
  102.5 27.3 %collective-permute-start.6 = (f32[512,128]{1,0:T(8,128)S(1)}, f32[512,128]{1,0:T(8,128)S(1)}, u32[]{:S(2)}, u32[]{:S(2)}) collective-permute-start(f32[512,128]{1,0:T(8,128)S(1)} %get-tuple-element.11), channel_id=1, source_target_pairs={{0,16},{16,0},{1,17},{17,1},{2,18},{18,2},{3,19},{19,3},{4,20},{20... | collective-permute-start | bytes 786440 | tf_op jit(solution)/shard_map/ppermute | solution.py:146
  129.9 2.1 %copy-start.7 = (f32[512,128]{1,0:T(8,128)}, f32[512,128]{1,0:T(8,128)S(1)}, u32[]{:S(2)}) copy-start(f32[512,128]{1,0:T(8,128)S(1)} %collective-permute-done.6) | copy-start | bytes 786436
  132.0 8.6 %copy-start.5 = (f32[512,128]{1,0:T(8,128)S(1)}, f32[512,128]{1,0:T(8,128)}, u32[]{:S(2)}) copy-start(f32[512,128]{1,0:T(8,128)} %copy-done.4) | copy-start | bytes 786436
  132.0 8.6 %copy-start.8 = (f32[512,128]{1,0:T(8,128)S(1)}, f32[512,128]{1,0:T(8,128)}, u32[]{:S(2)}) copy-start(f32[512,128]{1,0:T(8,128)} %copy-done.7) | copy-start | bytes 786436
  133.0 18.7 %all-to-all-start = ((f32[16,32,256]{2,1,0:T(8,128)}), f32[16,32,256]{2,1,0:T(8,128)S(1)}, u32[]{:S(2)}, u32[]{:S(2)}) async-start(f32[16,32,256]{2,1,0:T(8,128)} %bitcast.44), calls=%async_computation | async-start | bytes 1048576 | tf_op jit(solution)/shard_map/all_to_all | solution.py:194

commit v8 on v7

--- a/solution.py
+++ b/solution.py
@@ -23,24 +23,34 @@
     return wide.reshape(tok_count, head_count * head_width)
 
 
-def block_kernel(cum_row_ref, cum_col_ref, scores_t_ref, in_ref, grad_ref, flow_ref, acc_ref):
+def block_kernel(cum_ref, cum_t_ref, proj_in_ref, proj_out_ref, in_ref, grad_ref, flow_ref, acc_ref,
+                 scores_t_ref):
     step = pl.program_id(0)
 
     @pl.when(step == 0)
     def _():
         acc_ref[...] = jnp.zeros_like(acc_ref)
+        scores_t_ref[...] = lax.dot_general(
+            proj_in_ref[...], proj_out_ref[...], (((1,), (1,)), ((), ())), precision=highest,
+            preferred_element_type=jnp.float32,
+        )
 
     tok = scores_t_ref.shape[0]
     width = in_ref.shape[1] // HEADS_PER_STEP
+    head_count = cum_ref.shape[0]
     piece = 128
+    which = lax.broadcasted_iota(jnp.int32, (tok, head_count), 1)
     for k in range(HEADS_PER_STEP):
+        head = step * HEADS_PER_STEP + k
+        cum_row = cum_ref[pl.ds(head, 1), :]
+        cum_col = jnp.sum(jnp.where(which == head, cum_t_ref[...], 0.0), axis=1, keepdims=True)
         lanes = slice(k * width, (k + 1) * width)
         for first in range(0, tok, piece):
             span = tok - first
             rows = lax.broadcasted_iota(jnp.int32, (piece, span), 0)
             cols = lax.broadcasted_iota(jnp.int32, (piece, span), 1)
             later = cols >= rows
-            gap = cum_row_ref[k, :, first:] - cum_col_ref[k, first:first + piece, :]
+            gap = cum_row[:, first:] - cum_col[first:first + piece, :]
             decay_t = jnp.where(later, jnp.exp(jnp.where(later, gap, 0.0)), 0.0)
             own_in = in_ref[first:first + piece, lanes]
             own_grad = grad_ref[first:, lanes]
@@ -55,19 +65,19 @@
             acc_ref[first:first + piece, first:] += pair_t * decay_t
 
 
-def block_terms(cumul, scores_t, scaled_in, out_grad):
+def block_terms(cumul, input_proj, output_mapping, scaled_in, out_grad):
     head_count, tok = cumul.shape
     chan = scaled_in.shape[1]
+    state_width = input_proj.shape[1]
     lanes = chan // head_count * HEADS_PER_STEP
-    cum_row = cumul.reshape(head_count, 1, tok)
-    cum_col = cumul.reshape(head_count, tok, 1)
     return pl.pallas_call(
         block_kernel,
         grid=(head_count // HEADS_PER_STEP,),
         in_specs=[
-            pl.BlockSpec((HEADS_PER_STEP, 1, tok), lambda j: (j, 0, 0)),
-            pl.BlockSpec((HEADS_PER_STEP, tok, 1), lambda j: (j, 0, 0)),
-            pl.BlockSpec((tok, tok), lambda j: (0, 0)),
+            pl.BlockSpec((head_count, tok), lambda j: (0, 0)),
+            pl.BlockSpec((tok, head_count), lambda j: (0, 0)),
+            pl.BlockSpec((tok, state_width), lambda j: (0, 0)),
+            pl.BlockSpec((tok, state_width), lambda j: (0, 0)),
             pl.BlockSpec((tok, lanes), lambda j: (0, j)),
             pl.BlockSpec((tok, lanes), lambda j: (0, j)),
         ],
@@ -79,7 +89,8 @@
             jax.ShapeDtypeStruct((tok, chan), jnp.float32),
             jax.ShapeDtypeStruct((tok, tok), jnp.float32),
         ],
-    )(cum_row, cum_col, scores_t, scaled_in, out_grad)
+        scratch_shapes=[pltpu.VMEM((tok, tok), jnp.float32)],
+    )(cumul, cumul.T, input_proj, output_mapping, scaled_in, out_grad)
 
 
 def pack_total(total, state_width):
@@ -177,8 +188,7 @@
         group_total,
     )
 
-    scores_t = jnp.einsum("sn,tn->st", input_proj, output_mapping, precision=highest)
-    grad_scaled, grad_scores_t = block_terms(cumul, scores_t, scaled_in, out_grad)
+    grad_scaled, grad_scores_t = block_terms(cumul, input_proj, output_mapping, scaled_in, out_grad)
     block_b = jnp.dot(grad_scores_t, output_mapping, precision=highest)
     block_c = jnp.einsum("st,sn->tn", grad_scores_t, input_proj, precision=highest)
 

time: 153 us -> 149 us (0.974)
  waiting for transfers between devices: 41.2 us -> 47.6 us
  local copies, waits for them, and re-layouts: 15.9 us -> 9.74 us
  matrix products: 17.6 us -> 12.6 us
  other arithmetic: 14.8 us -> 17.1 us
  starting transfers between devices: 47.7 us -> 45.5 us
    ppermute x1, starting transfers between devices: 24.9 us -> 14.8 us  [chip_scans(): back = lax.ppermute(joined.reshape(rows, state_width), 'core', swap)]
    all_to_all x1, starting transfers between devices: 7.61 us -> 15.5 us  [per_device(): spread = lax.all_to_all(both, 'head', 0, 0, tiled=True)]
    ppermute x5, waiting for transfers between devices: 32.3 us -> 38.6 us  [move(): return lax.ppermute(value, both, pairs)]
    dot_general x1 -> x0, matrix products: 2.91 us -> none  [per_device(): jnp.einsum('sn,tn->st', input_proj, output_mapping, precision=highest)]
    exp x2 -> x3, other arithmetic: 0.02 us -> 2.07 us  [join(): return jnp.exp(later_total)[:, None, None] * earlier + later]
    unnamed x41, local copies, waits for them, and re-layouts: 6.38 us -> 4.4 us
    another operation x3, local copies, waits for them, and re-layouts: 2.6 us -> 0.84 us
  transfers between devices with their start and end apart: 8 -> 8, of which waited for: 6 -> 7; matrix products, arithmetic and copies ran while one was open for 9% -> 6% of each run, Pallas kernels for 9% -> 10%
where the time goes in v8:
time: 149 us; the launch traced here: 148 us
  waiting for transfers between devices  47.6 us (32%)
  starting transfers between devices  45.5 us (31%)
  other arithmetic  17.1 us (11%)
  Pallas kernels  14.4 us (10%)
  matrix products  12.6 us (8%)
  local copies, waits for them, and re-layouts  9.74 us (7%)
    ppermute x5, waiting for transfers between devices, move(): return lax.ppermute(value, both, pairs)  38.6 us
    all_to_all x1, starting transfers between devices, per_device(): spread = lax.all_to_all(both, 'head', 0, 0, tiled=True)  15.5 us
    ppermute x1, starting transfers between devices, chip_scans(): back = lax.ppermute(joined.reshape(rows, state_width), 'core', swap)  14.8 us
    pallas_call x1, Pallas kernels, block_terms(): pl.pallas_call(block_kernel, grid=(head_count // HEADS_PER_STEP,), in_spe...  14.4 us
    ppermute x1, starting transfers between devices, chip_scans(): incoming = lax.ppermute(outgoing, 'core', swap)  8.79 us
    all_to_all x1, waiting for transfers between devices, per_device(): spread = lax.all_to_all(both, 'head', 0, 0, tiled=True)  7.75 us
    ppermute x5, starting transfers between devices, move(): return lax.ppermute(value, both, pairs)  6.41 us
    add x5, other arithmetic, join(): return jnp.exp(later_total)[:, None, None] * earlier + later  5.52 us
  transfers between devices with their start and end apart: 8, of which 7 were waited for; matrix products, arithmetic and copies ran while one was open for 6% of the time, Pallas kernels for 10%

profile of v8, /device:TPU:1, one launch (start us, length us, event | category | flops | bytes accessed | tf_op | source)
XLA Modules:
  0.0 148.0 jit_solution(348393144444259938)
XLA Ops:
  0.6 0.8 select_reduce_fusion
  1.9 0.3 copy-done.18
  2.3 0.6 copy-done.19
  3.0 1.1 reduce-window.6
  4.6 0.8 exponential_bitcast_fusion
  5.6 0.3 copy.44
  6.0 2.6 %copy.37 = f32[512,512]{0,1:T(8,128)} copy(f32[512,512]{1,0:T(8,128)} %grad_ref.1) | data formatting | bytes 2097152 | tf_op args[6]
  8.7 2.6 %fusion.20 = (f32[512,512]{1,0:T(8,128)S(1)}, f32[512,512]{1,0:T(8,128)}) fusion(f32[512,512]{1,0:T(8,128)S(1)} %copy.44, f32[512,512]{1,0:T(8,128)} %param.7, f32[512,512]{1,0:T(8,128)S(1)} %copy.33), kind=kLoop, calls=%fused_computation.52 | loop fusion | flops 524288 | bytes 5242880 | tf_op jit(solution)/shard_map/mul | solution.py:181
  11.3 1.5 %fusion.22 = f32[512,128]{0,1:T(8,128)} fusion(f32[512,512]{1,0:T(8,128)S(1)} %get-tuple-element.15, f32[512,128]{1,0:T(8,128)S(1)} %copy-done.5), kind=kOutput, calls=%fused_computation.54 | convolution fusion | flops 402653184 | bytes 1572864 | tf_op jit(solution)/shard_map/tk,tn->kn/dot_general | solution.py:183
  12.8 1.4 bitcast_multiply_fusion
  14.2 1.9 %broadcast_select_fusion.2 = (f32[512,128]{0,1:T(8,128)S(1)}, f32[512,128]{0,1:T(8,128)}) fusion(f32[512,128]{0,1:T(8,128)S(1)} %copy-done.4, pred[]{:T(512)S(6)} %eq.19, f32[512,512]{0,1:T(8,128)S(1)} %bitcast_multiply_fusion, f32[512,128]{1,0:T(8,128)S(1)} %copy-done.13), kind=kOutput, calls=%fused_computation.31 | convolution fusion | flops 402718720 | bytes 2097153 | tf_op jit(solution)/shard_map/tk,tn->kn/dot_general | solution.py:184
  16.2 8.8 %collective-permute-start = (f32[520,128]{0,1:T(8,128)S(1)}, f32[520,128]{0,1:T(8,128)S(1)}, u32[]{:S(2)}, u32[]{:S(2)}) collective-permute-start(f32[520,128]{0,1:T(8,128)S(1)} %pad_maximum_fusion.1), channel_id=1, source_target_pairs={{0,16},{16,0},{1,17},{17,1},{2,18},{18,2},{3,19},{19,3},{4,20},{20... | collective-permute-start | bytes 798728 | tf_op jit(solution)/shard_map/ppermute | solution.py:125
  25.0 1.2 collective-permute-done
  26.2 0.7 copy-done.17
  27.1 1.1 slice_add_fusion.1
  28.2 1.3 collective-permute-start.1
  29.5 6.6 %collective-permute-done.1 = f32[520,128]{0,1:T(8,128)} collective-permute-done((f32[520,128]{0,1:T(8,128)S(1)}, f32[520,128]{0,1:T(8,128)}, u32[]{:S(2)}, u32[]{:S(2)}) %collective-permute-start.1) | collective-permute-done | bytes 266272 | tf_op jit(solution)/shard_map/ppermute | solution.py:146
  36.2 1.3 collective-permute-start.2
  37.4 0.7 exponential_bitcast_fusion.2
  38.3 6.0 %collective-permute-done.2 = f32[520,128]{0,1:T(8,128)} collective-permute-done((f32[520,128]{0,1:T(8,128)}, f32[520,128]{0,1:T(8,128)}, u32[]{:S(2)}, u32[]{:S(2)}) %collective-permute-start.2) | collective-permute-done | bytes 266272 | tf_op jit(solution)/shard_map/ppermute | solution.py:146
  44.3 0.7 fusion.18
  45.0 1.1 slice_add_fusion
  46.1 0.8 pad_maximum_fusion.3
  46.9 1.3 collective-permute-start.3
  48.3 9.4 %collective-permute-done.3 = f32[520,128]{0,1:T(8,128)} collective-permute-done((f32[520,128]{0,1:T(8,128)}, f32[520,128]{0,1:T(8,128)}, u32[]{:S(2)}, u32[]{:S(2)}) %collective-permute-start.3) | collective-permute-done | bytes 266272 | tf_op jit(solution)/shard_map/ppermute | solution.py:146
  57.7 0.7 fusion.16
  58.4 1.1 fusion.5
  59.5 0.8 pad_maximum_fusion.4
  60.3 1.3 collective-permute-start.4
  61.7 12.9 %collective-permute-done.4 = f32[520,128]{0,1:T(8,128)} collective-permute-done((f32[520,128]{0,1:T(8,128)}, f32[520,128]{0,1:T(8,128)}, u32[]{:S(2)}, u32[]{:S(2)}) %collective-permute-start.4) | collective-permute-done | bytes 266272 | tf_op jit(solution)/shard_map/ppermute | solution.py:146
  74.6 0.7 fusion.14
  75.3 1.1 fusion.4
  76.4 0.8 pad_maximum_fusion.5
  77.2 1.3 collective-permute-start.5
  78.6 0.7 copy.34.cum_ref
  79.4 14.4 %shard_map.94 = (f32[512,512]{1,0:T(8,128)}, f32[512,512]{1,0:T(8,128)}) custom-call(f32[8,512]{1,0:T(8,128)} %copy.34.cum_ref, f32[512,8]{1,0:T(8,128)} %bitcast.67, f32[512,128]{1,0:T(8,128)} %proj_in_ref.1, f32[512,128]{1,0:T(8,128)} %proj_out_ref.1, f32[512,512]{1,0:T(8,128)} %get-tuple-element.16.in_ref, f32[512,512]{1,0:T(8,128)} %grad_ref.1), custom_call_target="tpu_custom_call" | custom-call | tf_op jit(solution)/shard_map/pallas_call | solution.py:73
  93.8 2.7 %fusion.24 = f32[512,128]{0,1:T(8,128)} fusion(f32[512,512]{1,0:T(8,128)} %get-tuple-element.6, f32[512,128]{1,0:T(8,128)S(1)} %copy-done.6), kind=kOutput, calls=%fused_computation.56 | convolution fusion | flops 402653184 | bytes 1572864 | tf_op jit(solution)/shard_map/st,sn->tn/dot_general | solution.py:193
  96.7 3.7 %collective-permute-done.5 = f32[520,128]{0,1:T(8,128)} collective-permute-done((f32[520,128]{0,1:T(8,128)}, f32[520,128]{0,1:T(8,128)}, u32[]{:S(2)}, u32[]{:S(2)}) %collective-permute-start.5) | collective-permute-done | bytes 266272 | tf_op jit(solution)/shard_map/ppermute | solution.py:146
  100.4 1.2 multiply_add_fusion
  101.6 14.8 %collective-permute-start.6 = (f32[512,128]{0,1:T(8,128)S(1)}, f32[512,128]{0,1:T(8,128)S(1)}, u32[]{:S(2)}, u32[]{:S(2)}) collective-permute-start(f32[512,128]{0,1:T(8,128)S(1)} %get-tuple-element.7), channel_id=1, source_target_pairs={{0,16},{16,0},{1,17},{17,1},{2,18},{18,2},{3,19},{19,3},{4,20},{20... | collective-permute-start | bytes 786440 | tf_op jit(solution)/shard_map/ppermute | solution.py:157
  116.5 1.2 fusion.23
  117.7 0.7 convolution_add_fusion
  118.5 1.2 convolution_add_fusion.1
  119.7 1.0 copy.46
  120.8 15.5 %all-to-all-start = ((f32[16,32,256]{2,1,0:T(8,128)}), f32[16,32,256]{2,1,0:T(8,128)S(1)}, u32[]{:S(2)}, u32[]{:S(2)}) async-start(f32[16,32,256]{2,1,0:T(8,128)} %bitcast.70), calls=%async_computation | async-start | bytes 1048576 | tf_op jit(solution)/shard_map/all_to_all | solution.py:204
  136.3 3.3 %fusion.2 = f32[512,512]{1,0:T(8,128)} fusion(f32[512,512]{1,0:T(8,128)S(1)} %copy.33, f32[512,512]{1,0:T(8,128)} %get-tuple-element.5, f32[512,512]{1,0:T(8,128)S(1)} %copy.44, f32[512,128]{1,0:T(8,128)S(1)} %copy-done.7, f32[512,128]{0,1:T(8,128)S(1)} %copy-done.9, f32[512,128]{0,1:T(8,128)S(1)} %get-tuple-element.8, pred[]{:T(512)S(6)} %eq.19), kind=kOutput, calls=%fused_computation.3 | convolution fusion | flops 403505152 | bytes 4980737 | tf_op jit(solution)/shard_map/tn,kn->tk/dot_general | solution.py:199
  139.6 7.7 %all-to-all-done = f32[16,32,256]{2,1,0:T(8,128)S(1)} async-done(((f32[16,32,256]{2,1,0:T(8,128)}), f32[16,32,256]{2,1,0:T(8,128)S(1)}, u32[]{:S(2)}, u32[]{:S(2)}) %all-to-all-start) | async-done | bytes 524320 | tf_op jit(solution)/shard_map/all_to_all | solution.py:204
  147.3 0.6 fusion.21
  (76 shorter events, 2.4 us)
Async XLA Ops:
  1.6 0.7 copy-start.18
  2.3 0.7 copy-start.19
  4.5 74.0 %copy-start.2 = (f32[8,4,128]{0,2,1:T(8,128)}, f32[8,4,128]{0,2,1:T(8,128)S(1)}, u32[]{:S(2)}) copy-start(f32[8,4,128]{0,2,1:T(8,128)S(1)} %copy.32) | copy-start | bytes 49156
  5.9 2.6 %copy-start.16 = (f32[512,8]{1,0:T(8,128)S(1)}, f32[512,8]{1,0:T(8,128)}, u32[]{:S(2)}) copy-start(f32[512,8]{1,0:T(8,128)} %get-tuple-element.19) | copy-start | bytes 49156
  8.7 2.6 %copy-start.5 = (f32[512,128]{1,0:T(8,128)S(1)}, f32[512,128]{1,0:T(8,128)}, u32[]{:S(2)}) copy-start(f32[512,128]{1,0:T(8,128)} %proj_in_ref.1) | copy-start | bytes 786436
  12.8 1.4 copy-start.4
  12.8 1.4 copy-start.13
  14.2 1.9 %copy-start = (f32[512,512]{0,1:T(8,128)}, f32[512,512]{0,1:T(8,128)S(1)}, u32[]{:S(2)}) copy-start(f32[512,512]{0,1:T(8,128)S(1)} %bitcast_multiply_fusion) | copy-start | bytes 3145732
  16.2 10.0 %collective-permute-start = (f32[520,128]{0,1:T(8,128)S(1)}, f32[520,128]{0,1:T(8,128)S(1)}, u32[]{:S(2)}, u32[]{:S(2)}) collective-permute-start(f32[520,128]{0,1:T(8,128)S(1)} %pad_maximum_fusion.1), channel_id=1, source_target_pairs={{0,16},{16,0},{1,17},{17,1},{2,18},{18,2},{3,19},{19,3},{4,20},{20... | collective-permute-start | bytes 798728 | tf_op jit(solution)/shard_map/ppermute | solution.py:125
  26.2 0.7 copy-start.17
  28.2 7.9 %collective-permute-start.1 = (f32[520,128]{0,1:T(8,128)S(1)}, f32[520,128]{0,1:T(8,128)}, u32[]{:S(2)}, u32[]{:S(2)}) collective-permute-start(f32[520,128]{0,1:T(8,128)S(1)} %pad_maximum_fusion.2), channel_id=1, source_target_pairs={{0,32},{32,64},{48,16},{64,96},{80,48},{96,128},{112,80},{128,160}... | collective-permute-start | bytes 798728 | tf_op jit(solution)/shard_map/ppermute | solution.py:146
  36.2 8.1 %collective-permute-start.2 = (f32[520,128]{0,1:T(8,128)}, f32[520,128]{0,1:T(8,128)}, u32[]{:S(2)}, u32[]{:S(2)}) collective-permute-start(f32[520,128]{0,1:T(8,128)} %collective-permute-done.1), channel_id=1, source_target_pairs={{0,32},{32,64},{48,16},{64,96},{80,48},{96,128},{112,80},{128,160}... | collective-permute-start | bytes 798728 | tf_op jit(solution)/shard_map/ppermute | solution.py:146
  46.1 0.8 copy-start.11
  46.9 10.8 %collective-permute-start.3 = (f32[520,128]{0,1:T(8,128)}, f32[520,128]{0,1:T(8,128)}, u32[]{:S(2)}, u32[]{:S(2)}) collective-permute-start(f32[520,128]{0,1:T(8,128)} %pad_maximum_fusion.3), channel_id=1, source_target_pairs={{0,64},{32,96},{64,128},{80,16},{96,160},{112,48},{128,192},{144,8... | collective-permute-start | bytes 798728 | tf_op jit(solution)/shard_map/ppermute | solution.py:146
  59.5 0.8 copy-start.10
  60.3 14.4 %collective-permute-start.4 = (f32[520,128]{0,1:T(8,128)}, f32[520,128]{0,1:T(8,128)}, u32[]{:S(2)}, u32[]{:S(2)}) collective-permute-start(f32[520,128]{0,1:T(8,128)} %pad_maximum_fusion.4), channel_id=1, source_target_pairs={{0,128},{32,160},{64,192},{96,224},{128,256},{144,16},{160,288},{1... | collective-permute-start | bytes 798728 | tf_op jit(solution)/shard_map/ppermute | solution.py:146
  76.4 0.8 copy-start.12
  77.2 23.1 %collective-permute-start.5 = (f32[520,128]{0,1:T(8,128)}, f32[520,128]{0,1:T(8,128)}, u32[]{:S(2)}, u32[]{:S(2)}) collective-permute-start(f32[520,128]{0,1:T(8,128)} %pad_maximum_fusion.5), channel_id=1, source_target_pairs={{0,256},{32,288},{64,320},{96,352},{128,384},{160,416},{192,448},{... | collective-permute-start | bytes 798728 | tf_op jit(solution)/shard_map/ppermute | solution.py:146
  79.4 14.4 %copy-start.6 = (f32[512,128]{1,0:T(8,128)S(1)}, f32[512,128]{1,0:T(8,128)}, u32[]{:S(2)}) copy-start(f32[512,128]{1,0:T(8,128)} %proj_in_ref.1) | copy-start | bytes 786436
  96.7 19.8 %copy-start.3 = (f32[512,512]{1,0:T(8,128)S(1)}, f32[512,512]{1,0:T(8,128)}, u32[]{:S(2)}) copy-start(f32[512,512]{1,0:T(8,128)} %get-tuple-element.6) | copy-start | bytes 3145732
  96.7 19.8 %copy-start.14 = (f32[512,128]{1,0:T(8,128)S(1)}, f32[512,128]{1,0:T(8,128)}, u32[]{:S(2)}) copy-start(f32[512,128]{1,0:T(8,128)} %proj_out_ref.1) | copy-start | bytes 786436
  101.6 16.1 %copy-start.1 = (f32[512,512]{0,1:T(8,128)S(1)}, f32[512,512]{0,1:T(8,128)}, u32[]{:S(2)}) copy-start(f32[512,512]{0,1:T(8,128)} %copy-done) | copy-start | bytes 3145732
  101.6 16.1 %copy-start.15 = (f32[512,128]{0,1:T(8,128)S(1)}, f32[512,128]{0,1:T(8,128)}, u32[]{:S(2)}) copy-start(f32[512,128]{0,1:T(8,128)} %fusion.24) | copy-start | bytes 786436
  101.6 16.1 %collective-permute-start.6 = (f32[512,128]{0,1:T(8,128)S(1)}, f32[512,128]{0,1:T(8,128)S(1)}, u32[]{:S(2)}, u32[]{:S(2)}) collective-permute-start(f32[512,128]{0,1:T(8,128)S(1)} %get-tuple-element.7), channel_id=1, source_target_pairs={{0,16},{16,0},{1,17},{17,1},{2,18},{18,2},{3,19},{19,3},{4,20},{20... | collective-permute-start | bytes 786440 | tf_op jit(solution)/shard_map/ppermute | solution.py:157
  117.7 0.8 copy-start.8
  120.8 15.5 %copy-start.7 = (f32[512,128]{1,0:T(8,128)S(1)}, f32[512,128]{1,0:T(8,128)}, u32[]{:S(2)}) copy-start(f32[512,128]{1,0:T(8,128)} %proj_in_ref.1) | copy-start | bytes 786436
  120.8 15.5 %copy-start.9 = (f32[512,128]{0,1:T(8,128)S(1)}, f32[512,128]{0,1:T(8,128)}, u32[]{:S(2)}) copy-start(f32[512,128]{0,1:T(8,128)} %copy-done.8) | copy-start | bytes 786436
  120.8 26.5 %all-to-all-start = ((f32[16,32,256]{2,1,0:T(8,128)}), f32[16,32,256]{2,1,0:T(8,128)S(1)}, u32[]{:S(2)}, u32[]{:S(2)}) async-start(f32[16,32,256]{2,1,0:T(8,128)} %bitcast.70), calls=%async_computation | async-start | bytes 1048576 | tf_op jit(solution)/shard_map/all_to_all | solution.py:204

commit v9 on v8

--- a/solution.py
+++ b/solution.py
@@ -23,8 +23,8 @@
     return wide.reshape(tok_count, head_count * head_width)
 
 
-def block_kernel(cum_ref, cum_t_ref, proj_in_ref, proj_out_ref, in_ref, grad_ref, flow_ref, acc_ref,
-                 scores_t_ref):
+def block_kernel(cum_ref, cum_t_ref, proj_in_ref, proj_out_ref, in_ref, grad_ref, flow_ref, part_b_ref,
+                 part_c_ref, acc_ref, scores_t_ref):
     step = pl.program_id(0)
 
     @pl.when(step == 0)
@@ -64,6 +64,17 @@
             )
             acc_ref[first:first + piece, first:] += pair_t * decay_t
 
+    @pl.when(step == pl.num_programs(0) - 1)
+    def _():
+        acc = acc_ref[...]
+        part_b_ref[...] = jnp.dot(
+            acc, proj_out_ref[...], precision=highest, preferred_element_type=jnp.float32
+        )
+        part_c_ref[...] = jnp.dot(
+            jnp.transpose(acc), proj_in_ref[...], precision=highest,
+            preferred_element_type=jnp.float32,
+        )
+
 
 def block_terms(cumul, input_proj, output_mapping, scaled_in, out_grad):
     head_count, tok = cumul.shape
@@ -83,13 +94,15 @@
         ],
         out_specs=[
             pl.BlockSpec((tok, lanes), lambda j: (0, j)),
-            pl.BlockSpec((tok, tok), lambda j: (0, 0)),
+            pl.BlockSpec((tok, state_width), lambda j: (0, 0)),
+            pl.BlockSpec((tok, state_width), lambda j: (0, 0)),
         ],
         out_shape=[
             jax.ShapeDtypeStruct((tok, chan), jnp.float32),
-            jax.ShapeDtypeStruct((tok, tok), jnp.float32),
+            jax.ShapeDtypeStruct((tok, state_width), jnp.float32),
+            jax.ShapeDtypeStruct((tok, state_width), jnp.float32),
         ],
-        scratch_shapes=[pltpu.VMEM((tok, tok), jnp.float32)],
+        scratch_shapes=[pltpu.VMEM((tok, tok), jnp.float32), pltpu.VMEM((tok, tok), jnp.float32)],
     )(cumul, cumul.T, input_proj, output_mapping, scaled_in, out_grad)
 
 
@@ -188,9 +201,9 @@
         group_total,
     )
 
-    grad_scaled, grad_scores_t = block_terms(cumul, input_proj, output_mapping, scaled_in, out_grad)
-    block_b = jnp.dot(grad_scores_t, output_mapping, precision=highest)
-    block_c = jnp.einsum("st,sn->tn", grad_scores_t, input_proj, precision=highest)
+    grad_scaled, block_b, block_c = block_terms(
+        cumul, input_proj, output_mapping, scaled_in, out_grad
+    )
 
     flat_in = state_in.reshape(head_count * head_width, state_width)
     flat_grad = state_grad.reshape(head_count * head_width, state_width)

time: 149 us -> 160 us (1.074)
  the two profiles are of different devices: /device:TPU:1 before, /device:TPU:32 now
where the time goes in v9:
time: 160 us
  starting transfers between devices  53.6 us (34%)
  waiting for transfers between devices  49.6 us (31%)
  other arithmetic  18.6 us (12%)
  Pallas kernels  16.3 us (10%)
  matrix products  11.9 us (7%)
  local copies, waits for them, and re-layouts  8.69 us (5%)
    ppermute x5, starting transfers between devices, move(): return lax.ppermute(value, both, pairs)  42.5 us
    ppermute x5, waiting for transfers between devices, move(): return lax.ppermute(value, both, pairs)  40 us
    pallas_call x1, Pallas kernels, block_terms(): pl.pallas_call(block_kernel, grid=(head_count // HEADS_PER_STEP,), in_spe...  16.3 us
    all_to_all x1, waiting for transfers between devices, per_device(): spread = lax.all_to_all(both, 'head', 0, 0, tiled=True)  7.95 us
    all_to_all x1, starting transfers between devices, per_device(): spread = lax.all_to_all(both, 'head', 0, 0, tiled=True)  7.13 us
    add x5, other arithmetic, join(): return jnp.exp(later_total)[:, None, None] * earlier + later  6.33 us
    unnamed x31, local copies, waits for them, and re-layouts  4.35 us
    dot_general x1, matrix products, per_device(): jnp.einsum('tn,kn->tk', input_proj, flat_grad, precision=highest)  3.36 us
  transfers between devices with their start and end apart: 8, of which 7 were waited for; matrix products, arithmetic and copies ran while one was open for 3% of the time, Pallas kernels for 10%

profile of v9, /device:TPU:32, one launch (start us, length us, event | category | flops | bytes accessed | tf_op | source)
XLA Modules:
  0.0 159.5 jit_solution(6603671715114658434)
XLA Ops:
  0.6 0.8 select_reduce_fusion
  1.6 0.3 copy.36
  1.9 0.3 copy-done.13
  2.3 0.6 copy-done.14
  3.0 1.1 reduce-window.6
  4.1 0.2 slice_reduce_fusion
  4.6 0.8 exponential_bitcast_fusion
  5.6 0.3 copy.47
  5.9 2.6 %copy.40 = f32[512,512]{0,1:T(8,128)} copy(f32[512,512]{1,0:T(8,128)} %grad_ref.1) | data formatting | bytes 2097152 | tf_op args[6]
  8.6 2.6 %fusion.20 = (f32[512,512]{1,0:T(8,128)S(1)}, f32[512,512]{1,0:T(8,128)}) fusion(f32[512,512]{1,0:T(8,128)S(1)} %copy.47, f32[512,512]{1,0:T(8,128)} %param.7, f32[512,512]{1,0:T(8,128)S(1)} %copy.36), kind=kLoop, calls=%fused_computation.52 | loop fusion | flops 524288 | bytes 5242880 | tf_op jit(solution)/shard_map/mul | solution.py:194
  11.2 1.5 fusion.22
  12.8 1.4 bitcast_multiply_fusion
  14.2 1.9 %broadcast_select_fusion.2 = (f32[512,128]{0,1:T(8,128)S(1)}, f32[512,128]{0,1:T(8,128)}) fusion(f32[512,128]{0,1:T(8,128)S(1)} %copy-done.3, pred[]{:T(512)S(6)} %eq.19, f32[512,512]{0,1:T(8,128)S(1)} %bitcast_multiply_fusion, f32[512,128]{1,0:T(8,128)S(1)} %copy-done.10), kind=kOutput, calls=%fused_computation.31 | convolution fusion | flops 402718720 | bytes 2097153 | tf_op jit(solution)/shard_map/tk,tn->kn/dot_general | solution.py:197
  16.1 1.9 %collective-permute-start = (f32[520,128]{0,1:T(8,128)S(1)}, f32[520,128]{0,1:T(8,128)S(1)}, u32[]{:S(2)}, u32[]{:S(2)}) collective-permute-start(f32[520,128]{0,1:T(8,128)S(1)} %pad_maximum_fusion.1), channel_id=1, source_target_pairs={{0,16},{16,0},{1,17},{17,1},{2,18},{18,2},{3,19},{19,3},{4,20},{20... | collective-permute-start | bytes 798728 | tf_op jit(solution)/shard_map/ppermute | solution.py:138
  18.1 1.6 collective-permute-done
  19.7 0.7 copy-done.12
  20.6 1.1 slice_add_fusion.1
  21.7 3.8 %collective-permute-start.1 = (f32[520,128]{0,1:T(8,128)S(1)}, f32[520,128]{0,1:T(8,128)}, u32[]{:S(2)}, u32[]{:S(2)}) collective-permute-start(f32[520,128]{0,1:T(8,128)S(1)} %pad_maximum_fusion.2), channel_id=1, source_target_pairs={{0,32},{32,64},{48,16},{64,96},{80,48},{96,128},{112,80},{128,160}... | collective-permute-start | bytes 798728 | tf_op jit(solution)/shard_map/ppermute | solution.py:159
  25.5 8.1 %collective-permute-done.1 = f32[520,128]{0,1:T(8,128)} collective-permute-done((f32[520,128]{0,1:T(8,128)S(1)}, f32[520,128]{0,1:T(8,128)}, u32[]{:S(2)}, u32[]{:S(2)}) %collective-permute-start.1) | collective-permute-done | bytes 266272 | tf_op jit(solution)/shard_map/ppermute | solution.py:159
  33.6 1.9 %collective-permute-start.2 = (f32[520,128]{0,1:T(8,128)}, f32[520,128]{0,1:T(8,128)}, u32[]{:S(2)}, u32[]{:S(2)}) collective-permute-start(f32[520,128]{0,1:T(8,128)} %collective-permute-done.1), channel_id=1, source_target_pairs={{0,32},{32,64},{48,16},{64,96},{80,48},{96,128},{112,80},{128,160}... | collective-permute-start | bytes 798728 | tf_op jit(solution)/shard_map/ppermute | solution.py:159
  35.5 0.7 exponential_bitcast_fusion.2
  36.4 6.5 %collective-permute-done.2 = f32[520,128]{0,1:T(8,128)} collective-permute-done((f32[520,128]{0,1:T(8,128)}, f32[520,128]{0,1:T(8,128)}, u32[]{:S(2)}, u32[]{:S(2)}) %collective-permute-start.2) | collective-permute-done | bytes 266272 | tf_op jit(solution)/shard_map/ppermute | solution.py:159
  42.9 0.7 fusion.18
  43.6 1.1 slice_add_fusion
  44.7 0.8 pad_maximum_fusion.3
  45.5 4.9 %collective-permute-start.3 = (f32[520,128]{0,1:T(8,128)}, f32[520,128]{0,1:T(8,128)}, u32[]{:S(2)}, u32[]{:S(2)}) collective-permute-start(f32[520,128]{0,1:T(8,128)} %pad_maximum_fusion.3), channel_id=1, source_target_pairs={{0,64},{32,96},{64,128},{80,16},{96,160},{112,48},{128,192},{144,8... | collective-permute-start | bytes 798728 | tf_op jit(solution)/shard_map/ppermute | solution.py:159
  50.5 6.2 %collective-permute-done.3 = f32[520,128]{0,1:T(8,128)} collective-permute-done((f32[520,128]{0,1:T(8,128)}, f32[520,128]{0,1:T(8,128)}, u32[]{:S(2)}, u32[]{:S(2)}) %collective-permute-start.3) | collective-permute-done | bytes 266272 | tf_op jit(solution)/shard_map/ppermute | solution.py:159
  56.7 0.7 fusion.16
  57.4 1.1 fusion.5
  58.5 0.8 pad_maximum_fusion.4
  59.3 10.3 %collective-permute-start.4 = (f32[520,128]{0,1:T(8,128)}, f32[520,128]{0,1:T(8,128)}, u32[]{:S(2)}, u32[]{:S(2)}) collective-permute-start(f32[520,128]{0,1:T(8,128)} %pad_maximum_fusion.4), channel_id=1, source_target_pairs={{0,128},{32,160},{64,192},{96,224},{128,256},{144,16},{160,288},{1... | collective-permute-start | bytes 798728 | tf_op jit(solution)/shard_map/ppermute | solution.py:159
  69.8 7.6 %collective-permute-done.4 = f32[520,128]{0,1:T(8,128)} collective-permute-done((f32[520,128]{0,1:T(8,128)}, f32[520,128]{0,1:T(8,128)}, u32[]{:S(2)}, u32[]{:S(2)}) %collective-permute-start.4) | collective-permute-done | bytes 266272 | tf_op jit(solution)/shard_map/ppermute | solution.py:159
  77.4 0.7 fusion.14
  78.1 1.1 fusion.4
  79.2 0.8 pad_maximum_fusion.5
  80.0 21.5 %collective-permute-start.5 = (f32[520,128]{0,1:T(8,128)}, f32[520,128]{0,1:T(8,128)}, u32[]{:S(2)}, u32[]{:S(2)}) collective-permute-start(f32[520,128]{0,1:T(8,128)} %pad_maximum_fusion.5), channel_id=1, source_target_pairs={{0,256},{32,288},{64,320},{96,352},{128,384},{160,416},{192,448},{... | collective-permute-start | bytes 798728 | tf_op jit(solution)/shard_map/ppermute | solution.py:159
  101.8 11.6 %collective-permute-done.5 = f32[520,128]{0,1:T(8,128)} collective-permute-done((f32[520,128]{0,1:T(8,128)}, f32[520,128]{0,1:T(8,128)}, u32[]{:S(2)}, u32[]{:S(2)}) %collective-permute-start.5) | collective-permute-done | bytes 266272 | tf_op jit(solution)/shard_map/ppermute | solution.py:159
  113.4 2.0 %multiply_add_fusion = (f32[512,128]{0,1:T(8,128)}, f32[512,128]{0,1:T(8,128)}) fusion(f32[512]{0:T(512)S(1)} %mul.137, f32[512,128]{0,1:T(8,128)} %fusion.22, f32[512,128]{0,1:T(8,128)} %get-tuple-element.26, pred[]{:T(512)S(6)} %eq.19, f32[512,128]{0,1:T(8,128)} %copy-done.6, f32[520,128]{0,1:T(8,128)} %collective-permute-done.5, f32[512]{0:T(512)S(1)} %mul.154), kind=kLoop, calls=%fused_computation.23 | loop fusion | flops 327680 | bytes 1576961 | tf_op jit(solution)/shard_map/add | solution.py:118
  115.4 2.1 %collective-permute-start.6 = (f32[512,128]{0,1:T(8,128)}, f32[512,128]{0,1:T(8,128)}, u32[]{:S(2)}, u32[]{:S(2)}) collective-permute-start(f32[512,128]{0,1:T(8,128)} %get-tuple-element.9), channel_id=1, source_target_pairs={{0,16},{16,0},{1,17},{17,1},{2,18},{18,2},{3,19},{19,3},{4,20},{20... | collective-permute-start | bytes 786440 | tf_op jit(solution)/shard_map/ppermute | solution.py:170
  117.5 0.7 copy.37.cum_ref
  118.2 16.3 %shard_map.94 = (f32[512,512]{1,0:T(8,128)}, f32[512,128]{1,0:T(8,128)}, f32[512,128]{1,0:T(8,128)}) custom-call(f32[8,512]{1,0:T(8,128)} %copy.37.cum_ref, f32[512,8]{1,0:T(8,128)} %bitcast.63, f32[512,128]{1,0:T(8,128)} %proj_in_ref.1, f32[512,128]{1,0:T(8,128)} %proj_out_ref.1, f32[512,512]{1,0:T(8,128)} %get-tuple-element.18.in_ref, f32[512,512]{1,0:T(8,128)} %grad_ref.1), custom_call_target="tpu_custom_call" | custom-call | tf_op jit(solution)/shard_map/pallas_call | solution.py:84
  134.5 3.1 %convolution_add_fusion = f32[512,128]{1,0:T(8,128)S(1)} fusion(f32[512,128]{1,0:T(8,128)} %get-tuple-element.8, f32[512,512]{0,1:T(8,128)} %copy-done, f32[512,128]{0,1:T(8,128)S(1)} %copy-done.2, f32[512,128]{0,1:T(8,128)} %collective-permute-done.6, pred[]{:T(512)S(6)} %eq.19), kind=kOutput, calls=%fused_computation.4 | convolution fusion | flops 402784256 | bytes 2097153 | tf_op jit(solution)/shard_map/dot_general | solution.py:210
  137.6 1.9 %convolution_add_fusion.1 = f32[512,128]{1,0:T(8,128)S(1)} fusion(f32[512,128]{1,0:T(8,128)S(1)} %copy-done.11, f32[512,512]{1,0:T(8,128)S(1)} %get-tuple-element.17, f32[512,128]{0,1:T(8,128)} %collective-permute-done.6, f32[512,128]{0,1:T(8,128)S(1)} %copy-done.2, pred[]{:T(512)S(6)} %eq.19), kind=kOutput, calls=%fused_computation.5 | convolution fusion | flops 402784256 | bytes 2097153 | tf_op jit(solution)/shard_map/dot_general | solution.py:211
  139.6 0.8 pad_maximum_fusion
  140.4 7.1 %all-to-all-start = ((f32[16,32,256]{2,1,0:T(8,128)}), f32[16,32,256]{2,1,0:T(8,128)S(1)}, u32[]{:S(2)}, u32[]{:S(2)}) async-start(f32[16,32,256]{2,1,0:T(8,128)} %bitcast.66), calls=%async_computation | async-start | bytes 1048576 | tf_op jit(solution)/shard_map/all_to_all | solution.py:217
  147.6 3.4 %fusion.2 = f32[512,512]{1,0:T(8,128)} fusion(f32[512,512]{1,0:T(8,128)S(1)} %copy.36, f32[512,512]{1,0:T(8,128)} %get-tuple-element.6, f32[512,512]{1,0:T(8,128)S(1)} %copy.47, f32[512,128]{1,0:T(8,128)S(1)} %copy-done.8, f32[512,128]{0,1:T(8,128)} %collective-permute-done.6, f32[512,128]{0,1:T(8,128)S(1)} %copy-done.2, pred[]{:T(512)S(6)} %eq.19), kind=kOutput, calls=%fused_computation.3 | convolution fusion | flops 403505152 | bytes 4980737 | tf_op jit(solution)/shard_map/tn,kn->tk/dot_general | solution.py:212
  150.9 7.9 %all-to-all-done = f32[16,32,256]{2,1,0:T(8,128)S(1)} async-done(((f32[16,32,256]{2,1,0:T(8,128)}), f32[16,32,256]{2,1,0:T(8,128)S(1)}, u32[]{:S(2)}, u32[]{:S(2)}) %all-to-all-start) | async-done | bytes 524320 | tf_op jit(solution)/shard_map/all_to_all | solution.py:217
  158.9 0.6 fusion.21
  (63 shorter events, 1.8 us)
Async XLA Ops:
  1.6 0.7 copy-start.13
  2.3 0.7 copy-start.14
  4.5 112.9 %copy-start.1 = (f32[8,4,128]{0,2,1:T(8,128)}, f32[8,4,128]{0,2,1:T(8,128)S(1)}, u32[]{:S(2)}) copy-start(f32[8,4,128]{0,2,1:T(8,128)S(1)} %copy.35) | copy-start | bytes 49156
  5.9 2.6 %copy-start.9 = (f32[512,8]{1,0:T(8,128)S(1)}, f32[512,8]{1,0:T(8,128)}, u32[]{:S(2)}) copy-start(f32[512,8]{1,0:T(8,128)} %get-tuple-element.21) | copy-start | bytes 49156
  8.6 2.6 %copy-start.7 = (f32[512,128]{1,0:T(8,128)S(1)}, f32[512,128]{1,0:T(8,128)}, u32[]{:S(2)}) copy-start(f32[512,128]{1,0:T(8,128)} %proj_in_ref.1) | copy-start | bytes 786436
  12.8 1.4 copy-start.3
  12.8 1.4 copy-start.10
  14.2 1.9 %copy-start = (f32[512,512]{0,1:T(8,128)}, f32[512,512]{0,1:T(8,128)S(1)}, u32[]{:S(2)}) copy-start(f32[512,512]{0,1:T(8,128)S(1)} %bitcast_multiply_fusion) | copy-start | bytes 3145732
  16.1 3.5 %collective-permute-start = (f32[520,128]{0,1:T(8,128)S(1)}, f32[520,128]{0,1:T(8,128)S(1)}, u32[]{:S(2)}, u32[]{:S(2)}) collective-permute-start(f32[520,128]{0,1:T(8,128)S(1)} %pad_maximum_fusion.1), channel_id=1, source_target_pairs={{0,16},{16,0},{1,17},{17,1},{2,18},{18,2},{3,19},{19,3},{4,20},{20... | collective-permute-start | bytes 798728 | tf_op jit(solution)/shard_map/ppermute | solution.py:138
  19.7 0.7 copy-start.12
  21.7 11.9 %collective-permute-start.1 = (f32[520,128]{0,1:T(8,128)S(1)}, f32[520,128]{0,1:T(8,128)}, u32[]{:S(2)}, u32[]{:S(2)}) collective-permute-start(f32[520,128]{0,1:T(8,128)S(1)} %pad_maximum_fusion.2), channel_id=1, source_target_pairs={{0,32},{32,64},{48,16},{64,96},{80,48},{96,128},{112,80},{128,160}... | collective-permute-start | bytes 798728 | tf_op jit(solution)/shard_map/ppermute | solution.py:159
  33.6 9.3 %collective-permute-start.2 = (f32[520,128]{0,1:T(8,128)}, f32[520,128]{0,1:T(8,128)}, u32[]{:S(2)}, u32[]{:S(2)}) collective-permute-start(f32[520,128]{0,1:T(8,128)} %collective-permute-done.1), channel_id=1, source_target_pairs={{0,32},{32,64},{48,16},{64,96},{80,48},{96,128},{112,80},{128,160}... | collective-permute-start | bytes 798728 | tf_op jit(solution)/shard_map/ppermute | solution.py:159
  44.7 0.8 copy-start.5
  45.5 11.3 %collective-permute-start.3 = (f32[520,128]{0,1:T(8,128)}, f32[520,128]{0,1:T(8,128)}, u32[]{:S(2)}, u32[]{:S(2)}) collective-permute-start(f32[520,128]{0,1:T(8,128)} %pad_maximum_fusion.3), channel_id=1, source_target_pairs={{0,64},{32,96},{64,128},{80,16},{96,160},{112,48},{128,192},{144,8... | collective-permute-start | bytes 798728 | tf_op jit(solution)/shard_map/ppermute | solution.py:159
  58.5 0.8 copy-start.4
  59.3 18.1 %collective-permute-start.4 = (f32[520,128]{0,1:T(8,128)}, f32[520,128]{0,1:T(8,128)}, u32[]{:S(2)}, u32[]{:S(2)}) collective-permute-start(f32[520,128]{0,1:T(8,128)} %pad_maximum_fusion.4), channel_id=1, source_target_pairs={{0,128},{32,160},{64,192},{96,224},{128,256},{144,16},{160,288},{1... | collective-permute-start | bytes 798728 | tf_op jit(solution)/shard_map/ppermute | solution.py:159
  79.2 0.8 copy-start.6
  80.0 33.4 %collective-permute-start.5 = (f32[520,128]{0,1:T(8,128)}, f32[520,128]{0,1:T(8,128)}, u32[]{:S(2)}, u32[]{:S(2)}) collective-permute-start(f32[520,128]{0,1:T(8,128)} %pad_maximum_fusion.5), channel_id=1, source_target_pairs={{0,256},{32,288},{64,320},{96,352},{128,384},{160,416},{192,448},{... | collective-permute-start | bytes 798728 | tf_op jit(solution)/shard_map/ppermute | solution.py:159
  115.4 19.1 %collective-permute-start.6 = (f32[512,128]{0,1:T(8,128)}, f32[512,128]{0,1:T(8,128)}, u32[]{:S(2)}, u32[]{:S(2)}) collective-permute-start(f32[512,128]{0,1:T(8,128)} %get-tuple-element.9), channel_id=1, source_target_pairs={{0,16},{16,0},{1,17},{17,1},{2,18},{18,2},{3,19},{19,3},{4,20},{20... | collective-permute-start | bytes 786440 | tf_op jit(solution)/shard_map/ppermute | solution.py:170
  118.2 16.3 %copy-start.2 = (f32[512,128]{0,1:T(8,128)S(1)}, f32[512,128]{0,1:T(8,128)}, u32[]{:S(2)}) copy-start(f32[512,128]{0,1:T(8,128)} %get-tuple-element.10) | copy-start | bytes 786436
  134.5 3.1 %copy-start.11 = (f32[512,128]{1,0:T(8,128)S(1)}, f32[512,128]{1,0:T(8,128)}, u32[]{:S(2)}) copy-start(f32[512,128]{1,0:T(8,128)} %get-tuple-element.7) | copy-start | bytes 786436
  140.4 7.1 %copy-start.8 = (f32[512,128]{1,0:T(8,128)S(1)}, f32[512,128]{1,0:T(8,128)}, u32[]{:S(2)}) copy-start(f32[512,128]{1,0:T(8,128)} %proj_in_ref.1) | copy-start | bytes 786436
  140.4 18.5 %all-to-all-start = ((f32[16,32,256]{2,1,0:T(8,128)}), f32[16,32,256]{2,1,0:T(8,128)S(1)}, u32[]{:S(2)}, u32[]{:S(2)}) async-start(f32[16,32,256]{2,1,0:T(8,128)} %bitcast.66), calls=%async_computation | async-start | bytes 1048576 | tf_op jit(solution)/shard_map/all_to_all | solution.py:217

commit v10 on v8

--- a/solution.py
+++ b/solution.py
@@ -7,7 +7,7 @@
 
 sudden_falloff = 0.35
 highest = lax.Precision.HIGHEST
-HEADS_PER_STEP = 2
+HEADS_PER_STEP = 4
 
 
 def step_table(decay_codes):
@@ -51,7 +51,7 @@
             cols = lax.broadcasted_iota(jnp.int32, (piece, span), 1)
             later = cols >= rows
             gap = cum_row[:, first:] - cum_col[first:first + piece, :]
-            decay_t = jnp.where(later, jnp.exp(jnp.where(later, gap, 0.0)), 0.0)
+            decay_t = jnp.where(later, jnp.exp(gap), 0.0)
             own_in = in_ref[first:first + piece, lanes]
             own_grad = grad_ref[first:, lanes]
             flow_ref[first:first + piece, lanes] = jnp.dot(

time: 149 us -> 148 us (level)
  no operation moved by 1% of the time
where the time goes in v10:
time: 148 us; the launch traced here: 147 us
  waiting for transfers between devices  47.5 us (32%)
  starting transfers between devices  45.3 us (31%)
  other arithmetic  17.1 us (12%)
  Pallas kernels  14.1 us (10%)
  matrix products  12.6 us (9%)
  local copies, waits for them, and re-layouts  9.74 us (7%)
    ppermute x5, waiting for transfers between devices, move(): return lax.ppermute(value, both, pairs)  38.7 us
    all_to_all x1, starting transfers between devices, per_device(): spread = lax.all_to_all(both, 'head', 0, 0, tiled=True)  15.5 us
    ppermute x1, starting transfers between devices, chip_scans(): back = lax.ppermute(joined.reshape(rows, state_width), 'core', swap)  14.4 us
    pallas_call x1, Pallas kernels, block_terms(): pl.pallas_call(block_kernel, grid=(head_count // HEADS_PER_STEP,), in_spe...  14.1 us
    ppermute x1, starting transfers between devices, chip_scans(): incoming = lax.ppermute(outgoing, 'core', swap)  8.78 us
    all_to_all x1, waiting for transfers between devices, per_device(): spread = lax.all_to_all(both, 'head', 0, 0, tiled=True)  7.55 us
    ppermute x5, starting transfers between devices, move(): return lax.ppermute(value, both, pairs)  6.59 us
    add x5, other arithmetic, join(): return jnp.exp(later_total)[:, None, None] * earlier + later  5.52 us
  transfers between devices with their start and end apart: 8, of which 7 were waited for; matrix products, arithmetic and copies ran while one was open for 6% of the time, Pallas kernels for 10%

profile of v10, /device:TPU:1, one launch (start us, length us, event | category | flops | bytes accessed | tf_op | source)
XLA Modules:
  0.0 147.3 jit_solution(17624570874214616537)
XLA Ops:
  0.6 0.8 select_reduce_fusion
  1.9 0.3 copy-done.18
  2.3 0.6 copy-done.19
  3.0 1.1 reduce-window.6
  4.6 0.8 exponential_bitcast_fusion
  5.6 0.3 copy.44
  5.9 2.6 %copy.37 = f32[512,512]{0,1:T(8,128)} copy(f32[512,512]{1,0:T(8,128)} %grad_ref.1) | data formatting | bytes 2097152 | tf_op args[6]
  8.6 2.6 %fusion.20 = (f32[512,512]{1,0:T(8,128)S(1)}, f32[512,512]{1,0:T(8,128)}) fusion(f32[512,512]{1,0:T(8,128)S(1)} %copy.44, f32[512,512]{1,0:T(8,128)} %param.7, f32[512,512]{1,0:T(8,128)S(1)} %copy.33), kind=kLoop, calls=%fused_computation.52 | loop fusion | flops 524288 | bytes 5242880 | tf_op jit(solution)/shard_map/mul | solution.py:181
  11.2 1.5 %fusion.22 = f32[512,128]{0,1:T(8,128)} fusion(f32[512,512]{1,0:T(8,128)S(1)} %get-tuple-element.15, f32[512,128]{1,0:T(8,128)S(1)} %copy-done.5), kind=kOutput, calls=%fused_computation.54 | convolution fusion | flops 402653184 | bytes 1572864 | tf_op jit(solution)/shard_map/tk,tn->kn/dot_general | solution.py:183
  12.8 1.4 bitcast_multiply_fusion
  14.2 1.9 %broadcast_select_fusion.2 = (f32[512,128]{0,1:T(8,128)S(1)}, f32[512,128]{0,1:T(8,128)}) fusion(f32[512,128]{0,1:T(8,128)S(1)} %copy-done.4, pred[]{:T(512)S(6)} %eq.19, f32[512,512]{0,1:T(8,128)S(1)} %bitcast_multiply_fusion, f32[512,128]{1,0:T(8,128)S(1)} %copy-done.13), kind=kOutput, calls=%fused_computation.31 | convolution fusion | flops 402718720 | bytes 2097153 | tf_op jit(solution)/shard_map/tk,tn->kn/dot_general | solution.py:184
  16.1 8.8 %collective-permute-start = (f32[520,128]{0,1:T(8,128)S(1)}, f32[520,128]{0,1:T(8,128)S(1)}, u32[]{:S(2)}, u32[]{:S(2)}) collective-permute-start(f32[520,128]{0,1:T(8,128)S(1)} %pad_maximum_fusion.1), channel_id=1, source_target_pairs={{0,16},{16,0},{1,17},{17,1},{2,18},{18,2},{3,19},{19,3},{4,20},{20... | collective-permute-start | bytes 798728 | tf_op jit(solution)/shard_map/ppermute | solution.py:125
  24.9 1.2 collective-permute-done
  26.2 0.7 copy-done.17
  27.1 1.1 slice_add_fusion.1
  28.2 1.3 collective-permute-start.1
  29.5 6.6 %collective-permute-done.1 = f32[520,128]{0,1:T(8,128)} collective-permute-done((f32[520,128]{0,1:T(8,128)S(1)}, f32[520,128]{0,1:T(8,128)}, u32[]{:S(2)}, u32[]{:S(2)}) %collective-permute-start.1) | collective-permute-done | bytes 266272 | tf_op jit(solution)/shard_map/ppermute | solution.py:146
  36.1 1.3 collective-permute-start.2
  37.4 0.7 exponential_bitcast_fusion.2
  38.3 6.0 %collective-permute-done.2 = f32[520,128]{0,1:T(8,128)} collective-permute-done((f32[520,128]{0,1:T(8,128)}, f32[520,128]{0,1:T(8,128)}, u32[]{:S(2)}, u32[]{:S(2)}) %collective-permute-start.2) | collective-permute-done | bytes 266272 | tf_op jit(solution)/shard_map/ppermute | solution.py:146
  44.3 0.7 fusion.18
  45.0 1.1 slice_add_fusion
  46.0 0.8 pad_maximum_fusion.3
  46.9 1.3 collective-permute-start.3
  48.3 9.4 %collective-permute-done.3 = f32[520,128]{0,1:T(8,128)} collective-permute-done((f32[520,128]{0,1:T(8,128)}, f32[520,128]{0,1:T(8,128)}, u32[]{:S(2)}, u32[]{:S(2)}) %collective-permute-start.3) | collective-permute-done | bytes 266272 | tf_op jit(solution)/shard_map/ppermute | solution.py:146
  57.7 0.7 fusion.16
  58.4 1.1 fusion.5
  59.5 0.8 pad_maximum_fusion.4
  60.3 1.3 collective-permute-start.4
  61.7 12.9 %collective-permute-done.4 = f32[520,128]{0,1:T(8,128)} collective-permute-done((f32[520,128]{0,1:T(8,128)}, f32[520,128]{0,1:T(8,128)}, u32[]{:S(2)}, u32[]{:S(2)}) %collective-permute-start.4) | collective-permute-done | bytes 266272 | tf_op jit(solution)/shard_map/ppermute | solution.py:146
  74.6 0.7 fusion.14
  75.3 1.1 fusion.4
  76.4 0.8 pad_maximum_fusion.5
  77.2 1.5 collective-permute-start.5
  78.7 0.7 copy.34.cum_ref
  79.6 14.1 %shard_map.94 = (f32[512,512]{1,0:T(8,128)}, f32[512,512]{1,0:T(8,128)}) custom-call(f32[8,512]{1,0:T(8,128)} %copy.34.cum_ref, f32[512,8]{1,0:T(8,128)} %bitcast.67, f32[512,128]{1,0:T(8,128)} %proj_in_ref.1, f32[512,128]{1,0:T(8,128)} %proj_out_ref.1, f32[512,512]{1,0:T(8,128)} %get-tuple-element.16.in_ref, f32[512,512]{1,0:T(8,128)} %grad_ref.1), custom_call_target="tpu_custom_call" | custom-call | tf_op jit(solution)/shard_map/pallas_call | solution.py:73
  93.7 2.7 %fusion.24 = f32[512,128]{0,1:T(8,128)} fusion(f32[512,512]{1,0:T(8,128)} %get-tuple-element.6, f32[512,128]{1,0:T(8,128)S(1)} %copy-done.6), kind=kOutput, calls=%fused_computation.56 | convolution fusion | flops 402653184 | bytes 1572864 | tf_op jit(solution)/shard_map/st,sn->tn/dot_general | solution.py:193
  96.6 3.8 %collective-permute-done.5 = f32[520,128]{0,1:T(8,128)} collective-permute-done((f32[520,128]{0,1:T(8,128)}, f32[520,128]{0,1:T(8,128)}, u32[]{:S(2)}, u32[]{:S(2)}) %collective-permute-start.5) | collective-permute-done | bytes 266272 | tf_op jit(solution)/shard_map/ppermute | solution.py:146
  100.4 1.2 multiply_add_fusion
  101.6 14.4 %collective-permute-start.6 = (f32[512,128]{0,1:T(8,128)S(1)}, f32[512,128]{0,1:T(8,128)S(1)}, u32[]{:S(2)}, u32[]{:S(2)}) collective-permute-start(f32[512,128]{0,1:T(8,128)S(1)} %get-tuple-element.7), channel_id=1, source_target_pairs={{0,16},{16,0},{1,17},{17,1},{2,18},{18,2},{3,19},{19,3},{4,20},{20... | collective-permute-start | bytes 786440 | tf_op jit(solution)/shard_map/ppermute | solution.py:157
  116.0 1.2 fusion.23
  117.3 0.7 convolution_add_fusion
  118.0 1.2 convolution_add_fusion.1
  119.3 1.0 copy.46
  120.3 15.5 %all-to-all-start = ((f32[16,32,256]{2,1,0:T(8,128)}), f32[16,32,256]{2,1,0:T(8,128)S(1)}, u32[]{:S(2)}, u32[]{:S(2)}) async-start(f32[16,32,256]{2,1,0:T(8,128)} %bitcast.70), calls=%async_computation | async-start | bytes 1048576 | tf_op jit(solution)/shard_map/all_to_all | solution.py:204
  135.9 3.3 %fusion.2 = f32[512,512]{1,0:T(8,128)} fusion(f32[512,512]{1,0:T(8,128)S(1)} %copy.33, f32[512,512]{1,0:T(8,128)} %get-tuple-element.5, f32[512,512]{1,0:T(8,128)S(1)} %copy.44, f32[512,128]{1,0:T(8,128)S(1)} %copy-done.7, f32[512,128]{0,1:T(8,128)S(1)} %copy-done.9, f32[512,128]{0,1:T(8,128)S(1)} %get-tuple-element.8, pred[]{:T(512)S(6)} %eq.19), kind=kOutput, calls=%fused_computation.3 | convolution fusion | flops 403505152 | bytes 4980737 | tf_op jit(solution)/shard_map/tn,kn->tk/dot_general | solution.py:199
  139.1 7.5 %all-to-all-done = f32[16,32,256]{2,1,0:T(8,128)S(1)} async-done(((f32[16,32,256]{2,1,0:T(8,128)}), f32[16,32,256]{2,1,0:T(8,128)S(1)}, u32[]{:S(2)}, u32[]{:S(2)}) %all-to-all-start) | async-done | bytes 524320 | tf_op jit(solution)/shard_map/all_to_all | solution.py:204
  146.7 0.6 fusion.21
  (76 shorter events, 2.4 us)
Async XLA Ops:
  1.6 0.7 copy-start.18
  2.3 0.7 copy-start.19
  4.5 74.2 %copy-start.2 = (f32[8,4,128]{0,2,1:T(8,128)}, f32[8,4,128]{0,2,1:T(8,128)S(1)}, u32[]{:S(2)}) copy-start(f32[8,4,128]{0,2,1:T(8,128)S(1)} %copy.32) | copy-start | bytes 49156
  5.9 2.6 %copy-start.16 = (f32[512,8]{1,0:T(8,128)S(1)}, f32[512,8]{1,0:T(8,128)}, u32[]{:S(2)}) copy-start(f32[512,8]{1,0:T(8,128)} %get-tuple-element.19) | copy-start | bytes 49156
  8.6 2.6 %copy-start.5 = (f32[512,128]{1,0:T(8,128)S(1)}, f32[512,128]{1,0:T(8,128)}, u32[]{:S(2)}) copy-start(f32[512,128]{1,0:T(8,128)} %proj_in_ref.1) | copy-start | bytes 786436
  12.8 1.4 copy-start.4
  12.8 1.4 copy-start.13
  14.2 1.9 %copy-start = (f32[512,512]{0,1:T(8,128)}, f32[512,512]{0,1:T(8,128)S(1)}, u32[]{:S(2)}) copy-start(f32[512,512]{0,1:T(8,128)S(1)} %bitcast_multiply_fusion) | copy-start | bytes 3145732
  16.1 10.0 %collective-permute-start = (f32[520,128]{0,1:T(8,128)S(1)}, f32[520,128]{0,1:T(8,128)S(1)}, u32[]{:S(2)}, u32[]{:S(2)}) collective-permute-start(f32[520,128]{0,1:T(8,128)S(1)} %pad_maximum_fusion.1), channel_id=1, source_target_pairs={{0,16},{16,0},{1,17},{17,1},{2,18},{18,2},{3,19},{19,3},{4,20},{20... | collective-permute-start | bytes 798728 | tf_op jit(solution)/shard_map/ppermute | solution.py:125
  26.2 0.7 copy-start.17
  28.2 7.9 %collective-permute-start.1 = (f32[520,128]{0,1:T(8,128)S(1)}, f32[520,128]{0,1:T(8,128)}, u32[]{:S(2)}, u32[]{:S(2)}) collective-permute-start(f32[520,128]{0,1:T(8,128)S(1)} %pad_maximum_fusion.2), channel_id=1, source_target_pairs={{0,32},{32,64},{48,16},{64,96},{80,48},{96,128},{112,80},{128,160}... | collective-permute-start | bytes 798728 | tf_op jit(solution)/shard_map/ppermute | solution.py:146
  36.1 8.1 %collective-permute-start.2 = (f32[520,128]{0,1:T(8,128)}, f32[520,128]{0,1:T(8,128)}, u32[]{:S(2)}, u32[]{:S(2)}) collective-permute-start(f32[520,128]{0,1:T(8,128)} %collective-permute-done.1), channel_id=1, source_target_pairs={{0,32},{32,64},{48,16},{64,96},{80,48},{96,128},{112,80},{128,160}... | collective-permute-start | bytes 798728 | tf_op jit(solution)/shard_map/ppermute | solution.py:146
  46.0 0.8 copy-start.11
  46.9 10.8 %collective-permute-start.3 = (f32[520,128]{0,1:T(8,128)}, f32[520,128]{0,1:T(8,128)}, u32[]{:S(2)}, u32[]{:S(2)}) collective-permute-start(f32[520,128]{0,1:T(8,128)} %pad_maximum_fusion.3), channel_id=1, source_target_pairs={{0,64},{32,96},{64,128},{80,16},{96,160},{112,48},{128,192},{144,8... | collective-permute-start | bytes 798728 | tf_op jit(solution)/shard_map/ppermute | solution.py:146
  59.4 0.8 copy-start.10
  60.3 14.4 %collective-permute-start.4 = (f32[520,128]{0,1:T(8,128)}, f32[520,128]{0,1:T(8,128)}, u32[]{:S(2)}, u32[]{:S(2)}) collective-permute-start(f32[520,128]{0,1:T(8,128)} %pad_maximum_fusion.4), channel_id=1, source_target_pairs={{0,128},{32,160},{64,192},{96,224},{128,256},{144,16},{160,288},{1... | collective-permute-start | bytes 798728 | tf_op jit(solution)/shard_map/ppermute | solution.py:146
  76.4 0.8 copy-start.12
  77.2 23.1 %collective-permute-start.5 = (f32[520,128]{0,1:T(8,128)}, f32[520,128]{0,1:T(8,128)}, u32[]{:S(2)}, u32[]{:S(2)}) collective-permute-start(f32[520,128]{0,1:T(8,128)} %pad_maximum_fusion.5), channel_id=1, source_target_pairs={{0,256},{32,288},{64,320},{96,352},{128,384},{160,416},{192,448},{... | collective-permute-start | bytes 798728 | tf_op jit(solution)/shard_map/ppermute | solution.py:146
  79.6 14.1 %copy-start.6 = (f32[512,128]{1,0:T(8,128)S(1)}, f32[512,128]{1,0:T(8,128)}, u32[]{:S(2)}) copy-start(f32[512,128]{1,0:T(8,128)} %proj_in_ref.1) | copy-start | bytes 786436
  96.6 19.4 %copy-start.3 = (f32[512,512]{1,0:T(8,128)S(1)}, f32[512,512]{1,0:T(8,128)}, u32[]{:S(2)}) copy-start(f32[512,512]{1,0:T(8,128)} %get-tuple-element.6) | copy-start | bytes 3145732
  96.6 19.4 %copy-start.14 = (f32[512,128]{1,0:T(8,128)S(1)}, f32[512,128]{1,0:T(8,128)}, u32[]{:S(2)}) copy-start(f32[512,128]{1,0:T(8,128)} %proj_out_ref.1) | copy-start | bytes 786436
  101.6 15.7 %copy-start.1 = (f32[512,512]{0,1:T(8,128)S(1)}, f32[512,512]{0,1:T(8,128)}, u32[]{:S(2)}) copy-start(f32[512,512]{0,1:T(8,128)} %copy-done) | copy-start | bytes 3145732
  101.6 15.7 %copy-start.15 = (f32[512,128]{0,1:T(8,128)S(1)}, f32[512,128]{0,1:T(8,128)}, u32[]{:S(2)}) copy-start(f32[512,128]{0,1:T(8,128)} %fusion.24) | copy-start | bytes 786436
  101.6 15.6 %collective-permute-start.6 = (f32[512,128]{0,1:T(8,128)S(1)}, f32[512,128]{0,1:T(8,128)S(1)}, u32[]{:S(2)}, u32[]{:S(2)}) collective-permute-start(f32[512,128]{0,1:T(8,128)S(1)} %get-tuple-element.7), channel_id=1, source_target_pairs={{0,16},{16,0},{1,17},{17,1},{2,18},{18,2},{3,19},{19,3},{4,20},{20... | collective-permute-start | bytes 786440 | tf_op jit(solution)/shard_map/ppermute | solution.py:157
  117.3 0.8 copy-start.8
  120.3 15.5 %copy-start.7 = (f32[512,128]{1,0:T(8,128)S(1)}, f32[512,128]{1,0:T(8,128)}, u32[]{:S(2)}) copy-start(f32[512,128]{1,0:T(8,128)} %proj_in_ref.1) | copy-start | bytes 786436
  120.3 15.5 %copy-start.9 = (f32[512,128]{0,1:T(8,128)S(1)}, f32[512,128]{0,1:T(8,128)}, u32[]{:S(2)}) copy-start(f32[512,128]{0,1:T(8,128)} %copy-done.8) | copy-start | bytes 786436
  120.3 26.4 %all-to-all-start = ((f32[16,32,256]{2,1,0:T(8,128)}), f32[16,32,256]{2,1,0:T(8,128)S(1)}, u32[]{:S(2)}, u32[]{:S(2)}) async-start(f32[16,32,256]{2,1,0:T(8,128)} %bitcast.70), calls=%async_computation | async-start | bytes 1048576 | tf_op jit(solution)/shard_map/all_to_all | solution.py:204

commit v11 on v10

--- a/solution.py
+++ b/solution.py
@@ -117,16 +117,8 @@
     both = ("z", "core")
     swap = [(0, 1), (1, 0)]
     is_fwd = core == 0
-    tot_rows = pack_total(total, state_width)
     mine = pick(is_fwd, ends, starts)
-    outgoing = jnp.concatenate(
-        [pick(is_fwd, starts, ends).reshape(rows, state_width), tot_rows], axis=0
-    )
-    incoming = lax.ppermute(outgoing, "core", swap)
-    partner = incoming[:rows].reshape(head_count, width, state_width)
-    partner_t = incoming[rows:rows + head_count, 0]
-    chip_state = join(mine, partner, partner_t)
-    chip_t = total + partner_t
+    other = pick(is_fwd, starts, ends)
 
     def packed(state, tot):
         return jnp.concatenate(
@@ -145,7 +137,15 @@
                 pairs.append((2 * z + 1, 2 * (z - hop) + 1))
         return lax.ppermute(value, both, pairs)
 
-    running = move(packed(chip_state, chip_t), 1)
+    cross = []
+    for z in range(chips):
+        if z + 1 < chips:
+            cross.append((2 * z + 1, 2 * (z + 1)))
+        if z - 1 >= 0:
+            cross.append((2 * z, 2 * (z - 1) + 1))
+    near_state, near_t = unpacked(move(packed(mine, total), 1))
+    far_state, far_t = unpacked(lax.ppermute(packed(other, total), both, cross))
+    running = packed(join(near_state, far_state, far_t), near_t + far_t)
     hop = 1
     while hop < chips:
         got_state, got_t = unpacked(move(running, hop))

time: 148 us -> 143 us (0.966)
  starting transfers between devices: 45.3 us -> 41.4 us
  local copies, waits for them, and re-layouts: 9.74 us -> 12.3 us
  other arithmetic: 17.1 us -> 15 us
    ppermute x1, starting transfers between devices: 14.4 us -> 23 us  [chip_scans(): back = lax.ppermute(joined.reshape(rows, state_width), 'core', swap)]
    all_to_all x1, starting transfers between devices: 15.5 us -> 6.89 us  [per_device(): spread = lax.all_to_all(both, 'head', 0, 0, tiled=True)]
    ppermute x1, starting transfers between devices: 8.78 us -> 4.92 us  [chip_scans(): far_state, far_t = unpacked(lax.ppermute(packed(other, total), both, cross))]
    ppermute x5, waiting for transfers between devices: 38.7 us -> 36 us  [move(): return lax.ppermute(value, both, pairs)]
    unnamed x41 -> x45, local copies, waits for them, and re-layouts: 4.4 us -> 6.67 us
    exp x3, other arithmetic: 2.07 us -> 0.03 us  [join(): return jnp.exp(later_total)[:, None, None] * earlier + later]
    ppermute x1, waiting for transfers between devices: 1.23 us -> 2.79 us  [chip_scans(): far_state, far_t = unpacked(lax.ppermute(packed(other, total), both, cross))]
where the time goes in v11:
time: 143 us; the launch traced here: 142 us
  waiting for transfers between devices  46.4 us (32%)
  starting transfers between devices  41.4 us (29%)
  other arithmetic  15 us (10%)
  Pallas kernels  14.1 us (10%)
  local copies, waits for them, and re-layouts  12.3 us (9%)
  matrix products  12 us (8%)
    ppermute x5, waiting for transfers between devices, move(): return lax.ppermute(value, both, pairs)  36 us
    ppermute x1, starting transfers between devices, chip_scans(): back = lax.ppermute(joined.reshape(rows, state_width), 'core', swap)  23 us
    pallas_call x1, Pallas kernels, block_terms(): pl.pallas_call(block_kernel, grid=(head_count // HEADS_PER_STEP,), in_spe...  14.1 us
    all_to_all x1, waiting for transfers between devices, per_device(): spread = lax.all_to_all(both, 'head', 0, 0, tiled=True)  7.54 us
    all_to_all x1, starting transfers between devices, per_device(): spread = lax.all_to_all(both, 'head', 0, 0, tiled=True)  6.89 us
    unnamed x45, local copies, waits for them, and re-layouts  6.67 us
    ppermute x5, starting transfers between devices, move(): return lax.ppermute(value, both, pairs)  6.61 us
    add x5, other arithmetic, join(): return jnp.exp(later_total)[:, None, None] * earlier + later  5.8 us
  transfers between devices with their start and end apart: 8, of which 7 were waited for; matrix products, arithmetic and copies ran while one was open for 6% of the time, Pallas kernels for 10%

profile of v11, /device:TPU:1, one launch (start us, length us, event | category | flops | bytes accessed | tf_op | source)
XLA Modules:
  0.0 142.4 jit_solution(7001613226103303356)
XLA Ops:
  0.6 0.8 select_reduce_fusion
  1.9 0.3 copy-done.20
  2.3 0.6 copy-done.21
  3.0 1.1 reduce-window.6
  4.7 0.6 copy-done.6
  5.5 0.3 copy.32
  5.8 2.5 %copy.29 = f32[512,512]{0,1:T(8,128)} copy(f32[512,512]{1,0:T(8,128)} %grad_ref.1) | data formatting | bytes 2097152 | tf_op args[6]
  8.5 2.6 %fusion.16 = (f32[512,512]{1,0:T(8,128)S(1)}, f32[512,512]{1,0:T(8,128)}) fusion(f32[512,512]{1,0:T(8,128)S(1)} %copy.32, f32[512,512]{1,0:T(8,128)} %param.7, f32[512,512]{1,0:T(8,128)S(1)} %copy.25), kind=kLoop, calls=%fused_computation.51 | loop fusion | flops 524288 | bytes 5242880 | tf_op jit(solution)/shard_map/mul | solution.py:181
  11.1 1.8 %fusion.18 = f32[512,128]{1,0:T(8,128)S(1)} fusion(f32[512,512]{1,0:T(8,128)S(1)} %get-tuple-element.17, f32[512,128]{1,0:T(8,128)S(1)} %copy-done.3), kind=kOutput, calls=%fused_computation.53 | convolution fusion | flops 402653184 | bytes 1572864 | tf_op jit(solution)/shard_map/tk,tn->kn/dot_general | solution.py:183
  12.9 1.4 bitcast_multiply_fusion
  14.3 1.0 broadcast_select_fusion.2
  15.5 0.6 copy-done.12
  16.0 4.9 %collective-permute-start = (f32[520,128]{1,0:T(8,128)S(1)}, f32[520,128]{1,0:T(8,128)S(1)}, u32[]{:S(2)}, u32[]{:S(2)}) collective-permute-start(f32[520,128]{1,0:T(8,128)S(1)} %get-tuple-element.26), channel_id=1, source_target_pairs={{16,32},{48,64},{32,16},{80,96},{64,48},{112,128},{96,80},{144,160... | collective-permute-start | bytes 798728 | tf_op jit(solution)/shard_map/ppermute | solution.py:147
  21.0 1.3 collective-permute-start.1
  22.3 2.8 %collective-permute-done = f32[520,128]{1,0:T(8,128)S(1)} collective-permute-done((f32[520,128]{1,0:T(8,128)S(1)}, f32[520,128]{1,0:T(8,128)S(1)}, u32[]{:S(2)}, u32[]{:S(2)}) %collective-permute-start) | collective-permute-done | bytes 266272 | tf_op jit(solution)/shard_map/ppermute | solution.py:147
  25.0 3.3 %collective-permute-done.1 = f32[520,128]{1,0:T(8,128)S(1)} collective-permute-done((f32[520,128]{1,0:T(8,128)S(1)}, f32[520,128]{1,0:T(8,128)S(1)}, u32[]{:S(2)}, u32[]{:S(2)}) %collective-permute-start.1) | collective-permute-done | bytes 266272 | tf_op jit(solution)/shard_map/ppermute | solution.py:138
  28.5 0.6 copy-done.17
  29.2 1.2 slice_add_fusion
  30.5 1.3 collective-permute-start.2
  31.8 6.3 %collective-permute-done.2 = f32[520,128]{1,0:T(8,128)S(1)} collective-permute-done((f32[520,128]{1,0:T(8,128)S(1)}, f32[520,128]{1,0:T(8,128)S(1)}, u32[]{:S(2)}, u32[]{:S(2)}) %collective-permute-start.2) | collective-permute-done | bytes 266272 | tf_op jit(solution)/shard_map/ppermute | solution.py:138
  38.1 0.7 copy-done.18
  39.1 1.1 fusion.6
  40.2 0.9 pad_maximum_fusion.4
  41.1 1.3 collective-permute-start.3
  42.5 10.4 %collective-permute-done.3 = f32[520,128]{1,0:T(8,128)S(1)} collective-permute-done((f32[520,128]{1,0:T(8,128)}, f32[520,128]{1,0:T(8,128)S(1)}, u32[]{:S(2)}, u32[]{:S(2)}) %collective-permute-start.3) | collective-permute-done | bytes 266272 | tf_op jit(solution)/shard_map/ppermute | solution.py:138
  53.1 0.6 copy-done.19
  53.7 1.2 fusion.5
  54.8 0.8 pad_maximum_fusion.5
  55.7 1.3 collective-permute-start.4
  57.1 14.8 %collective-permute-done.4 = f32[520,128]{1,0:T(8,128)} collective-permute-done((f32[520,128]{1,0:T(8,128)}, f32[520,128]{1,0:T(8,128)}, u32[]{:S(2)}, u32[]{:S(2)}) %collective-permute-start.4) | collective-permute-done | bytes 266272 | tf_op jit(solution)/shard_map/ppermute | solution.py:138
  71.9 0.8 slice_reduce_fusion.1
  72.7 1.1 fusion.4
  73.8 0.8 pad_maximum_fusion.6
  74.7 1.5 %collective-permute-start.5 = (f32[520,128]{1,0:T(8,128)}, f32[520,128]{1,0:T(8,128)}, u32[]{:S(2)}, u32[]{:S(2)}) collective-permute-start(f32[520,128]{1,0:T(8,128)} %pad_maximum_fusion.6), channel_id=1, source_target_pairs={{0,256},{32,288},{64,320},{96,352},{128,384},{160,416},{192,448},{... | collective-permute-start | bytes 798728 | tf_op jit(solution)/shard_map/ppermute | solution.py:138
  76.2 0.7 copy.26.cum_ref
  77.0 14.1 %shard_map.94 = (f32[512,512]{1,0:T(8,128)}, f32[512,512]{1,0:T(8,128)}) custom-call(f32[8,512]{1,0:T(8,128)} %copy.26.cum_ref, f32[512,8]{1,0:T(8,128)} %bitcast.47, f32[512,128]{1,0:T(8,128)} %proj_in_ref.1, f32[512,128]{1,0:T(8,128)} %proj_out_ref.1, f32[512,512]{1,0:T(8,128)} %get-tuple-element.18.in_ref, f32[512,512]{1,0:T(8,128)} %grad_ref.1), custom_call_target="tpu_custom_call" | custom-call | tf_op jit(solution)/shard_map/pallas_call | solution.py:73
  91.1 2.7 %fusion.20 = f32[512,128]{0,1:T(8,128)} fusion(f32[512,512]{1,0:T(8,128)} %get-tuple-element.6, f32[512,128]{1,0:T(8,128)S(1)} %copy-done.4), kind=kOutput, calls=%fused_computation.55 | convolution fusion | flops 402653184 | bytes 1572864 | tf_op jit(solution)/shard_map/st,sn->tn/dot_general | solution.py:193
  94.0 1.3 collective-permute-done.5
  95.3 1.3 multiply_add_fusion
  96.6 23.0 %collective-permute-start.6 = (f32[512,128]{1,0:T(8,128)S(1)}, f32[512,128]{1,0:T(8,128)S(1)}, u32[]{:S(2)}, u32[]{:S(2)}) collective-permute-start(f32[512,128]{1,0:T(8,128)S(1)} %get-tuple-element.9), channel_id=1, source_target_pairs={{0,16},{16,0},{1,17},{17,1},{2,18},{18,2},{3,19},{19,3},{4,20},{20... | collective-permute-start | bytes 786440 | tf_op jit(solution)/shard_map/ppermute | solution.py:157
  119.7 1.2 fusion.19
  121.0 0.8 convolution_add_fusion
  121.8 1.2 convolution_add_fusion.1
  123.0 1.0 copy.34
  124.1 6.9 %all-to-all-start = ((f32[16,32,256]{2,1,0:T(8,128)}), f32[16,32,256]{2,1,0:T(8,128)S(1)}, u32[]{:S(2)}, u32[]{:S(2)}) async-start(f32[16,32,256]{2,1,0:T(8,128)} %bitcast.50), calls=%async_computation | async-start | bytes 1048576 | tf_op jit(solution)/shard_map/all_to_all | solution.py:204
  131.0 3.3 %fusion.2 = f32[512,512]{1,0:T(8,128)} fusion(f32[512,512]{1,0:T(8,128)S(1)} %copy.25, f32[512,512]{1,0:T(8,128)} %get-tuple-element.5, f32[512,512]{1,0:T(8,128)S(1)} %copy.32, f32[512,128]{1,0:T(8,128)S(1)} %copy-done.5, f32[512,128]{1,0:T(8,128)S(1)} %copy-done.9, f32[512,128]{1,0:T(8,128)S(1)} %get-tuple-element.10, pred[]{:T(512)S(6)} %eq.19), kind=kOutput, calls=%fused_computation.3 | convolution fusion | flops 403505152 | bytes 4980737 | tf_op jit(solution)/shard_map/tn,kn->tk/dot_general | solution.py:199
  134.2 7.5 %all-to-all-done = f32[16,32,256]{2,1,0:T(8,128)S(1)} async-done(((f32[16,32,256]{2,1,0:T(8,128)}), f32[16,32,256]{2,1,0:T(8,128)S(1)}, u32[]{:S(2)}, u32[]{:S(2)}) %all-to-all-start) | async-done | bytes 524320 | tf_op jit(solution)/shard_map/all_to_all | solution.py:204
  141.8 0.6 fusion.17
  (82 shorter events, 3.1 us)
Async XLA Ops:
  1.6 0.7 copy-start.20
  2.3 0.7 copy-start.21
  4.5 0.7 copy-start.6
  8.5 2.6 %copy-start.3 = (f32[512,128]{1,0:T(8,128)S(1)}, f32[512,128]{1,0:T(8,128)}, u32[]{:S(2)}) copy-start(f32[512,128]{1,0:T(8,128)} %proj_in_ref.1) | copy-start | bytes 786436
  12.9 1.4 copy-start.13
  14.3 1.0 copy-start
  15.3 0.7 copy-start.12
  16.0 9.0 %collective-permute-start = (f32[520,128]{1,0:T(8,128)S(1)}, f32[520,128]{1,0:T(8,128)S(1)}, u32[]{:S(2)}, u32[]{:S(2)}) collective-permute-start(f32[520,128]{1,0:T(8,128)S(1)} %get-tuple-element.26), channel_id=1, source_target_pairs={{16,32},{48,64},{32,16},{80,96},{64,48},{112,128},{96,80},{144,160... | collective-permute-start | bytes 798728 | tf_op jit(solution)/shard_map/ppermute | solution.py:147
  21.0 7.3 %collective-permute-start.1 = (f32[520,128]{1,0:T(8,128)S(1)}, f32[520,128]{1,0:T(8,128)S(1)}, u32[]{:S(2)}, u32[]{:S(2)}) collective-permute-start(f32[520,128]{1,0:T(8,128)S(1)} %get-tuple-element.25), channel_id=1, source_target_pairs={{0,32},{32,64},{48,16},{64,96},{80,48},{96,128},{112,80},{128,160}... | collective-permute-start | bytes 798728 | tf_op jit(solution)/shard_map/ppermute | solution.py:138
  25.0 3.3 %copy-start.16 = (f32[520,128]{1,0:T(8,128)}, f32[520,128]{1,0:T(8,128)S(1)}, u32[]{:S(2)}) copy-start(f32[520,128]{1,0:T(8,128)S(1)} %collective-permute-done) | copy-start | bytes 798724
  28.3 0.7 copy-start.17
  30.5 7.6 %collective-permute-start.2 = (f32[520,128]{1,0:T(8,128)S(1)}, f32[520,128]{1,0:T(8,128)S(1)}, u32[]{:S(2)}, u32[]{:S(2)}) collective-permute-start(f32[520,128]{1,0:T(8,128)S(1)} %pad_maximum_fusion.3), channel_id=1, source_target_pairs={{0,32},{32,64},{48,16},{64,96},{80,48},{96,128},{112,80},{128,160}... | collective-permute-start | bytes 798728 | tf_op jit(solution)/shard_map/ppermute | solution.py:138
  38.1 0.7 copy-start.18
  40.2 0.9 copy-start.11
  41.1 11.8 %collective-permute-start.3 = (f32[520,128]{1,0:T(8,128)}, f32[520,128]{1,0:T(8,128)S(1)}, u32[]{:S(2)}, u32[]{:S(2)}) collective-permute-start(f32[520,128]{1,0:T(8,128)} %pad_maximum_fusion.4), channel_id=1, source_target_pairs={{0,64},{32,96},{64,128},{80,16},{96,160},{112,48},{128,192},{144,8... | collective-permute-start | bytes 798728 | tf_op jit(solution)/shard_map/ppermute | solution.py:138
  52.9 0.7 copy-start.19
  55.7 16.2 %collective-permute-start.4 = (f32[520,128]{1,0:T(8,128)}, f32[520,128]{1,0:T(8,128)}, u32[]{:S(2)}, u32[]{:S(2)}) collective-permute-start(f32[520,128]{1,0:T(8,128)} %pad_maximum_fusion.5), channel_id=1, source_target_pairs={{0,128},{32,160},{64,192},{96,224},{128,256},{144,16},{160,288},{1... | collective-permute-start | bytes 798728 | tf_op jit(solution)/shard_map/ppermute | solution.py:138
  73.8 0.9 copy-start.10
  73.8 2.3 %copy-start.7 = (f32[8,4,128]{0,2,1:T(8,128)S(1)}, f32[8,4,128]{0,2,1:T(8,128)}, u32[]{:S(2)}) copy-start(f32[8,4,128]{0,2,1:T(8,128)} %copy-done.6) | copy-start | bytes 49156
  74.7 20.6 %collective-permute-start.5 = (f32[520,128]{1,0:T(8,128)}, f32[520,128]{1,0:T(8,128)}, u32[]{:S(2)}, u32[]{:S(2)}) collective-permute-start(f32[520,128]{1,0:T(8,128)} %pad_maximum_fusion.6), channel_id=1, source_target_pairs={{0,256},{32,288},{64,320},{96,352},{128,384},{160,416},{192,448},{... | collective-permute-start | bytes 798728 | tf_op jit(solution)/shard_map/ppermute | solution.py:138
  77.0 14.1 %copy-start.4 = (f32[512,128]{1,0:T(8,128)S(1)}, f32[512,128]{1,0:T(8,128)}, u32[]{:S(2)}) copy-start(f32[512,128]{1,0:T(8,128)} %proj_in_ref.1) | copy-start | bytes 786436
  94.0 25.6 %copy-start.2 = (f32[512,512]{1,0:T(8,128)S(1)}, f32[512,512]{1,0:T(8,128)}, u32[]{:S(2)}) copy-start(f32[512,512]{1,0:T(8,128)} %get-tuple-element.6) | copy-start | bytes 3145732
  94.0 25.7 %copy-start.14 = (f32[512,128]{1,0:T(8,128)S(1)}, f32[512,128]{1,0:T(8,128)}, u32[]{:S(2)}) copy-start(f32[512,128]{1,0:T(8,128)} %proj_out_ref.1) | copy-start | bytes 786436
  96.6 24.3 %copy-start.1 = (f32[512,512]{0,1:T(8,128)S(1)}, f32[512,512]{0,1:T(8,128)}, u32[]{:S(2)}) copy-start(f32[512,512]{0,1:T(8,128)} %copy-done) | copy-start | bytes 3145732
  96.6 24.3 %copy-start.15 = (f32[512,128]{0,1:T(8,128)S(1)}, f32[512,128]{0,1:T(8,128)}, u32[]{:S(2)}) copy-start(f32[512,128]{0,1:T(8,128)} %fusion.20) | copy-start | bytes 786436
  96.6 24.3 %collective-permute-start.6 = (f32[512,128]{1,0:T(8,128)S(1)}, f32[512,128]{1,0:T(8,128)S(1)}, u32[]{:S(2)}, u32[]{:S(2)}) collective-permute-start(f32[512,128]{1,0:T(8,128)S(1)} %get-tuple-element.9), channel_id=1, source_target_pairs={{0,16},{16,0},{1,17},{17,1},{2,18},{18,2},{3,19},{19,3},{4,20},{20... | collective-permute-start | bytes 786440 | tf_op jit(solution)/shard_map/ppermute | solution.py:157
  120.9 0.8 copy-start.8
  124.0 6.9 %copy-start.5 = (f32[512,128]{1,0:T(8,128)S(1)}, f32[512,128]{1,0:T(8,128)}, u32[]{:S(2)}) copy-start(f32[512,128]{1,0:T(8,128)} %proj_in_ref.1) | copy-start | bytes 786436
  124.0 6.9 %copy-start.9 = (f32[512,128]{1,0:T(8,128)S(1)}, f32[512,128]{1,0:T(8,128)}, u32[]{:S(2)}) copy-start(f32[512,128]{1,0:T(8,128)} %copy-done.8) | copy-start | bytes 786436
  124.1 17.7 %all-to-all-start = ((f32[16,32,256]{2,1,0:T(8,128)}), f32[16,32,256]{2,1,0:T(8,128)S(1)}, u32[]{:S(2)}, u32[]{:S(2)}) async-start(f32[16,32,256]{2,1,0:T(8,128)} %bitcast.50), calls=%async_computation | async-start | bytes 1048576 | tf_op jit(solution)/shard_map/all_to_all | solution.py:204

commit v12 on v11

--- a/solution.py
+++ b/solution.py
@@ -148,9 +148,12 @@
     running = packed(join(near_state, far_state, far_t), near_t + far_t)
     hop = 1
     while hop < chips:
-        got_state, got_t = unpacked(move(running, hop))
-        run_state, run_t = unpacked(running)
-        running = packed(join(got_state, run_state, run_t), got_t + run_t)
+        got = move(running, hop)
+        run_t = running[rows:rows + head_count, 0]
+        scale = jnp.concatenate(
+            [jnp.repeat(jnp.exp(run_t), width), jnp.ones((running.shape[0] - rows,), jnp.float32)]
+        )
+        running = scale[:, None] * got + running
         hop *= 2
     prefix, unused = unpacked(running)
     joined = join(prefix, mine, total)

time: 143 us -> 135 us (0.944)
  starting transfers between devices: 41.4 us -> 25.7 us
  waiting for transfers between devices: 46.4 us -> 53.6 us
    ppermute x1, starting transfers between devices: 23 us -> 7.32 us  [chip_scans(): back = lax.ppermute(joined.reshape(rows, state_width), 'core', swap)]
    ppermute x5, waiting for transfers between devices: 36 us -> 43.3 us  [move(): return lax.ppermute(value, both, pairs)]
    add x0 -> x3, other arithmetic: none -> 4.94 us  [chip_scans(): running = scale[:, None] * got + running]
    add x5 -> x2, other arithmetic: 5.8 us -> 2.4 us  [join(): return jnp.exp(later_total)[:, None, None] * earlier + later]
    concatenate x5 -> x2, other arithmetic: 2.82 us -> 0.97 us  [packed(): jnp.concatenate([state.reshape(rows, state_width), pack_total(tot, state_...]
    exp x0 -> x4, local copies, waits for them, and re-layouts: none -> 1.73 us  [chip_scans(): jnp.exp(run_t)]
    unnamed x45 -> x37, local copies, waits for them, and re-layouts: 6.67 us -> 5.43 us
  transfers between devices with their start and end apart: 8 -> 8, of which waited for: 7 -> 6; matrix products, arithmetic and copies ran while one was open for 6% -> 8% of each run, Pallas kernels for 10% -> 11%
where the time goes in v12:
time: 135 us; the launch traced here: 134 us
  waiting for transfers between devices  53.6 us (40%)
  starting transfers between devices  25.7 us (19%)
  other arithmetic  14.7 us (11%)
  Pallas kernels  14.1 us (10%)
  local copies, waits for them, and re-layouts  12.5 us (9%)
  matrix products  12.1 us (9%)
    ppermute x5, waiting for transfers between devices, move(): return lax.ppermute(value, both, pairs)  43.3 us
    pallas_call x1, Pallas kernels, block_terms(): pl.pallas_call(block_kernel, grid=(head_count // HEADS_PER_STEP,), in_spe...  14.1 us
    all_to_all x1, waiting for transfers between devices, per_device(): spread = lax.all_to_all(both, 'head', 0, 0, tiled=True)  7.54 us
    ppermute x1, starting transfers between devices, chip_scans(): back = lax.ppermute(joined.reshape(rows, state_width), 'core', swap)  7.32 us
    all_to_all x1, starting transfers between devices, per_device(): spread = lax.all_to_all(both, 'head', 0, 0, tiled=True)  6.88 us
    ppermute x5, starting transfers between devices, move(): return lax.ppermute(value, both, pairs)  6.61 us
    unnamed x37, local copies, waits for them, and re-layouts  5.43 us
    add x3, other arithmetic, chip_scans(): running = scale[:, None] * got + running  4.94 us
  transfers between devices with their start and end apart: 8, of which 6 were waited for; matrix products, arithmetic and copies ran while one was open for 8% of the time, Pallas kernels for 11%

profile of v12, /device:TPU:1, one launch (start us, length us, event | category | flops | bytes accessed | tf_op | source)
XLA Modules:
  0.0 133.7 jit_solution(902669792015303971)
XLA Ops:
  0.6 0.8 select_reduce_fusion
  1.6 0.3 copy.25
  1.9 0.3 copy-done.16
  2.3 0.6 copy-done.17
  3.0 1.1 reduce-window.6
  4.1 0.2 slice_reduce_fusion
  4.7 0.6 copy-done.6
  5.5 0.3 copy.32
  5.8 2.5 %copy.30 = f32[512,512]{0,1:T(8,128)} copy(f32[512,512]{1,0:T(8,128)} %grad_ref.1) | data formatting | bytes 2097152 | tf_op args[6]
  8.5 2.6 %fusion.11 = (f32[512,512]{1,0:T(8,128)S(1)}, f32[512,512]{1,0:T(8,128)}) fusion(f32[512,512]{1,0:T(8,128)S(1)} %copy.32, f32[512,512]{1,0:T(8,128)} %param.7, f32[512,512]{1,0:T(8,128)S(1)} %copy.25), kind=kLoop, calls=%fused_computation.46 | loop fusion | flops 524288 | bytes 5242880 | tf_op jit(solution)/shard_map/mul | solution.py:184
  11.1 1.8 %fusion.13 = f32[512,128]{1,0:T(8,128)S(1)} fusion(f32[512,512]{1,0:T(8,128)S(1)} %get-tuple-element.11, f32[512,128]{1,0:T(8,128)S(1)} %copy-done.3), kind=kOutput, calls=%fused_computation.48 | convolution fusion | flops 402653184 | bytes 1572864 | tf_op jit(solution)/shard_map/tk,tn->kn/dot_general | solution.py:186
  12.9 1.4 %bitcast_multiply_fusion = f32[512,512]{0,1:T(8,128)S(1)} fusion(f32[512,512]{0,1:T(8,128)} %copy.30, f32[512,8]{0,1:T(8,128)S(1)} %copy.29), kind=kLoop, calls=%fused_computation.6 | loop fusion | flops 262144 | bytes 2113536 | tf_op jit(solution)/shard_map/mul | solution.py:185
  14.3 1.0 broadcast_select_fusion.1
  15.4 0.6 copy-done.11
  16.0 4.9 %collective-permute-start.1 = (f32[520,128]{1,0:T(8,128)S(1)}, f32[520,128]{1,0:T(8,128)S(1)}, u32[]{:S(2)}, u32[]{:S(2)}) collective-permute-start(f32[520,128]{1,0:T(8,128)S(1)} %get-tuple-element.20), channel_id=1, source_target_pairs={{16,32},{48,64},{32,16},{80,96},{64,48},{112,128},{96,80},{144,160... | collective-permute-start | bytes 798728 | tf_op jit(solution)/shard_map/ppermute | solution.py:147
  20.9 1.3 collective-permute-start
  22.2 2.8 %collective-permute-done.1 = f32[520,128]{1,0:T(8,128)S(1)} collective-permute-done((f32[520,128]{1,0:T(8,128)S(1)}, f32[520,128]{1,0:T(8,128)S(1)}, u32[]{:S(2)}, u32[]{:S(2)}) %collective-permute-start.1) | collective-permute-done | bytes 266272 | tf_op jit(solution)/shard_map/ppermute | solution.py:147
  25.0 3.3 %collective-permute-done = f32[520,128]{1,0:T(8,128)S(1)} collective-permute-done((f32[520,128]{1,0:T(8,128)S(1)}, f32[520,128]{1,0:T(8,128)S(1)}, u32[]{:S(2)}, u32[]{:S(2)}) %collective-permute-start) | collective-permute-done | bytes 266272 | tf_op jit(solution)/shard_map/ppermute | solution.py:138
  28.3 0.7 copy-done.15
  29.0 0.1 fusion.9
  29.3 1.1 slice_add_fusion.1
  30.4 0.8 pad_maximum_fusion.3
  31.2 1.3 collective-permute-start.2
  32.7 6.5 %collective-permute-done.2 = f32[520,128]{1,0:T(8,128)} collective-permute-done((f32[520,128]{1,0:T(8,128)}, f32[520,128]{1,0:T(8,128)}, u32[]{:S(2)}, u32[]{:S(2)}) %collective-permute-start.2) | collective-permute-done | bytes 266272 | tf_op jit(solution)/shard_map/ppermute | solution.py:138
  39.2 1.9 %multiply_add_fusion.2 = f32[520,128]{1,0:T(8,128)} fusion(f32[520,128]{1,0:T(8,128)} %collective-permute-done.2, f32[520]{0:T(1024)S(1)} %concatenate.26, f32[520]{0:T(1024)S(1)} %pad.7.clone, f32[512,128]{1,0:T(8,128)} %copy-done.10), kind=kLoop, calls=%fused_computation.13 | loop fusion | flops 199680 | bytes 798784 | tf_op jit(solution)/shard_map/add | solution.py:156
  41.1 1.5 %collective-permute-start.3 = (f32[520,128]{1,0:T(8,128)}, f32[520,128]{1,0:T(8,128)}, u32[]{:S(2)}, u32[]{:S(2)}) collective-permute-start(f32[520,128]{1,0:T(8,128)} %multiply_add_fusion.2), channel_id=1, source_target_pairs={{0,64},{32,96},{64,128},{80,16},{96,160},{112,48},{128,192},{144,8... | collective-permute-start | bytes 798728 | tf_op jit(solution)/shard_map/ppermute | solution.py:138
  42.6 0.7 copy.26.cum_ref
  43.3 14.1 %shard_map.94 = (f32[512,512]{1,0:T(8,128)}, f32[512,512]{1,0:T(8,128)}) custom-call(f32[8,512]{1,0:T(8,128)} %copy.26.cum_ref, f32[512,8]{1,0:T(8,128)} %bitcast.47, f32[512,128]{1,0:T(8,128)} %proj_in_ref.1, f32[512,128]{1,0:T(8,128)} %proj_out_ref.1, f32[512,512]{1,0:T(8,128)} %get-tuple-element.12.in_ref, f32[512,512]{1,0:T(8,128)} %grad_ref.1), custom_call_target="tpu_custom_call" | custom-call | tf_op jit(solution)/shard_map/pallas_call | solution.py:73
  57.4 0.8 fusion.8
  58.3 1.2 multiply_add_fusion.1
  59.5 1.3 collective-permute-start.4
  60.9 2.7 %fusion.15 = f32[512,128]{0,1:T(8,128)} fusion(f32[512,512]{1,0:T(8,128)} %get-tuple-element.6, f32[512,128]{1,0:T(8,128)S(1)} %copy-done.4), kind=kOutput, calls=%fused_computation.50 | convolution fusion | flops 402653184 | bytes 1572864 | tf_op jit(solution)/shard_map/st,sn->tn/dot_general | solution.py:196
  63.9 14.8 %collective-permute-done.4 = f32[520,128]{1,0:T(8,128)} collective-permute-done((f32[520,128]{1,0:T(8,128)S(1)}, f32[520,128]{1,0:T(8,128)}, u32[]{:S(2)}, u32[]{:S(2)}) %collective-permute-start.4) | collective-permute-done | bytes 266272 | tf_op jit(solution)/shard_map/ppermute | solution.py:138
  78.6 1.8 %multiply_add_fusion = f32[520,128]{1,0:T(8,128)} fusion(f32[520,128]{1,0:T(8,128)S(1)} %multiply_add_fusion.1, f32[520,128]{1,0:T(8,128)} %collective-permute-done.4, f32[520]{0:T(1024)S(1)} %concatenate.29), kind=kLoop, calls=%fused_computation.11 | loop fusion | flops 133120 | bytes 800800 | tf_op jit(solution)/shard_map/add | solution.py:156
  80.4 1.3 collective-permute-start.5
  81.7 0.7 fusion.10
  82.6 0.8 fusion.6
  83.5 18.8 %collective-permute-done.5 = f32[520,128]{1,0:T(8,128)} collective-permute-done((f32[520,128]{1,0:T(8,128)}, f32[520,128]{1,0:T(8,128)}, u32[]{:S(2)}, u32[]{:S(2)}) %collective-permute-start.5) | collective-permute-done | bytes 266272 | tf_op jit(solution)/shard_map/ppermute | solution.py:138
  102.3 1.3 multiply_add_fusion.3
  103.6 7.3 %collective-permute-start.6 = (f32[512,128]{1,0:T(8,128)S(1)}, f32[512,128]{1,0:T(8,128)S(1)}, u32[]{:S(2)}, u32[]{:S(2)}) collective-permute-start(f32[512,128]{1,0:T(8,128)S(1)} %get-tuple-element.9), channel_id=1, source_target_pairs={{0,16},{16,0},{1,17},{17,1},{2,18},{18,2},{3,19},{19,3},{4,20},{20... | collective-permute-start | bytes 786440 | tf_op jit(solution)/shard_map/ppermute | solution.py:160
  111.0 1.2 fusion.14
  112.3 0.8 convolution_add_fusion
  113.1 1.2 convolution_add_fusion.1
  114.3 1.0 copy.34
  115.3 6.9 %all-to-all-start = ((f32[16,32,256]{2,1,0:T(8,128)}), f32[16,32,256]{2,1,0:T(8,128)S(1)}, u32[]{:S(2)}, u32[]{:S(2)}) async-start(f32[16,32,256]{2,1,0:T(8,128)} %bitcast.50), calls=%async_computation | async-start | bytes 1048576 | tf_op jit(solution)/shard_map/all_to_all | solution.py:207
  122.3 3.3 %fusion.2 = f32[512,512]{1,0:T(8,128)} fusion(f32[512,512]{1,0:T(8,128)S(1)} %copy.25, f32[512,512]{1,0:T(8,128)} %get-tuple-element.5, f32[512,512]{1,0:T(8,128)S(1)} %copy.32, f32[512,128]{1,0:T(8,128)S(1)} %copy-done.5, f32[512,128]{1,0:T(8,128)S(1)} %copy-done.9, f32[512,128]{1,0:T(8,128)S(1)} %get-tuple-element.10, pred[]{:T(512)S(6)} %eq.19), kind=kOutput, calls=%fused_computation.3 | convolution fusion | flops 403505152 | bytes 4980737 | tf_op jit(solution)/shard_map/tn,kn->tk/dot_general | solution.py:202
  125.5 7.5 %all-to-all-done = f32[16,32,256]{2,1,0:T(8,128)S(1)} async-done(((f32[16,32,256]{2,1,0:T(8,128)}), f32[16,32,256]{2,1,0:T(8,128)S(1)}, u32[]{:S(2)}, u32[]{:S(2)}) %all-to-all-start) | async-done | bytes 524320 | tf_op jit(solution)/shard_map/all_to_all | solution.py:207
  133.1 0.6 fusion.12
  (70 shorter events, 2.2 us)
Async XLA Ops:
  1.6 0.7 copy-start.16
  2.3 0.7 copy-start.17
  4.5 0.7 copy-start.6
  8.5 2.6 %copy-start.3 = (f32[512,128]{1,0:T(8,128)S(1)}, f32[512,128]{1,0:T(8,128)}, u32[]{:S(2)}) copy-start(f32[512,128]{1,0:T(8,128)} %proj_in_ref.1) | copy-start | bytes 786436
  12.9 1.4 %copy-start.12 = (f32[512,128]{1,0:T(8,128)S(1)}, f32[512,128]{1,0:T(8,128)}, u32[]{:S(2)}) copy-start(f32[512,128]{1,0:T(8,128)} %proj_out_ref.1) | copy-start | bytes 786436
  14.3 1.0 copy-start
  15.3 0.7 copy-start.11
  16.0 9.0 %collective-permute-start.1 = (f32[520,128]{1,0:T(8,128)S(1)}, f32[520,128]{1,0:T(8,128)S(1)}, u32[]{:S(2)}, u32[]{:S(2)}) collective-permute-start(f32[520,128]{1,0:T(8,128)S(1)} %get-tuple-element.20), channel_id=1, source_target_pairs={{16,32},{48,64},{32,16},{80,96},{64,48},{112,128},{96,80},{144,160... | collective-permute-start | bytes 798728 | tf_op jit(solution)/shard_map/ppermute | solution.py:147
  20.9 7.3 %collective-permute-start = (f32[520,128]{1,0:T(8,128)S(1)}, f32[520,128]{1,0:T(8,128)S(1)}, u32[]{:S(2)}, u32[]{:S(2)}) collective-permute-start(f32[520,128]{1,0:T(8,128)S(1)} %get-tuple-element.19), channel_id=1, source_target_pairs={{0,32},{32,64},{48,16},{64,96},{80,48},{96,128},{112,80},{128,160}... | collective-permute-start | bytes 798728 | tf_op jit(solution)/shard_map/ppermute | solution.py:138
  28.3 0.7 copy-start.15
  30.4 0.8 copy-start.10
  31.2 7.9 %collective-permute-start.2 = (f32[520,128]{1,0:T(8,128)}, f32[520,128]{1,0:T(8,128)}, u32[]{:S(2)}, u32[]{:S(2)}) collective-permute-start(f32[520,128]{1,0:T(8,128)} %pad_maximum_fusion.3), channel_id=1, source_target_pairs={{0,32},{32,64},{48,16},{64,96},{80,48},{96,128},{112,80},{128,160}... | collective-permute-start | bytes 798728 | tf_op jit(solution)/shard_map/ppermute | solution.py:138
  32.7 9.9 %copy-start.7 = (f32[8,4,128]{0,2,1:T(8,128)S(1)}, f32[8,4,128]{0,2,1:T(8,128)}, u32[]{:S(2)}) copy-start(f32[8,4,128]{0,2,1:T(8,128)} %copy-done.6) | copy-start | bytes 49156
  41.1 17.2 %collective-permute-start.3 = (f32[520,128]{1,0:T(8,128)}, f32[520,128]{1,0:T(8,128)}, u32[]{:S(2)}, u32[]{:S(2)}) collective-permute-start(f32[520,128]{1,0:T(8,128)} %multiply_add_fusion.2), channel_id=1, source_target_pairs={{0,64},{32,96},{64,128},{80,16},{96,160},{112,48},{128,192},{144,8... | collective-permute-start | bytes 798728 | tf_op jit(solution)/shard_map/ppermute | solution.py:138
  58.3 2.5 %copy-start.4 = (f32[512,128]{1,0:T(8,128)S(1)}, f32[512,128]{1,0:T(8,128)}, u32[]{:S(2)}) copy-start(f32[512,128]{1,0:T(8,128)} %proj_in_ref.1) | copy-start | bytes 786436
  59.5 19.1 %collective-permute-start.4 = (f32[520,128]{1,0:T(8,128)S(1)}, f32[520,128]{1,0:T(8,128)}, u32[]{:S(2)}, u32[]{:S(2)}) collective-permute-start(f32[520,128]{1,0:T(8,128)S(1)} %multiply_add_fusion.1), channel_id=1, source_target_pairs={{0,128},{32,160},{64,192},{96,224},{128,256},{144,16},{160,288},{1... | collective-permute-start | bytes 798728 | tf_op jit(solution)/shard_map/ppermute | solution.py:138
  80.4 21.9 %collective-permute-start.5 = (f32[520,128]{1,0:T(8,128)}, f32[520,128]{1,0:T(8,128)}, u32[]{:S(2)}, u32[]{:S(2)}) collective-permute-start(f32[520,128]{1,0:T(8,128)} %multiply_add_fusion), channel_id=1, source_target_pairs={{0,256},{32,288},{64,320},{96,352},{128,384},{160,416},{192,448},{... | collective-permute-start | bytes 798728 | tf_op jit(solution)/shard_map/ppermute | solution.py:138
  83.5 27.5 %copy-start.2 = (f32[512,512]{1,0:T(8,128)S(1)}, f32[512,512]{1,0:T(8,128)}, u32[]{:S(2)}) copy-start(f32[512,512]{1,0:T(8,128)} %get-tuple-element.6) | copy-start | bytes 3145732
  83.5 27.5 %copy-start.13 = (f32[512,128]{1,0:T(8,128)S(1)}, f32[512,128]{1,0:T(8,128)}, u32[]{:S(2)}) copy-start(f32[512,128]{1,0:T(8,128)} %proj_out_ref.1) | copy-start | bytes 786436
  103.6 8.6 %copy-start.1 = (f32[512,512]{0,1:T(8,128)S(1)}, f32[512,512]{0,1:T(8,128)}, u32[]{:S(2)}) copy-start(f32[512,512]{0,1:T(8,128)} %copy-done) | copy-start | bytes 3145732
  103.6 8.6 %copy-start.14 = (f32[512,128]{0,1:T(8,128)S(1)}, f32[512,128]{0,1:T(8,128)}, u32[]{:S(2)}) copy-start(f32[512,128]{0,1:T(8,128)} %fusion.15) | copy-start | bytes 786436
  103.6 8.6 %collective-permute-start.6 = (f32[512,128]{1,0:T(8,128)S(1)}, f32[512,128]{1,0:T(8,128)S(1)}, u32[]{:S(2)}, u32[]{:S(2)}) collective-permute-start(f32[512,128]{1,0:T(8,128)S(1)} %get-tuple-element.9), channel_id=1, source_target_pairs={{0,16},{16,0},{1,17},{17,1},{2,18},{18,2},{3,19},{19,3},{4,20},{20... | collective-permute-start | bytes 786440 | tf_op jit(solution)/shard_map/ppermute | solution.py:160
  112.2 0.8 copy-start.8
  115.3 6.9 %copy-start.5 = (f32[512,128]{1,0:T(8,128)S(1)}, f32[512,128]{1,0:T(8,128)}, u32[]{:S(2)}) copy-start(f32[512,128]{1,0:T(8,128)} %proj_in_ref.1) | copy-start | bytes 786436
  115.3 6.9 %copy-start.9 = (f32[512,128]{1,0:T(8,128)S(1)}, f32[512,128]{1,0:T(8,128)}, u32[]{:S(2)}) copy-start(f32[512,128]{1,0:T(8,128)} %copy-done.8) | copy-start | bytes 786436
  115.3 17.7 %all-to-all-start = ((f32[16,32,256]{2,1,0:T(8,128)}), f32[16,32,256]{2,1,0:T(8,128)S(1)}, u32[]{:S(2)}, u32[]{:S(2)}) async-start(f32[16,32,256]{2,1,0:T(8,128)} %bitcast.50), calls=%async_computation | async-start | bytes 1048576 | tf_op jit(solution)/shard_map/all_to_all | solution.py:207

commit v13 on v12

--- a/solution.py
+++ b/solution.py
@@ -143,9 +143,13 @@
             cross.append((2 * z + 1, 2 * (z + 1)))
         if z - 1 >= 0:
             cross.append((2 * z, 2 * (z - 1) + 1))
-    near_state, near_t = unpacked(move(packed(mine, total), 1))
-    far_state, far_t = unpacked(lax.ppermute(packed(other, total), both, cross))
-    running = packed(join(near_state, far_state, far_t), near_t + far_t)
+    near = move(packed(mine, total), 1)
+    far = lax.ppermute(packed(other, total), both, cross)
+    far_t = far[rows:rows + head_count, 0]
+    first_scale = jnp.concatenate(
+        [jnp.repeat(jnp.exp(far_t), width), jnp.ones((far.shape[0] - rows,), jnp.float32)]
+    )
+    running = first_scale[:, None] * near + far
     hop = 1
     while hop < chips:
         got = move(running, hop)

time: 135 us -> 135 us (level)
    add x1, other arithmetic: 0.14 us -> 1.79 us  [chip_scans(): running = first_scale[:, None] * near + far]
    unnamed x37 -> x33, local copies, waits for them, and re-layouts: 5.43 us -> 4.19 us
  transfers between devices with their start and end apart: 8 -> 8, of which waited for: 6 -> 6; matrix products, arithmetic and copies ran while one was open for 8% -> 9% of each run, Pallas kernels for 11% -> 10%
where the time goes in v13:
time: 135 us; the launch traced here: 134 us
  waiting for transfers between devices  53 us (39%)
  starting transfers between devices  26.8 us (20%)
  other arithmetic  15.1 us (11%)
  Pallas kernels  14.1 us (10%)
  local copies, waits for them, and re-layouts  12.1 us (9%)
  matrix products  12.1 us (9%)
    ppermute x5, waiting for transfers between devices, move(): return lax.ppermute(value, both, pairs)  42.7 us
    pallas_call x1, Pallas kernels, block_terms(): pl.pallas_call(block_kernel, grid=(head_count // HEADS_PER_STEP,), in_spe...  14.1 us
    ppermute x1, starting transfers between devices, chip_scans(): back = lax.ppermute(joined.reshape(rows, state_width), 'core', swap)  8.37 us
    all_to_all x1, waiting for transfers between devices, per_device(): spread = lax.all_to_all(both, 'head', 0, 0, tiled=True)  7.55 us
    all_to_all x1, starting transfers between devices, per_device(): spread = lax.all_to_all(both, 'head', 0, 0, tiled=True)  6.9 us
    ppermute x5, starting transfers between devices, move(): return lax.ppermute(value, both, pairs)  6.6 us
    ppermute x1, starting transfers between devices, chip_scans(): far = lax.ppermute(packed(other, total), both, cross)  4.92 us
    add x3, other arithmetic, chip_scans(): running = scale[:, None] * got + running  4.87 us
  transfers between devices with their start and end apart: 8, of which 6 were waited for; matrix products, arithmetic and copies ran while one was open for 9% of the time, Pallas kernels for 10%

profile of v13, /device:TPU:1, one launch (start us, length us, event | category | flops | bytes accessed | tf_op | source)
XLA Modules:
  0.0 134.2 jit_solution(1979020229826892770)
XLA Ops:
  0.6 0.8 select_reduce_fusion
  1.6 0.3 copy.25
  1.9 0.3 copy-done.14
  2.3 0.6 copy-done.15
  3.0 1.1 reduce-window.6
  4.1 0.2 slice_reduce_fusion
  4.4 0.1 copy.24
  4.7 0.6 copy-done.6
  5.4 0.1 broadcast_in_dim.33
  5.5 0.3 copy.32
  5.8 2.5 %copy.29 = f32[512,512]{0,1:T(8,128)} copy(f32[512,512]{1,0:T(8,128)} %grad_ref.1) | data formatting | bytes 2097152 | tf_op args[6]
  8.5 2.6 %fusion.12 = (f32[512,512]{1,0:T(8,128)S(1)}, f32[512,512]{1,0:T(8,128)}) fusion(f32[512,512]{1,0:T(8,128)S(1)} %copy.32, f32[512,512]{1,0:T(8,128)} %param.7, f32[512,512]{1,0:T(8,128)S(1)} %copy.25), kind=kLoop, calls=%fused_computation.45 | loop fusion | flops 524288 | bytes 5242880 | tf_op jit(solution)/shard_map/mul | solution.py:188
  11.1 1.8 %fusion.14 = f32[512,128]{1,0:T(8,128)S(1)} fusion(f32[512,512]{1,0:T(8,128)S(1)} %get-tuple-element.9, f32[512,128]{1,0:T(8,128)S(1)} %copy-done.3), kind=kOutput, calls=%fused_computation.47 | convolution fusion | flops 402653184 | bytes 1572864 | tf_op jit(solution)/shard_map/tk,tn->kn/dot_general | solution.py:190
  12.9 1.4 %bitcast_multiply_fusion = f32[512,512]{0,1:T(8,128)S(1)} fusion(f32[512,512]{0,1:T(8,128)} %copy.29, f32[512,8]{0,1:T(8,128)S(1)} %copy.28), kind=kLoop, calls=%fused_computation.6 | loop fusion | flops 262144 | bytes 2113536 | tf_op jit(solution)/shard_map/mul | solution.py:189
  14.3 1.0 broadcast_select_fusion.2
  15.3 0.8 pad_maximum_fusion.2
  16.2 4.9 %collective-permute-start = (f32[520,128]{1,0:T(8,128)S(1)}, f32[520,128]{1,0:T(8,128)S(1)}, u32[]{:S(2)}, u32[]{:S(2)}) collective-permute-start(f32[520,128]{1,0:T(8,128)S(1)} %get-tuple-element.18), channel_id=1, source_target_pairs={{16,32},{48,64},{32,16},{80,96},{64,48},{112,128},{96,80},{144,160... | collective-permute-start | bytes 798728 | tf_op jit(solution)/shard_map/ppermute | solution.py:147
  21.1 1.3 collective-permute-start.1
  22.4 2.8 %collective-permute-done = f32[520,128]{1,0:T(8,128)S(1)} collective-permute-done((f32[520,128]{1,0:T(8,128)S(1)}, f32[520,128]{1,0:T(8,128)S(1)}, u32[]{:S(2)}, u32[]{:S(2)}) %collective-permute-start) | collective-permute-done | bytes 266272 | tf_op jit(solution)/shard_map/ppermute | solution.py:147
  25.4 3.3 %collective-permute-done.1 = f32[520,128]{1,0:T(8,128)} collective-permute-done((f32[520,128]{1,0:T(8,128)}, f32[520,128]{1,0:T(8,128)}, u32[]{:S(2)}, u32[]{:S(2)}) %collective-permute-start.1) | collective-permute-done | bytes 266272 | tf_op jit(solution)/shard_map/ppermute | solution.py:138
  28.8 1.8 %multiply_add_fusion.3 = f32[520,128]{1,0:T(8,128)} fusion(f32[520,128]{1,0:T(8,128)S(1)} %collective-permute-done, f32[520,128]{1,0:T(8,128)} %collective-permute-done.1, f32[520]{0:T(1024)S(1)} %concatenate.25), kind=kLoop, calls=%fused_computation.13 | loop fusion | flops 133120 | bytes 800800 | tf_op jit(solution)/shard_map/add | solution.py:152
  30.5 1.3 collective-permute-start.2
  31.8 0.8 fusion.9
  32.8 5.7 %collective-permute-done.2 = f32[520,128]{1,0:T(8,128)} collective-permute-done((f32[520,128]{1,0:T(8,128)}, f32[520,128]{1,0:T(8,128)}, u32[]{:S(2)}, u32[]{:S(2)}) %collective-permute-start.2) | collective-permute-done | bytes 266272 | tf_op jit(solution)/shard_map/ppermute | solution.py:138
  38.5 1.9 %multiply_add_fusion.2 = f32[520,128]{1,0:T(8,128)} fusion(f32[520,128]{1,0:T(8,128)} %multiply_add_fusion.3, f32[520,128]{1,0:T(8,128)} %collective-permute-done.2, f32[520]{0:T(1024)S(1)} %concatenate.27), kind=kLoop, calls=%fused_computation.12 | loop fusion | flops 133120 | bytes 800800 | tf_op jit(solution)/shard_map/add | solution.py:160
  40.4 1.5 %collective-permute-start.3 = (f32[520,128]{1,0:T(8,128)}, f32[520,128]{1,0:T(8,128)}, u32[]{:S(2)}, u32[]{:S(2)}) collective-permute-start(f32[520,128]{1,0:T(8,128)} %multiply_add_fusion.2), channel_id=1, source_target_pairs={{0,64},{32,96},{64,128},{80,16},{96,160},{112,48},{128,192},{144,8... | collective-permute-start | bytes 798728 | tf_op jit(solution)/shard_map/ppermute | solution.py:138
  41.8 0.7 copy.26.cum_ref
  42.5 14.1 %shard_map.94 = (f32[512,512]{1,0:T(8,128)}, f32[512,512]{1,0:T(8,128)}) custom-call(f32[8,512]{1,0:T(8,128)} %copy.26.cum_ref, f32[512,8]{1,0:T(8,128)} %bitcast.47, f32[512,128]{1,0:T(8,128)} %proj_in_ref.1, f32[512,128]{1,0:T(8,128)} %proj_out_ref.1, f32[512,512]{1,0:T(8,128)} %get-tuple-element.10.in_ref, f32[512,512]{1,0:T(8,128)} %grad_ref.1), custom_call_target="tpu_custom_call" | custom-call | tf_op jit(solution)/shard_map/pallas_call | solution.py:73
  56.6 0.8 fusion.8
  57.6 1.2 multiply_add_fusion.1
  58.8 1.3 collective-permute-start.4
  60.1 2.8 %fusion.16 = f32[512,128]{0,1:T(8,128)} fusion(f32[512,512]{1,0:T(8,128)} %get-tuple-element.6, f32[512,128]{1,0:T(8,128)S(1)} %copy-done.4), kind=kOutput, calls=%fused_computation.49 | convolution fusion | flops 402653184 | bytes 1572864 | tf_op jit(solution)/shard_map/st,sn->tn/dot_general | solution.py:200
  63.1 14.8 %collective-permute-done.4 = f32[520,128]{1,0:T(8,128)} collective-permute-done((f32[520,128]{1,0:T(8,128)S(1)}, f32[520,128]{1,0:T(8,128)}, u32[]{:S(2)}, u32[]{:S(2)}) %collective-permute-start.4) | collective-permute-done | bytes 266272 | tf_op jit(solution)/shard_map/ppermute | solution.py:138
  77.9 1.8 %multiply_add_fusion = f32[520,128]{1,0:T(8,128)} fusion(f32[520,128]{1,0:T(8,128)S(1)} %multiply_add_fusion.1, f32[520,128]{1,0:T(8,128)} %collective-permute-done.4, f32[520]{0:T(1024)S(1)} %concatenate.29), kind=kLoop, calls=%fused_computation.10 | loop fusion | flops 133120 | bytes 800800 | tf_op jit(solution)/shard_map/add | solution.py:160
  79.7 1.3 collective-permute-start.5
  81.0 0.7 fusion.11
  81.8 0.8 fusion.6
  82.8 18.9 %collective-permute-done.5 = f32[520,128]{1,0:T(8,128)} collective-permute-done((f32[520,128]{1,0:T(8,128)}, f32[520,128]{1,0:T(8,128)}, u32[]{:S(2)}, u32[]{:S(2)}) %collective-permute-start.5) | collective-permute-done | bytes 266272 | tf_op jit(solution)/shard_map/ppermute | solution.py:138
  101.7 1.3 multiply_add_fusion.4
  103.0 8.4 %collective-permute-start.6 = (f32[512,128]{1,0:T(8,128)S(1)}, f32[512,128]{1,0:T(8,128)S(1)}, u32[]{:S(2)}, u32[]{:S(2)}) collective-permute-start(f32[512,128]{1,0:T(8,128)S(1)} %get-tuple-element.7), channel_id=1, source_target_pairs={{0,16},{16,0},{1,17},{17,1},{2,18},{18,2},{3,19},{19,3},{4,20},{20... | collective-permute-start | bytes 786440 | tf_op jit(solution)/shard_map/ppermute | solution.py:164
  111.4 1.2 fusion.15
  112.7 0.8 convolution_add_fusion
  113.5 1.2 convolution_add_fusion.1
  114.8 1.0 copy.34
  115.8 6.9 %all-to-all-start = ((f32[16,32,256]{2,1,0:T(8,128)}), f32[16,32,256]{2,1,0:T(8,128)S(1)}, u32[]{:S(2)}, u32[]{:S(2)}) async-start(f32[16,32,256]{2,1,0:T(8,128)} %bitcast.50), calls=%async_computation | async-start | bytes 1048576 | tf_op jit(solution)/shard_map/all_to_all | solution.py:211
  122.7 3.3 %fusion.2 = f32[512,512]{1,0:T(8,128)} fusion(f32[512,512]{1,0:T(8,128)S(1)} %copy.25, f32[512,512]{1,0:T(8,128)} %get-tuple-element.5, f32[512,512]{1,0:T(8,128)S(1)} %copy.32, f32[512,128]{1,0:T(8,128)S(1)} %copy-done.5, f32[512,128]{1,0:T(8,128)S(1)} %copy-done.9, f32[512,128]{1,0:T(8,128)S(1)} %get-tuple-element.8, pred[]{:T(512)S(6)} %eq.19), kind=kOutput, calls=%fused_computation.3 | convolution fusion | flops 403505152 | bytes 4980737 | tf_op jit(solution)/shard_map/tn,kn->tk/dot_general | solution.py:206
  126.0 7.5 %all-to-all-done = f32[16,32,256]{2,1,0:T(8,128)S(1)} async-done(((f32[16,32,256]{2,1,0:T(8,128)}), f32[16,32,256]{2,1,0:T(8,128)S(1)}, u32[]{:S(2)}, u32[]{:S(2)}) %all-to-all-start) | async-done | bytes 524320 | tf_op jit(solution)/shard_map/all_to_all | solution.py:211
  133.5 0.6 fusion.13
  (65 shorter events, 1.9 us)
Async XLA Ops:
  1.6 0.7 copy-start.14
  2.3 0.7 copy-start.15
  4.5 0.7 copy-start.6
  8.5 2.6 %copy-start.3 = (f32[512,128]{1,0:T(8,128)S(1)}, f32[512,128]{1,0:T(8,128)}, u32[]{:S(2)}) copy-start(f32[512,128]{1,0:T(8,128)} %proj_in_ref.1) | copy-start | bytes 786436
  12.9 1.4 %copy-start.11 = (f32[512,128]{1,0:T(8,128)S(1)}, f32[512,128]{1,0:T(8,128)}, u32[]{:S(2)}) copy-start(f32[512,128]{1,0:T(8,128)} %proj_out_ref.1) | copy-start | bytes 786436
  14.3 1.0 copy-start
  15.3 0.9 copy-start.10
  16.2 9.0 %collective-permute-start = (f32[520,128]{1,0:T(8,128)S(1)}, f32[520,128]{1,0:T(8,128)S(1)}, u32[]{:S(2)}, u32[]{:S(2)}) collective-permute-start(f32[520,128]{1,0:T(8,128)S(1)} %get-tuple-element.18), channel_id=1, source_target_pairs={{16,32},{48,64},{32,16},{80,96},{64,48},{112,128},{96,80},{144,160... | collective-permute-start | bytes 798728 | tf_op jit(solution)/shard_map/ppermute | solution.py:147
  21.1 7.7 %collective-permute-start.1 = (f32[520,128]{1,0:T(8,128)}, f32[520,128]{1,0:T(8,128)}, u32[]{:S(2)}, u32[]{:S(2)}) collective-permute-start(f32[520,128]{1,0:T(8,128)} %get-tuple-element.17), channel_id=1, source_target_pairs={{0,32},{32,64},{48,16},{64,96},{80,48},{96,128},{112,80},{128,160}... | collective-permute-start | bytes 798728 | tf_op jit(solution)/shard_map/ppermute | solution.py:138
  30.5 7.9 %collective-permute-start.2 = (f32[520,128]{1,0:T(8,128)}, f32[520,128]{1,0:T(8,128)}, u32[]{:S(2)}, u32[]{:S(2)}) collective-permute-start(f32[520,128]{1,0:T(8,128)} %multiply_add_fusion.3), channel_id=1, source_target_pairs={{0,32},{32,64},{48,16},{64,96},{80,48},{96,128},{112,80},{128,160}... | collective-permute-start | bytes 798728 | tf_op jit(solution)/shard_map/ppermute | solution.py:138
  32.8 9.0 %copy-start.7 = (f32[8,4,128]{0,2,1:T(8,128)S(1)}, f32[8,4,128]{0,2,1:T(8,128)}, u32[]{:S(2)}) copy-start(f32[8,4,128]{0,2,1:T(8,128)} %copy-done.6) | copy-start | bytes 49156
  40.4 17.2 %collective-permute-start.3 = (f32[520,128]{1,0:T(8,128)}, f32[520,128]{1,0:T(8,128)}, u32[]{:S(2)}, u32[]{:S(2)}) collective-permute-start(f32[520,128]{1,0:T(8,128)} %multiply_add_fusion.2), channel_id=1, source_target_pairs={{0,64},{32,96},{64,128},{80,16},{96,160},{112,48},{128,192},{144,8... | collective-permute-start | bytes 798728 | tf_op jit(solution)/shard_map/ppermute | solution.py:138
  57.6 2.5 %copy-start.4 = (f32[512,128]{1,0:T(8,128)S(1)}, f32[512,128]{1,0:T(8,128)}, u32[]{:S(2)}) copy-start(f32[512,128]{1,0:T(8,128)} %proj_in_ref.1) | copy-start | bytes 786436
  58.8 19.1 %collective-permute-start.4 = (f32[520,128]{1,0:T(8,128)S(1)}, f32[520,128]{1,0:T(8,128)}, u32[]{:S(2)}, u32[]{:S(2)}) collective-permute-start(f32[520,128]{1,0:T(8,128)S(1)} %multiply_add_fusion.1), channel_id=1, source_target_pairs={{0,128},{32,160},{64,192},{96,224},{128,256},{144,16},{160,288},{1... | collective-permute-start | bytes 798728 | tf_op jit(solution)/shard_map/ppermute | solution.py:138
  79.7 22.0 %collective-permute-start.5 = (f32[520,128]{1,0:T(8,128)}, f32[520,128]{1,0:T(8,128)}, u32[]{:S(2)}, u32[]{:S(2)}) collective-permute-start(f32[520,128]{1,0:T(8,128)} %multiply_add_fusion), channel_id=1, source_target_pairs={{0,256},{32,288},{64,320},{96,352},{128,384},{160,416},{192,448},{... | collective-permute-start | bytes 798728 | tf_op jit(solution)/shard_map/ppermute | solution.py:138
  82.8 28.6 %copy-start.2 = (f32[512,512]{1,0:T(8,128)S(1)}, f32[512,512]{1,0:T(8,128)}, u32[]{:S(2)}) copy-start(f32[512,512]{1,0:T(8,128)} %get-tuple-element.6) | copy-start | bytes 3145732
  82.8 28.6 %copy-start.12 = (f32[512,128]{1,0:T(8,128)S(1)}, f32[512,128]{1,0:T(8,128)}, u32[]{:S(2)}) copy-start(f32[512,128]{1,0:T(8,128)} %proj_out_ref.1) | copy-start | bytes 786436
  103.0 9.7 %copy-start.1 = (f32[512,512]{0,1:T(8,128)S(1)}, f32[512,512]{0,1:T(8,128)}, u32[]{:S(2)}) copy-start(f32[512,512]{0,1:T(8,128)} %copy-done) | copy-start | bytes 3145732
  103.0 9.7 %copy-start.13 = (f32[512,128]{0,1:T(8,128)S(1)}, f32[512,128]{0,1:T(8,128)}, u32[]{:S(2)}) copy-start(f32[512,128]{0,1:T(8,128)} %fusion.16) | copy-start | bytes 786436
  103.0 9.6 %collective-permute-start.6 = (f32[512,128]{1,0:T(8,128)S(1)}, f32[512,128]{1,0:T(8,128)S(1)}, u32[]{:S(2)}, u32[]{:S(2)}) collective-permute-start(f32[512,128]{1,0:T(8,128)S(1)} %get-tuple-element.7), channel_id=1, source_target_pairs={{0,16},{16,0},{1,17},{17,1},{2,18},{18,2},{3,19},{19,3},{4,20},{20... | collective-permute-start | bytes 786440 | tf_op jit(solution)/shard_map/ppermute | solution.py:164
  112.6 0.8 copy-start.8
  115.7 6.9 %copy-start.5 = (f32[512,128]{1,0:T(8,128)S(1)}, f32[512,128]{1,0:T(8,128)}, u32[]{:S(2)}) copy-start(f32[512,128]{1,0:T(8,128)} %proj_in_ref.1) | copy-start | bytes 786436
  115.8 6.9 %copy-start.9 = (f32[512,128]{1,0:T(8,128)S(1)}, f32[512,128]{1,0:T(8,128)}, u32[]{:S(2)}) copy-start(f32[512,128]{1,0:T(8,128)} %copy-done.8) | copy-start | bytes 786436
  115.8 17.7 %all-to-all-start = ((f32[16,32,256]{2,1,0:T(8,128)}), f32[16,32,256]{2,1,0:T(8,128)S(1)}, u32[]{:S(2)}, u32[]{:S(2)}) async-start(f32[16,32,256]{2,1,0:T(8,128)} %bitcast.50), calls=%async_computation | async-start | bytes 1048576 | tf_op jit(solution)/shard_map/all_to_all | solution.py:211

commit v14 on v12

--- a/solution.py
+++ b/solution.py
@@ -38,7 +38,7 @@
     tok = scores_t_ref.shape[0]
     width = in_ref.shape[1] // HEADS_PER_STEP
     head_count = cum_ref.shape[0]
-    piece = 128
+    piece = 64
     which = lax.broadcasted_iota(jnp.int32, (tok, head_count), 1)
     for k in range(HEADS_PER_STEP):
         head = step * HEADS_PER_STEP + k

time: 135 us -> 142 us (1.052)
  Pallas kernels: 14.1 us -> 21 us
    pallas_call x1, Pallas kernels: 14.1 us -> 21 us  [block_terms(): pl.pallas_call(block_kernel, grid=(head_count // HEADS_PER_STEP,), in_spe...]
  transfers between devices with their start and end apart: 8 -> 8, of which waited for: 6 -> 6; matrix products, arithmetic and copies ran while one was open for 8% -> 8% of each run, Pallas kernels for 11% -> 15%
where the time goes in v14:
time: 142 us; the launch traced here: 141 us
  waiting for transfers between devices  53.9 us (38%)
  starting transfers between devices  26 us (18%)
  Pallas kernels  21 us (15%)
  other arithmetic  14.7 us (10%)
  local copies, waits for them, and re-layouts  12.5 us (9%)
  matrix products  12.1 us (9%)
    ppermute x5, waiting for transfers between devices, move(): return lax.ppermute(value, both, pairs)  43.3 us
    pallas_call x1, Pallas kernels, block_terms(): pl.pallas_call(block_kernel, grid=(head_count // HEADS_PER_STEP,), in_spe...  21 us
    all_to_all x1, waiting for transfers between devices, per_device(): spread = lax.all_to_all(both, 'head', 0, 0, tiled=True)  7.78 us
    ppermute x1, starting transfers between devices, chip_scans(): back = lax.ppermute(joined.reshape(rows, state_width), 'core', swap)  7.54 us
    all_to_all x1, starting transfers between devices, per_device(): spread = lax.all_to_all(both, 'head', 0, 0, tiled=True)  6.88 us
    ppermute x5, starting transfers between devices, move(): return lax.ppermute(value, both, pairs)  6.61 us
    unnamed x37, local copies, waits for them, and re-layouts  5.43 us
    add x3, other arithmetic, chip_scans(): running = scale[:, None] * got + running  4.94 us
  transfers between devices with their start and end apart: 8, of which 6 were waited for; matrix products, arithmetic and copies ran while one was open for 8% of the time, Pallas kernels for 15%

profile of v14, /device:TPU:1, one launch (start us, length us, event | category | flops | bytes accessed | tf_op | source)
XLA Modules:
  0.0 141.1 jit_solution(15354213675899766433)
XLA Ops:
  0.6 0.8 select_reduce_fusion
  1.6 0.3 copy.25
  1.9 0.3 copy-done.16
  2.3 0.6 copy-done.17
  3.0 1.1 reduce-window.6
  4.1 0.2 slice_reduce_fusion
  4.7 0.6 copy-done.6
  5.5 0.3 copy.32
  5.8 2.5 %copy.30 = f32[512,512]{0,1:T(8,128)} copy(f32[512,512]{1,0:T(8,128)} %grad_ref.1) | data formatting | bytes 2097152 | tf_op args[6]
  8.5 2.6 %fusion.11 = (f32[512,512]{1,0:T(8,128)S(1)}, f32[512,512]{1,0:T(8,128)}) fusion(f32[512,512]{1,0:T(8,128)S(1)} %copy.32, f32[512,512]{1,0:T(8,128)} %param.7, f32[512,512]{1,0:T(8,128)S(1)} %copy.25), kind=kLoop, calls=%fused_computation.46 | loop fusion | flops 524288 | bytes 5242880 | tf_op jit(solution)/shard_map/mul | solution.py:184
  11.1 1.8 %fusion.13 = f32[512,128]{1,0:T(8,128)S(1)} fusion(f32[512,512]{1,0:T(8,128)S(1)} %get-tuple-element.11, f32[512,128]{1,0:T(8,128)S(1)} %copy-done.3), kind=kOutput, calls=%fused_computation.48 | convolution fusion | flops 402653184 | bytes 1572864 | tf_op jit(solution)/shard_map/tk,tn->kn/dot_general | solution.py:186
  12.9 1.4 bitcast_multiply_fusion
  14.3 1.0 broadcast_select_fusion.1
  15.4 0.6 copy-done.11
  16.0 4.9 %collective-permute-start.1 = (f32[520,128]{1,0:T(8,128)S(1)}, f32[520,128]{1,0:T(8,128)S(1)}, u32[]{:S(2)}, u32[]{:S(2)}) collective-permute-start(f32[520,128]{1,0:T(8,128)S(1)} %get-tuple-element.20), channel_id=1, source_target_pairs={{16,32},{48,64},{32,16},{80,96},{64,48},{112,128},{96,80},{144,160... | collective-permute-start | bytes 798728 | tf_op jit(solution)/shard_map/ppermute | solution.py:147
  20.9 1.3 collective-permute-start
  22.2 2.8 %collective-permute-done.1 = f32[520,128]{1,0:T(8,128)S(1)} collective-permute-done((f32[520,128]{1,0:T(8,128)S(1)}, f32[520,128]{1,0:T(8,128)S(1)}, u32[]{:S(2)}, u32[]{:S(2)}) %collective-permute-start.1) | collective-permute-done | bytes 266272 | tf_op jit(solution)/shard_map/ppermute | solution.py:147
  25.0 3.3 %collective-permute-done = f32[520,128]{1,0:T(8,128)S(1)} collective-permute-done((f32[520,128]{1,0:T(8,128)S(1)}, f32[520,128]{1,0:T(8,128)S(1)}, u32[]{:S(2)}, u32[]{:S(2)}) %collective-permute-start) | collective-permute-done | bytes 266272 | tf_op jit(solution)/shard_map/ppermute | solution.py:138
  28.3 0.7 copy-done.15
  29.0 0.1 fusion.9
  29.3 1.1 slice_add_fusion.1
  30.4 0.8 pad_maximum_fusion.3
  31.2 1.3 collective-permute-start.2
  32.7 6.5 %collective-permute-done.2 = f32[520,128]{1,0:T(8,128)} collective-permute-done((f32[520,128]{1,0:T(8,128)}, f32[520,128]{1,0:T(8,128)}, u32[]{:S(2)}, u32[]{:S(2)}) %collective-permute-start.2) | collective-permute-done | bytes 266272 | tf_op jit(solution)/shard_map/ppermute | solution.py:138
  39.2 1.9 %multiply_add_fusion.2 = f32[520,128]{1,0:T(8,128)} fusion(f32[520,128]{1,0:T(8,128)} %collective-permute-done.2, f32[520]{0:T(1024)S(1)} %concatenate.26, f32[520]{0:T(1024)S(1)} %pad.7.clone, f32[512,128]{1,0:T(8,128)} %copy-done.10), kind=kLoop, calls=%fused_computation.13 | loop fusion | flops 199680 | bytes 798784 | tf_op jit(solution)/shard_map/add | solution.py:156
  41.1 1.5 %collective-permute-start.3 = (f32[520,128]{1,0:T(8,128)}, f32[520,128]{1,0:T(8,128)}, u32[]{:S(2)}, u32[]{:S(2)}) collective-permute-start(f32[520,128]{1,0:T(8,128)} %multiply_add_fusion.2), channel_id=1, source_target_pairs={{0,64},{32,96},{64,128},{80,16},{96,160},{112,48},{128,192},{144,8... | collective-permute-start | bytes 798728 | tf_op jit(solution)/shard_map/ppermute | solution.py:138
  42.6 0.7 copy.26.cum_ref
  43.3 21.0 %shard_map.94 = (f32[512,512]{1,0:T(8,128)}, f32[512,512]{1,0:T(8,128)}) custom-call(f32[8,512]{1,0:T(8,128)} %copy.26.cum_ref, f32[512,8]{1,0:T(8,128)} %bitcast.47, f32[512,128]{1,0:T(8,128)} %proj_in_ref.1, f32[512,128]{1,0:T(8,128)} %proj_out_ref.1, f32[512,512]{1,0:T(8,128)} %get-tuple-element.12.in_ref, f32[512,512]{1,0:T(8,128)} %grad_ref.1), custom_call_target="tpu_custom_call" | custom-call | tf_op jit(solution)/shard_map/pallas_call | solution.py:73
  64.2 0.8 fusion.8
  65.2 1.2 multiply_add_fusion.1
  66.4 1.3 collective-permute-start.4
  67.7 2.7 %fusion.15 = f32[512,128]{0,1:T(8,128)} fusion(f32[512,512]{1,0:T(8,128)} %get-tuple-element.6, f32[512,128]{1,0:T(8,128)S(1)} %copy-done.4), kind=kOutput, calls=%fused_computation.50 | convolution fusion | flops 402653184 | bytes 1572864 | tf_op jit(solution)/shard_map/st,sn->tn/dot_general | solution.py:196
  70.8 14.8 %collective-permute-done.4 = f32[520,128]{1,0:T(8,128)} collective-permute-done((f32[520,128]{1,0:T(8,128)S(1)}, f32[520,128]{1,0:T(8,128)}, u32[]{:S(2)}, u32[]{:S(2)}) %collective-permute-start.4) | collective-permute-done | bytes 266272 | tf_op jit(solution)/shard_map/ppermute | solution.py:138
  85.5 1.8 %multiply_add_fusion = f32[520,128]{1,0:T(8,128)} fusion(f32[520,128]{1,0:T(8,128)S(1)} %multiply_add_fusion.1, f32[520,128]{1,0:T(8,128)} %collective-permute-done.4, f32[520]{0:T(1024)S(1)} %concatenate.29), kind=kLoop, calls=%fused_computation.11 | loop fusion | flops 133120 | bytes 800800 | tf_op jit(solution)/shard_map/add | solution.py:156
  87.3 1.3 collective-permute-start.5
  88.6 0.7 fusion.10
  89.5 0.8 fusion.6
  90.4 18.8 %collective-permute-done.5 = f32[520,128]{1,0:T(8,128)} collective-permute-done((f32[520,128]{1,0:T(8,128)}, f32[520,128]{1,0:T(8,128)}, u32[]{:S(2)}, u32[]{:S(2)}) %collective-permute-start.5) | collective-permute-done | bytes 266272 | tf_op jit(solution)/shard_map/ppermute | solution.py:138
  109.2 1.3 multiply_add_fusion.3
  110.5 7.5 %collective-permute-start.6 = (f32[512,128]{1,0:T(8,128)S(1)}, f32[512,128]{1,0:T(8,128)S(1)}, u32[]{:S(2)}, u32[]{:S(2)}) collective-permute-start(f32[512,128]{1,0:T(8,128)S(1)} %get-tuple-element.9), channel_id=1, source_target_pairs={{0,16},{16,0},{1,17},{17,1},{2,18},{18,2},{3,19},{19,3},{4,20},{20... | collective-permute-start | bytes 786440 | tf_op jit(solution)/shard_map/ppermute | solution.py:160
  118.1 1.2 fusion.14
  119.4 0.8 convolution_add_fusion
  120.2 1.2 convolution_add_fusion.1
  121.5 1.0 copy.34
  122.5 6.9 %all-to-all-start = ((f32[16,32,256]{2,1,0:T(8,128)}), f32[16,32,256]{2,1,0:T(8,128)S(1)}, u32[]{:S(2)}, u32[]{:S(2)}) async-start(f32[16,32,256]{2,1,0:T(8,128)} %bitcast.50), calls=%async_computation | async-start | bytes 1048576 | tf_op jit(solution)/shard_map/all_to_all | solution.py:207
  129.4 3.3 %fusion.2 = f32[512,512]{1,0:T(8,128)} fusion(f32[512,512]{1,0:T(8,128)S(1)} %copy.25, f32[512,512]{1,0:T(8,128)} %get-tuple-element.5, f32[512,512]{1,0:T(8,128)S(1)} %copy.32, f32[512,128]{1,0:T(8,128)S(1)} %copy-done.5, f32[512,128]{1,0:T(8,128)S(1)} %copy-done.9, f32[512,128]{1,0:T(8,128)S(1)} %get-tuple-element.10, pred[]{:T(512)S(6)} %eq.19), kind=kOutput, calls=%fused_computation.3 | convolution fusion | flops 403505152 | bytes 4980737 | tf_op jit(solution)/shard_map/tn,kn->tk/dot_general | solution.py:202
  132.6 7.8 %all-to-all-done = f32[16,32,256]{2,1,0:T(8,128)S(1)} async-done(((f32[16,32,256]{2,1,0:T(8,128)}), f32[16,32,256]{2,1,0:T(8,128)S(1)}, u32[]{:S(2)}, u32[]{:S(2)}) %all-to-all-start) | async-done | bytes 524320 | tf_op jit(solution)/shard_map/all_to_all | solution.py:207
  140.5 0.6 fusion.12
  (70 shorter events, 2.2 us)
Async XLA Ops:
  1.6 0.7 copy-start.16
  2.3 0.7 copy-start.17
  4.5 0.7 copy-start.6
  8.5 2.6 %copy-start.3 = (f32[512,128]{1,0:T(8,128)S(1)}, f32[512,128]{1,0:T(8,128)}, u32[]{:S(2)}) copy-start(f32[512,128]{1,0:T(8,128)} %proj_in_ref.1) | copy-start | bytes 786436
  12.9 1.4 copy-start.12
  14.3 1.0 copy-start
  15.3 0.7 copy-start.11
  16.0 9.0 %collective-permute-start.1 = (f32[520,128]{1,0:T(8,128)S(1)}, f32[520,128]{1,0:T(8,128)S(1)}, u32[]{:S(2)}, u32[]{:S(2)}) collective-permute-start(f32[520,128]{1,0:T(8,128)S(1)} %get-tuple-element.20), channel_id=1, source_target_pairs={{16,32},{48,64},{32,16},{80,96},{64,48},{112,128},{96,80},{144,160... | collective-permute-start | bytes 798728 | tf_op jit(solution)/shard_map/ppermute | solution.py:147
  20.9 7.3 %collective-permute-start = (f32[520,128]{1,0:T(8,128)S(1)}, f32[520,128]{1,0:T(8,128)S(1)}, u32[]{:S(2)}, u32[]{:S(2)}) collective-permute-start(f32[520,128]{1,0:T(8,128)S(1)} %get-tuple-element.19), channel_id=1, source_target_pairs={{0,32},{32,64},{48,16},{64,96},{80,48},{96,128},{112,80},{128,160}... | collective-permute-start | bytes 798728 | tf_op jit(solution)/shard_map/ppermute | solution.py:138
  28.3 0.7 copy-start.15
  30.4 0.8 copy-start.10
  31.2 7.9 %collective-permute-start.2 = (f32[520,128]{1,0:T(8,128)}, f32[520,128]{1,0:T(8,128)}, u32[]{:S(2)}, u32[]{:S(2)}) collective-permute-start(f32[520,128]{1,0:T(8,128)} %pad_maximum_fusion.3), channel_id=1, source_target_pairs={{0,32},{32,64},{48,16},{64,96},{80,48},{96,128},{112,80},{128,160}... | collective-permute-start | bytes 798728 | tf_op jit(solution)/shard_map/ppermute | solution.py:138
  32.7 9.9 %copy-start.7 = (f32[8,4,128]{0,2,1:T(8,128)S(1)}, f32[8,4,128]{0,2,1:T(8,128)}, u32[]{:S(2)}) copy-start(f32[8,4,128]{0,2,1:T(8,128)} %copy-done.6) | copy-start | bytes 49156
  41.1 24.1 %collective-permute-start.3 = (f32[520,128]{1,0:T(8,128)}, f32[520,128]{1,0:T(8,128)}, u32[]{:S(2)}, u32[]{:S(2)}) collective-permute-start(f32[520,128]{1,0:T(8,128)} %multiply_add_fusion.2), channel_id=1, source_target_pairs={{0,64},{32,96},{64,128},{80,16},{96,160},{112,48},{128,192},{144,8... | collective-permute-start | bytes 798728 | tf_op jit(solution)/shard_map/ppermute | solution.py:138
  65.2 2.5 %copy-start.4 = (f32[512,128]{1,0:T(8,128)S(1)}, f32[512,128]{1,0:T(8,128)}, u32[]{:S(2)}) copy-start(f32[512,128]{1,0:T(8,128)} %proj_in_ref.1) | copy-start | bytes 786436
  66.4 19.1 %collective-permute-start.4 = (f32[520,128]{1,0:T(8,128)S(1)}, f32[520,128]{1,0:T(8,128)}, u32[]{:S(2)}, u32[]{:S(2)}) collective-permute-start(f32[520,128]{1,0:T(8,128)S(1)} %multiply_add_fusion.1), channel_id=1, source_target_pairs={{0,128},{32,160},{64,192},{96,224},{128,256},{144,16},{160,288},{1... | collective-permute-start | bytes 798728 | tf_op jit(solution)/shard_map/ppermute | solution.py:138
  87.3 21.9 %collective-permute-start.5 = (f32[520,128]{1,0:T(8,128)}, f32[520,128]{1,0:T(8,128)}, u32[]{:S(2)}, u32[]{:S(2)}) collective-permute-start(f32[520,128]{1,0:T(8,128)} %multiply_add_fusion), channel_id=1, source_target_pairs={{0,256},{32,288},{64,320},{96,352},{128,384},{160,416},{192,448},{... | collective-permute-start | bytes 798728 | tf_op jit(solution)/shard_map/ppermute | solution.py:138
  90.4 27.7 %copy-start.2 = (f32[512,512]{1,0:T(8,128)S(1)}, f32[512,512]{1,0:T(8,128)}, u32[]{:S(2)}) copy-start(f32[512,512]{1,0:T(8,128)} %get-tuple-element.6) | copy-start | bytes 3145732
  90.4 27.7 %copy-start.13 = (f32[512,128]{1,0:T(8,128)S(1)}, f32[512,128]{1,0:T(8,128)}, u32[]{:S(2)}) copy-start(f32[512,128]{1,0:T(8,128)} %proj_out_ref.1) | copy-start | bytes 786436
  110.5 8.8 %copy-start.1 = (f32[512,512]{0,1:T(8,128)S(1)}, f32[512,512]{0,1:T(8,128)}, u32[]{:S(2)}) copy-start(f32[512,512]{0,1:T(8,128)} %copy-done) | copy-start | bytes 3145732
  110.5 8.8 %copy-start.14 = (f32[512,128]{0,1:T(8,128)S(1)}, f32[512,128]{0,1:T(8,128)}, u32[]{:S(2)}) copy-start(f32[512,128]{0,1:T(8,128)} %fusion.15) | copy-start | bytes 786436
  110.5 8.8 %collective-permute-start.6 = (f32[512,128]{1,0:T(8,128)S(1)}, f32[512,128]{1,0:T(8,128)S(1)}, u32[]{:S(2)}, u32[]{:S(2)}) collective-permute-start(f32[512,128]{1,0:T(8,128)S(1)} %get-tuple-element.9), channel_id=1, source_target_pairs={{0,16},{16,0},{1,17},{17,1},{2,18},{18,2},{3,19},{19,3},{4,20},{20... | collective-permute-start | bytes 786440 | tf_op jit(solution)/shard_map/ppermute | solution.py:160
  119.3 0.8 copy-start.8
  122.4 6.9 %copy-start.5 = (f32[512,128]{1,0:T(8,128)S(1)}, f32[512,128]{1,0:T(8,128)}, u32[]{:S(2)}) copy-start(f32[512,128]{1,0:T(8,128)} %proj_in_ref.1) | copy-start | bytes 786436
  122.4 6.9 %copy-start.9 = (f32[512,128]{1,0:T(8,128)S(1)}, f32[512,128]{1,0:T(8,128)}, u32[]{:S(2)}) copy-start(f32[512,128]{1,0:T(8,128)} %copy-done.8) | copy-start | bytes 786436
  122.5 18.0 %all-to-all-start = ((f32[16,32,256]{2,1,0:T(8,128)}), f32[16,32,256]{2,1,0:T(8,128)S(1)}, u32[]{:S(2)}, u32[]{:S(2)}) async-start(f32[16,32,256]{2,1,0:T(8,128)} %bitcast.50), calls=%async_computation | async-start | bytes 1048576 | tf_op jit(solution)/shard_map/all_to_all | solution.py:207
